TPU v7x, 256 devices: a whole 4x4x8 slice. The times are simulated.
256 devices in a mesh: seq: 32 (over z, y_hi, core), tp: 8 (over y_lo, x).
Axes of the slice: x: 4, y: 4 (y_hi: 2, y_lo: 2; y = y_hi * 2 + y_lo), z: 8, core: 2. Of those that a mesh axis runs over, the one named last changes fastest.
Arguments:
- queries: bfloat16 [12288, 3072], P('seq', 'tp'), may hold values from -16 to 16
- keys: bfloat16 [12288, 3072], P('seq', 'tp'), may hold values from -6 to 6
- values: bfloat16 [12288, 3072], P('seq', 'tp'), may hold values from -6 to 6
- resid: bfloat16 [12288, 6144], P(('seq', 'tp')), may hold values from -6 to 6
- out_weight: bfloat16 [3072, 6144], P('tp'), may hold values from -0.109375 to 0.109375
- gain: float32 [6144], replicated, may hold values from 0.1 to 1.9
- pair_of_device: int32 [32], replicated, may hold values from 0 to 31, each once
- frame_of_tile: int32 [64], replicated, may hold values from 0 to 8, as said below
Outputs:
- layer_out: bfloat16 [12288, 6144], P(('seq', 'tp'))
Inputs may be any that keep to these rules, and one draw needn't show every extreme that they name: `pair_of_device`: each value once. Frames have equal length, 8 tiles; the sequence starts inside frame 0 and ends inside frame 8, so only these two are partial: frame_of_tile[t] = (t + o) // 8 for an offset o from 1 to 7.
All inputs are finite; a program needn't handle non-finite values.
Results may differ from a plain program's by a relative error of at most 0.025.
Values may be sent and summed in bfloat16 or wider, within the bound.
No kernel may reach another device: no remote copies, remote signals or barrier semaphores. Data moves between devices by JAX's collectives and lax.ppermute only.
A program may use at most 128 MiB of HBM per device.

v0:
```python
import math

import jax
import jax.numpy as jnp
from jax import lax
from jax.sharding import PartitionSpec as P

HEAD = 128


def slot_frames(pair_of_device, frame_of_tile, tile_count):
    slot_ids = jnp.arange(tile_count, dtype=jnp.int32)
    paired = jnp.repeat(pair_of_device, 2)
    tile_ids = jnp.where(slot_ids % 2 == 0, paired, tile_count - 1 - paired)
    matches = tile_ids[:, None] == jnp.arange(tile_count, dtype=jnp.int32)[None, :]
    return jnp.sum(jnp.where(matches, frame_of_tile[None, :], 0), axis=1)


def frames_of_rows(slot_frame, offset, row_count, span_rows):
    row_slots = (offset + jnp.arange(row_count, dtype=jnp.int32)) // span_rows
    matches = row_slots[:, None] == jnp.arange(slot_frame.shape[0], dtype=jnp.int32)[None, :]
    return jnp.sum(jnp.where(matches, slot_frame[None, :], 0), axis=1)


def softmax_update(carry_state, query_heads, query_frame, key_rows, value_rows, key_frame):
    head_count = query_heads.shape[1]
    key_heads = key_rows.reshape(key_rows.shape[0], head_count, HEAD)
    value_heads = value_rows.reshape(value_rows.shape[0], head_count, HEAD)
    allowed = (key_frame[None, :] <= query_frame[:, None])[None, :, :]
    score_scale = 1.0 / math.sqrt(HEAD)
    run_max, run_totals, weighted = carry_state
    scores = (
        jnp.einsum("qhd,khd->hqk", query_heads, key_heads, preferred_element_type=jnp.float32)
        * score_scale
    )
    masked = jnp.where(allowed, scores, jnp.float32(-1e30))
    new_max = jnp.maximum(run_max, jnp.max(masked, axis=-1))
    probs = jnp.where(allowed, jnp.exp(masked - new_max[..., None]), jnp.float32(0.0))
    rescale = jnp.exp(run_max - new_max)
    new_totals = run_totals * rescale + jnp.sum(probs, axis=-1)
    product = jnp.einsum(
        "hqk,khd->hqd", probs.astype(jnp.bfloat16), value_heads, preferred_element_type=jnp.float32
    )
    return (new_max, new_totals, weighted * rescale[..., None] + product)


def empty_state(head_count, row_count):
    return (
        jnp.full((head_count, row_count), -1e30, jnp.float32),
        jnp.zeros((head_count, row_count), jnp.float32),
        jnp.zeros((head_count, row_count, HEAD), jnp.float32),
    )


def local(queries, keys, values, resid, out_weight, gain, pair_of_device, frame_of_tile):
    tok_rows, row_width = queries.shape
    head_count = row_width // HEAD
    span_rows = tok_rows // 2
    seq_count = lax.axis_size("seq")
    seq_index = lax.axis_index("seq")
    slot_frame = slot_frames(pair_of_device, frame_of_tile, 2 * seq_count)
    own_frames = lax.dynamic_slice_in_dim(slot_frame, 2 * seq_index, 2, 0)
    row_frame = jnp.repeat(own_frames, span_rows)
    query_heads = queries.reshape(tok_rows, head_count, HEAD)
    key_rows = lax.all_gather(keys, "seq", axis=0, tiled=True)
    value_rows = lax.all_gather(values, "seq", axis=0, tiled=True)
    key_count = key_rows.shape[0]
    key_blocks = key_rows.reshape(key_count // 512, 512, row_width)
    value_blocks = value_rows.reshape(key_count // 512, 512, row_width)

    def advance(inner_state, entry):
        key_block, value_block, block_index = entry
        key_frame = frames_of_rows(slot_frame, block_index * 512, 512, span_rows)
        return (
            softmax_update(inner_state, query_heads, row_frame, key_block, value_block, key_frame),
            None,
        )

    final_state, unused = lax.scan(
        advance,
        empty_state(head_count, tok_rows),
        (key_blocks, value_blocks, jnp.arange(key_count // 512, dtype=jnp.int32)),
    )
    run_max, run_totals, weighted = final_state
    attn_heads = jnp.transpose(weighted / run_totals[..., None], (1, 0, 2))
    attn = attn_heads.reshape(tok_rows, row_width).astype(jnp.bfloat16)
    branch = lax.psum_scatter(
        jnp.dot(attn, out_weight, preferred_element_type=jnp.float32).astype(jnp.bfloat16),
        "tp",
        scatter_dimension=0,
        tiled=True,
    ).astype(jnp.float32)
    rms = jnp.sqrt(jnp.mean(branch * branch, axis=-1) + 1e-06)
    layer_out = resid.astype(jnp.float32) + gain[None, :] * branch / rms[:, None]
    return layer_out.astype(jnp.bfloat16)


def solution(mesh):
    in_specs = (
        P("seq", "tp"),
        P("seq", "tp"),
        P("seq", "tp"),
        P(("seq", "tp"), None),
        P("tp", None),
        P(),
        P(),
        P(),
    )
    out_specs = P(("seq", "tp"), None)
    return jax.shard_map(local, mesh=mesh, in_specs=in_specs, out_specs=out_specs, check_vma=False)
```

profile of v0, /device:TPU:2, one launch (start us, length us, event | category | flops | bytes accessed | tf_op | source)
XLA Modules:
  0.0 433.4 jit_solution(12909804964037090042)
XLA Ops:
  8.9 1.2 copy.27
  11.2 107.2 %all-gather.3.cloned.1.call-done = bf16[12288,384]{1,0:T(8,128)(2,1)} async-done(((bf16[384,384]{1,0:T(8,128)(2,1)}), bf16[12288,384]{1,0:T(8,128)(2,1)}) %all-gather.3.cloned.1.call-update) | async-done | bytes 9437200 | tf_op jit(solution)/shard_map/all_gather | solution.py:65
  118.5 104.7 %all-gather.5.cloned.1.call-done = bf16[12288,384]{1,0:T(8,128)(2,1)} async-done(((bf16[384,384]{1,0:T(8,128)(2,1)}), bf16[12288,384]{1,0:T(8,128)(2,1)}) %all-gather.5.cloned.1.call-update) | async-done | bytes 9437200 | tf_op jit(solution)/shard_map/all_gather | solution.py:66
  223.2 137.8 %while.17 = (s32[]{:T(128)}, f32[3,384]{1,0:T(4,128)S(1)}, f32[3,384]{1,0:T(4,128)S(1)}, f32[3,384,128]{2,1,0:T(8,128)S(1)}, s32[24]{0:T(128)S(1)}, /*index=5*/s...) while((s32[]{:T(128)}, f32[3,384]{1,0:T(4,128)S(1)}, ...), condition=%wide.region_5.6_spmd.clone, body=%wide.region_1.5_spmd.clone.sunk | while | flops 310404736 | bytes 13359545 | solution.py:79
  224.9 1.2 constant_dynamic-slice_fusion.3
  230.6 1.2 constant_dynamic-slice_fusion.3
  236.3 1.2 constant_dynamic-slice_fusion.3
  242.1 1.2 constant_dynamic-slice_fusion.3
  247.8 1.2 constant_dynamic-slice_fusion.3
  253.6 1.2 constant_dynamic-slice_fusion.3
  259.3 1.2 constant_dynamic-slice_fusion.3
  265.1 1.2 constant_dynamic-slice_fusion.3
  270.8 1.2 constant_dynamic-slice_fusion.3
  276.6 1.2 constant_dynamic-slice_fusion.3
  282.3 1.2 constant_dynamic-slice_fusion.3
  288.0 1.2 constant_dynamic-slice_fusion.3
  293.8 1.2 constant_dynamic-slice_fusion.3
  299.5 1.2 constant_dynamic-slice_fusion.3
  305.3 1.2 constant_dynamic-slice_fusion.3
  311.0 1.2 constant_dynamic-slice_fusion.3
  316.8 1.2 constant_dynamic-slice_fusion.3
  322.5 1.2 constant_dynamic-slice_fusion.3
  328.2 1.2 constant_dynamic-slice_fusion.3
  334.0 1.2 constant_dynamic-slice_fusion.3
  339.7 1.2 constant_dynamic-slice_fusion.3
  345.5 1.2 constant_dynamic-slice_fusion.3
  351.2 1.2 constant_dynamic-slice_fusion.3
  357.0 1.2 constant_dynamic-slice_fusion.3
  361.3 7.1 %convolution_convert_fusion = bf16[384,6144]{1,0:T(8,128)(2,1)} fusion(bf16[384,384]{0,1:T(8,128)(2,1)S(1)} %bitcast.45, bf16[384,6144]{1,0:T(8,128)(2,1)} %param.14), kind=kOutput, calls=%fused_computation.29 | convolution fusion | flops 1814298624 | bytes 9732096 | tf_op jit(solution)/shard_map/dot_general | solution.py:88
  368.4 55.0 %reduce-scatter.2.cloned.1.call-done = bf16[48,6144]{1,0:T(8,128)(2,1)} async-done(((bf16[384,6144]{1,0:T(8,128)(2,1)}), bf16[48,6144]{1,0:T(8,128)(2,1)}) %reduce-scatter.2.cloned.1.call-update) | async-done | bytes 589840 | tf_op jit(solution)/shard_map/reduce_scatter | solution.py:87
  423.5 1.3 fusion.18
  424.8 2.1 fusion.17
  (359 shorter events, 96.3 us)
Async XLA Ops:
  6.5 112.0 %all-gather.3.cloned.1.call-start = ((), (), s32[]{:S(2)}) async-start(), calls=%async_computation.1 | async-start | bytes 9732096 | tf_op jit(solution)/shard_map/all_gather | solution.py:65
  7.3 215.9 %all-gather.5.cloned.1.call-start = ((), (), s32[]{:S(2)}) async-start(), calls=%async_computation.2 | async-start | bytes 9732096 | tf_op jit(solution)/shard_map/all_gather | solution.py:66
  8.0 415.4 %reduce-scatter.2.cloned.1.call-start = ((), (), s32[]{:S(2)}) async-start(), calls=%async_computation.3 | async-start | bytes 5308416 | tf_op jit(solution)/shard_map/reduce_scatter | solution.py:87
  368.4 56.3 %copy-start = (bf16[48,6144]{1,0:T(8,128)(2,1)S(1)}, bf16[48,6144]{1,0:T(8,128)(2,1)}, u32[]{:S(2)}) copy-start(bf16[48,6144]{1,0:T(8,128)(2,1)} %param.13) | copy-start | bytes 1769476
  368.4 56.3 %copy-start.1 = (f32[6144]{0:T(1024)S(1)}, f32[6144]{0:T(1024)}, u32[]{:S(2)}) copy-start(f32[6144]{0:T(1024)} %param.15) | copy-start | bytes 73732
Sparse Core Ops, SparseCore 0:
  10.1 108.3 all-gather.2
  121.3 101.8 all-gather.4
  368.6 54.8 reduce-scatter.1
where the time goes:
time: 437 us; the launch traced here: 433 us
  waiting for transfers between devices  268 us (61%)
  local copies, waits for them, and re-layouts  59.5 us (14%)
  matrix products  49.3 us (11%)
  other arithmetic  26.6 us (6%)
  loops' own time  16.4 us (4%)
  between operations  13.2 us (3%)
    all_gather x1, waiting for transfers between devices, local(): key_rows = lax.all_gather(keys, 'seq', axis=0, tiled=True)  107 us
    all_gather x1, waiting for transfers between devices, local(): value_rows = lax.all_gather(values, 'seq', axis=0, tiled=True)  105 us
    reduce_scatter x1, waiting for transfers between devices, local(): lax.psum_scatter(jnp.dot(attn, out_weight, preferred_element_type=jnp.flo...  55 us
    dynamic_slice x96, local copies, waits for them, and re-layouts, local(): lax.scan(advance, empty_state(head_count, tok_rows), (key_blocks, value_b...  53.2 us
    dot_general x24, matrix products, softmax_update(): jnp.einsum('hqk,khd->hqd', probs.astype(jnp.bfloat16), value_heads, prefe...  25.8 us
    another operation x1, loops' own time, local(): lax.scan(advance, empty_state(head_count, tok_rows), (key_blocks, value_b...  16.4 us
    dot_general x24, matrix products, softmax_update(): jnp.einsum('qhd,khd->hqk', query_heads, key_heads, preferred_element_type...  16.3 us
    reduce_sum x24, other arithmetic, softmax_update(): new_totals = run_totals * rescale + jnp.sum(probs, axis=-1)  14.9 us
  transfers between devices with their start and end apart: 3, of which 3 were waited for; matrix products, arithmetic and copies ran while one was open for 1% of the time, Pallas kernels for 0%

commit v1 on v0

v1 whole, which is shorter than its diff:
```python
import functools
import math

import jax
import jax.numpy as jnp
from jax import lax
from jax.experimental import pallas as pl
from jax.experimental.pallas import tpu as pltpu
from jax.sharding import PartitionSpec as P

HEAD = 128
KEY_CHUNK = 1536


def slot_frames(pair_of_device, frame_of_tile, tile_count):
    slot_ids = jnp.arange(tile_count, dtype=jnp.int32)
    paired = jnp.repeat(pair_of_device, 2)
    tile_ids = jnp.where(slot_ids % 2 == 0, paired, tile_count - 1 - paired)
    matches = tile_ids[:, None] == jnp.arange(tile_count, dtype=jnp.int32)[None, :]
    return jnp.sum(jnp.where(matches, frame_of_tile[None, :], 0), axis=1)


def attn_kernel(frame_ref, q_ref, k_ref, v_ref, kf_ref, o_ref, s_sc):
    own_frame = frame_ref[pl.program_id(0)]
    key_count = k_ref.shape[0]
    chunks = key_count // KEY_CHUNK
    rows = q_ref.shape[0]
    score_scale = 1.0 / math.sqrt(HEAD)
    q = q_ref[...]

    def first(c, run_max):
        start = pl.multiple_of(c * KEY_CHUNK, KEY_CHUNK)
        k = k_ref[pl.ds(start, KEY_CHUNK), :]
        s = lax.dot_general(
            q, k, (((1,), (1,)), ((), ())), preferred_element_type=jnp.float32
        ) * score_scale
        allowed = kf_ref[:, pl.ds(start, KEY_CHUNK)] <= own_frame
        masked = jnp.where(allowed, s, jnp.float32(-1e30))
        s_sc[:, pl.ds(start, KEY_CHUNK)] = masked
        return jnp.maximum(run_max, jnp.max(masked, axis=1, keepdims=True))

    row_max = lax.fori_loop(
        0, chunks, first, jnp.full((rows, 1), -1e30, jnp.float32)
    )

    def second(c, carry):
        totals, acc = carry
        start = pl.multiple_of(c * KEY_CHUNK, KEY_CHUNK)
        allowed = kf_ref[:, pl.ds(start, KEY_CHUNK)] <= own_frame
        probs = jnp.where(
            allowed, jnp.exp(s_sc[:, pl.ds(start, KEY_CHUNK)] - row_max), jnp.float32(0.0)
        )
        totals = totals + jnp.sum(probs, axis=1, keepdims=True)
        v = v_ref[pl.ds(start, KEY_CHUNK), :]
        acc = acc + jnp.dot(
            probs.astype(jnp.bfloat16), v, preferred_element_type=jnp.float32
        )
        return totals, acc

    totals, acc = lax.fori_loop(
        0,
        chunks,
        second,
        (jnp.zeros((rows, 1), jnp.float32), jnp.zeros((rows, HEAD), jnp.float32)),
    )
    o_ref[...] = (acc / totals).astype(o_ref.dtype)


def head_attention(own_frames, queries, kv_rows, key_frame, head):
    tok_rows = queries.shape[0]
    tile_rows = tok_rows // 2
    key_count = kv_rows.shape[0]
    cost = pl.CostEstimate(
        flops=4 * tok_rows * key_count * HEAD,
        transcendentals=tok_rows * key_count,
        bytes_accessed=key_count * 2 * HEAD * 2 + tok_rows * HEAD * 4,
    )
    return pl.pallas_call(
        attn_kernel,
        out_shape=jax.ShapeDtypeStruct((tok_rows, HEAD), jnp.bfloat16),
        grid_spec=pltpu.PrefetchScalarGridSpec(
            num_scalar_prefetch=1,
            grid=(2,),
            in_specs=[
                pl.BlockSpec((tile_rows, HEAD), lambda i, fr: (i, head)),
                pl.BlockSpec((key_count, HEAD), lambda i, fr: (0, 0)),
                pl.BlockSpec((key_count, HEAD), lambda i, fr: (0, 1)),
                pl.BlockSpec((1, key_count), lambda i, fr: (0, 0)),
            ],
            out_specs=pl.BlockSpec((tile_rows, HEAD), lambda i, fr: (i, 0)),
            scratch_shapes=[pltpu.VMEM((tile_rows, key_count), jnp.float32)],
        ),
        compiler_params=pltpu.CompilerParams(vmem_limit_bytes=56 * 1024 * 1024),
        cost_estimate=cost,
    )(own_frames, queries, kv_rows, kv_rows, key_frame)


def local(queries, keys, values, resid, out_weight, gain, pair_of_device, frame_of_tile):
    tok_rows, row_width = queries.shape
    head_count = row_width // HEAD
    span_rows = tok_rows // 2
    seq_count = lax.axis_size("seq")
    seq_index = lax.axis_index("seq")
    slot_frame = slot_frames(pair_of_device, frame_of_tile, 2 * seq_count)
    own_frames = lax.dynamic_slice_in_dim(slot_frame, 2 * seq_index, 2, 0).astype(jnp.int32)
    key_frame = jnp.repeat(slot_frame.astype(jnp.int32), span_rows).reshape(1, -1)

    partial = None
    for head in range(head_count):
        cols = slice(head * HEAD, (head + 1) * HEAD)
        kv_local = jnp.concatenate([keys[:, cols], values[:, cols]], axis=1)
        kv_rows = lax.all_gather(kv_local, "seq", axis=0, tiled=True)
        attn_h = head_attention(own_frames, queries, kv_rows, key_frame, head)
        term = jnp.dot(attn_h, out_weight[cols, :], preferred_element_type=jnp.float32)
        partial = term if partial is None else partial + term

    branch = lax.psum_scatter(
        partial.astype(jnp.bfloat16),
        "tp",
        scatter_dimension=0,
        tiled=True,
    ).astype(jnp.float32)
    rms = jnp.sqrt(jnp.mean(branch * branch, axis=-1) + 1e-06)
    layer_out = resid.astype(jnp.float32) + gain[None, :] * branch / rms[:, None]
    return layer_out.astype(jnp.bfloat16)


def solution(mesh):
    in_specs = (
        P("seq", "tp"),
        P("seq", "tp"),
        P("seq", "tp"),
        P(("seq", "tp"), None),
        P("tp", None),
        P(),
        P(),
        P(),
    )
    out_specs = P(("seq", "tp"), None)
    return jax.shard_map(local, mesh=mesh, in_specs=in_specs, out_specs=out_specs, check_vma=False)
```

time: 437 us -> 391 us (0.89)
  local copies, waits for them, and re-layouts: 59.5 us -> 3.47 us
  Pallas kernels: 0 us -> 50.4 us
  matrix products: 49.3 us -> 23.4 us
  waiting for transfers between devices: 268 us -> 291 us
  other arithmetic: 26.6 us -> 6.37 us
  loops' own time: 16.4 us -> 0 us
    dynamic_slice x97 -> x1, local copies, waits for them, and re-layouts: 53.3 us -> 0.66 us  [local(): lax.dynamic_slice_in_dim(slot_frame, 2 * seq_index, 2, 0).astype(jnp.int32)]
    pallas_call x0 -> x3, Pallas kernels: none -> 50.4 us  [head_attention(): pl.pallas_call(attn_kernel, out_shape=jax.ShapeDtypeStruct((tok_rows, HEA...]
    dot_general x49 -> x3, matrix products: 49.3 us -> 23.4 us  [local(): jnp.dot(attn_h, out_weight[cols, :], preferred_element_type=jnp.float32)]
    all_gather x2 -> x3, waiting for transfers between devices: 212 us -> 236 us  [local(): kv_rows = lax.all_gather(kv_local, 'seq', axis=0, tiled=True)]
    reduce_sum x48 -> x0, other arithmetic: 17.2 us -> none  [the longest x24 14.9 us: softmax_update(): new_totals = run_totals * rescale + jnp.sum(probs, axis=-1)]
    another operation x1 -> x0, loops' own time: 16.4 us -> none  [local(): lax.scan(advance, empty_state(head_count, tok_rows), (key_blocks, value_b...]
  transfers between devices with their start and end apart: 3 -> 4, of which waited for: 3 -> 4; matrix products, arithmetic and copies ran while one was open for 1% -> 5% of each run, Pallas kernels for 0% -> 9%
where the time goes in v1:
time: 391 us; the launch traced here: 388 us
  waiting for transfers between devices  291 us (74%)
  Pallas kernels  50.4 us (13%)
  matrix products  23.4 us (6%)
  between operations  13.2 us (3%)
  other arithmetic  6.37 us (2%)
    all_gather x3, waiting for transfers between devices, local(): kv_rows = lax.all_gather(kv_local, 'seq', axis=0, tiled=True)  236 us
    reduce_scatter x1, waiting for transfers between devices, local(): lax.psum_scatter(partial.astype(jnp.bfloat16), 'tp', scatter_dimension=0,...  55.2 us
    pallas_call x3, Pallas kernels, head_attention(): pl.pallas_call(attn_kernel, out_shape=jax.ShapeDtypeStruct((tok_rows, HEA...  50.4 us
    dot_general x3, matrix products, local(): jnp.dot(attn_h, out_weight[cols, :], preferred_element_type=jnp.float32)  23.4 us
  transfers between devices with their start and end apart: 4, of which 4 were waited for; matrix products, arithmetic and copies ran while one was open for 5% of the time, Pallas kernels for 9%

profile of v1, /device:TPU:2, one launch (start us, length us, event | category | flops | bytes accessed | tf_op | source)
XLA Modules:
  0.0 388.0 jit_solution(2232958572707947982)
XLA Ops:
  6.5 0.0 all-gather.4.cloned.1.call-start
  6.5 1.2 fusion.9
  7.7 0.7 pad_maximum_fusion
  8.4 0.0 all-gather.4.cloned.1.call-update
  8.4 0.0 all-gather.6.cloned.1.call-start
  8.5 0.7 pad_maximum_fusion.1
  9.2 0.0 all-gather.6.cloned.1.call-update
  9.2 0.0 all-gather.8.cloned.1.call-start
  9.3 0.7 pad_maximum_fusion.2
  10.0 0.0 all-gather.8.cloned.1.call-update
  10.0 0.0 reduce-scatter.2.cloned.1.call-start
  10.0 0.7 broadcast_in_dim.23
  10.8 0.1 reshape.29
  10.9 0.8 select_reduce_fusion
  11.7 0.7 dynamic_slice.3.frame_ref
  12.4 0.1 broadcast_in_dim.26
  12.5 0.7 reshape_reshape.3.kf_ref
  13.2 94.5 %all-gather.4.cloned.1.call-done.k_ref.v_ref = bf16[12288,256]{1,0:T(8,128)(2,1)} async-done(((bf16[384,256]{1,0:T(8,128)(2,1)}), bf16[12288,256]{1,0:T(8,128)(2,1)}) %all-gather.4.cloned.1.call-update) | async-done | bytes 6291472 | tf_op jit(solution)/shard_map/all_gather | solution.py:112
  107.7 16.8 %shard_map.82 = bf16[384,128]{1,0:T(8,128)(2,1)} custom-call(s32[2]{0:T(128)} %dynamic_slice.3.frame_ref, bf16[384,384]{1,0:T(8,128)(2,1)} %q_ref.5, bf16[12288,256]{1,0:T(8,128)(2,1)} %all-gather.4.cloned.1.call-done.k_ref.v_ref, bf16[12288,256]{1,0:T(8,128)(2,1)} %all-gather.4.cloned.1.call-done.k_ref.v_ref, s32[1,12288]{1,0:T(1,128)} %reshape_reshape.3.kf_ref), custom_call_target="tpu_custom_call" | custom-call | flops 2415919104 | bytes 6488064 | tf_op jit(solution)/shard_map/pallas_call | solution.py:78
  124.5 77.1 %all-gather.6.cloned.1.call-done.k_ref.v_ref = bf16[12288,256]{1,0:T(8,128)(2,1)} async-done(((bf16[384,256]{1,0:T(8,128)(2,1)}), bf16[12288,256]{1,0:T(8,128)(2,1)}) %all-gather.6.cloned.1.call-update) | async-done | bytes 6291472 | tf_op jit(solution)/shard_map/all_gather | solution.py:112
  201.6 16.8 %shard_map.83 = bf16[384,128]{1,0:T(8,128)(2,1)} custom-call(s32[2]{0:T(128)} %dynamic_slice.3.frame_ref, bf16[384,384]{1,0:T(8,128)(2,1)} %q_ref.5, bf16[12288,256]{1,0:T(8,128)(2,1)} %all-gather.6.cloned.1.call-done.k_ref.v_ref, bf16[12288,256]{1,0:T(8,128)(2,1)} %all-gather.6.cloned.1.call-done.k_ref.v_ref, s32[1,12288]{1,0:T(1,128)} %reshape_reshape.3.kf_ref), custom_call_target="tpu_custom_call" | custom-call | flops 2415919104 | bytes 6488064 | tf_op jit(solution)/shard_map/pallas_call | solution.py:78
  218.4 6.5 %fusion.1 = f32[384,6144]{1,0:T(8,128)} fusion(bf16[384,128]{1,0:T(8,128)(2,1)} %shard_map.83, bf16[384,6144]{1,0:T(8,128)(2,1)} %param.12), kind=kOutput, calls=%fused_computation.2 | convolution fusion | flops 603979776 | bytes 11108352 | tf_op jit(solution)/shard_map/dot_general | solution.py:114
  224.9 6.5 %fusion.3 = f32[384,6144]{1,0:T(8,128)} fusion(bf16[384,128]{1,0:T(8,128)(2,1)S(1)} %copy-done.1, bf16[384,6144]{1,0:T(8,128)(2,1)} %param.12), kind=kOutput, calls=%fused_computation.4 | convolution fusion | flops 603979776 | bytes 11108352 | tf_op jit(solution)/shard_map/dot_general | solution.py:114
  231.4 64.2 %all-gather.8.cloned.1.call-done.k_ref.v_ref = bf16[12288,256]{1,0:T(8,128)(2,1)} async-done(((bf16[384,256]{1,0:T(8,128)(2,1)}), bf16[12288,256]{1,0:T(8,128)(2,1)}) %all-gather.8.cloned.1.call-update) | async-done | bytes 6291472 | tf_op jit(solution)/shard_map/all_gather | solution.py:112
  295.6 16.8 %shard_map.84 = bf16[384,128]{1,0:T(8,128)(2,1)} custom-call(s32[2]{0:T(128)} %dynamic_slice.3.frame_ref, bf16[384,384]{1,0:T(8,128)(2,1)} %q_ref.5, bf16[12288,256]{1,0:T(8,128)(2,1)} %all-gather.8.cloned.1.call-done.k_ref.v_ref, bf16[12288,256]{1,0:T(8,128)(2,1)} %all-gather.8.cloned.1.call-done.k_ref.v_ref, s32[1,12288]{1,0:T(1,128)} %reshape_reshape.3.kf_ref), custom_call_target="tpu_custom_call" | custom-call | flops 2415919104 | bytes 6488064 | tf_op jit(solution)/shard_map/pallas_call | solution.py:78
  312.4 10.4 %add_convert_fusion = bf16[384,6144]{1,0:T(8,128)(2,1)} fusion(f32[384,6144]{1,0:T(8,128)} %fusion.3, f32[384,6144]{1,0:T(8,128)} %fusion.1, bf16[384,128]{1,0:T(8,128)(2,1)} %shard_map.84, bf16[384,6144]{1,0:T(8,128)(2,1)} %param.12), kind=kOutput, calls=%fused_computation | convolution fusion | flops 611057664 | bytes 25264128 | tf_op jit(solution)/shard_map/dot_general | solution.py:114
  322.8 0.0 reduce-scatter.2.cloned.1.call-update
  322.9 55.2 %reduce-scatter.2.cloned.1.call-done = bf16[48,6144]{1,0:T(8,128)(2,1)} async-done(((bf16[384,6144]{1,0:T(8,128)(2,1)}), bf16[48,6144]{1,0:T(8,128)(2,1)}) %reduce-scatter.2.cloned.1.call-update) | async-done | bytes 589840 | tf_op jit(solution)/shard_map/reduce_scatter | solution.py:117
  378.0 1.3 fusion.8
  379.3 0.0 copy-done
  379.3 0.0 copy-done.2
  379.3 2.1 fusion.7
  (6 shorter events, 0.0 us)
Async XLA Ops:
  6.5 101.1 %all-gather.4.cloned.1.call-start = ((), (), s32[]{:S(2)}) async-start(), calls=%async_computation.1 | async-start | bytes 6488064 | tf_op jit(solution)/shard_map/all_gather | solution.py:112
  8.4 193.2 %all-gather.6.cloned.1.call-start = ((), (), s32[]{:S(2)}) async-start(), calls=%async_computation.2 | async-start | bytes 6488064 | tf_op jit(solution)/shard_map/all_gather | solution.py:112
  9.2 286.4 %all-gather.8.cloned.1.call-start = ((), (), s32[]{:S(2)}) async-start(), calls=%async_computation.3 | async-start | bytes 6488064 | tf_op jit(solution)/shard_map/all_gather | solution.py:112
  10.0 368.0 %reduce-scatter.2.cloned.1.call-start = ((), (), s32[]{:S(2)}) async-start(), calls=%async_computation.4 | async-start | bytes 5308416 | tf_op jit(solution)/shard_map/reduce_scatter | solution.py:117
  218.4 6.5 %copy-start.1 = (bf16[384,128]{1,0:T(8,128)(2,1)S(1)}, bf16[384,128]{1,0:T(8,128)(2,1)}, u32[]{:S(2)}) copy-start(bf16[384,128]{1,0:T(8,128)(2,1)} %shard_map.82) | copy-start | bytes 294916
  322.8 56.5 %copy-start = (bf16[48,6144]{1,0:T(8,128)(2,1)S(1)}, bf16[48,6144]{1,0:T(8,128)(2,1)}, u32[]{:S(2)}) copy-start(bf16[48,6144]{1,0:T(8,128)(2,1)} %param.11) | copy-start | bytes 1769476
  322.8 56.5 %copy-start.2 = (f32[6144]{0:T(1024)S(1)}, f32[6144]{0:T(1024)}, u32[]{:S(2)}) copy-start(f32[6144]{0:T(1024)} %param.13) | copy-start | bytes 73732
Sparse Core Ops, SparseCore 0:
  10.1 97.4 all-gather.3
  110.4 91.1 all-gather.5
  204.4 91.1 all-gather.7
  323.0 54.9 reduce-scatter.1

commit v2 on v1

--- a/solution.py
+++ b/solution.py
@@ -20,8 +20,7 @@
     return jnp.sum(jnp.where(matches, frame_of_tile[None, :], 0), axis=1)
 
 
-def attn_kernel(frame_ref, q_ref, k_ref, v_ref, kf_ref, o_ref, s_sc):
-    own_frame = frame_ref[pl.program_id(0)]
+def attn_kernel(q_ref, k_ref, v_ref, kf_ref, o_ref, s_sc):
     key_count = k_ref.shape[0]
     chunks = key_count // KEY_CHUNK
     rows = q_ref.shape[0]
@@ -34,8 +33,7 @@
         s = lax.dot_general(
             q, k, (((1,), (1,)), ((), ())), preferred_element_type=jnp.float32
         ) * score_scale
-        allowed = kf_ref[:, pl.ds(start, KEY_CHUNK)] <= own_frame
-        masked = jnp.where(allowed, s, jnp.float32(-1e30))
+        masked = s + kf_ref[:, pl.ds(start, KEY_CHUNK)]
         s_sc[:, pl.ds(start, KEY_CHUNK)] = masked
         return jnp.maximum(run_max, jnp.max(masked, axis=1, keepdims=True))
 
@@ -46,10 +44,7 @@
     def second(c, carry):
         totals, acc = carry
         start = pl.multiple_of(c * KEY_CHUNK, KEY_CHUNK)
-        allowed = kf_ref[:, pl.ds(start, KEY_CHUNK)] <= own_frame
-        probs = jnp.where(
-            allowed, jnp.exp(s_sc[:, pl.ds(start, KEY_CHUNK)] - row_max), jnp.float32(0.0)
-        )
+        probs = jnp.exp(s_sc[:, pl.ds(start, KEY_CHUNK)] - row_max)
         totals = totals + jnp.sum(probs, axis=1, keepdims=True)
         v = v_ref[pl.ds(start, KEY_CHUNK), :]
         acc = acc + jnp.dot(
@@ -66,10 +61,11 @@
     o_ref[...] = (acc / totals).astype(o_ref.dtype)
 
 
-def head_attention(own_frames, queries, kv_rows, key_frame, head):
+def head_attention(queries, kv_rows, key_bias, head):
     tok_rows = queries.shape[0]
     tile_rows = tok_rows // 2
     key_count = kv_rows.shape[0]
+    head_count = queries.shape[1] // HEAD
     cost = pl.CostEstimate(
         flops=4 * tok_rows * key_count * HEAD,
         transcendentals=tok_rows * key_count,
@@ -78,21 +74,18 @@
     return pl.pallas_call(
         attn_kernel,
         out_shape=jax.ShapeDtypeStruct((tok_rows, HEAD), jnp.bfloat16),
-        grid_spec=pltpu.PrefetchScalarGridSpec(
-            num_scalar_prefetch=1,
-            grid=(2,),
-            in_specs=[
-                pl.BlockSpec((tile_rows, HEAD), lambda i, fr: (i, head)),
-                pl.BlockSpec((key_count, HEAD), lambda i, fr: (0, 0)),
-                pl.BlockSpec((key_count, HEAD), lambda i, fr: (0, 1)),
-                pl.BlockSpec((1, key_count), lambda i, fr: (0, 0)),
-            ],
-            out_specs=pl.BlockSpec((tile_rows, HEAD), lambda i, fr: (i, 0)),
-            scratch_shapes=[pltpu.VMEM((tile_rows, key_count), jnp.float32)],
-        ),
+        grid=(2,),
+        in_specs=[
+            pl.BlockSpec((tile_rows, HEAD), lambda i: (i, head)),
+            pl.BlockSpec((key_count, HEAD), lambda i: (0, head)),
+            pl.BlockSpec((key_count, HEAD), lambda i: (0, head_count + head)),
+            pl.BlockSpec((None, 1, key_count), lambda i: (i, 0, 0)),
+        ],
+        out_specs=pl.BlockSpec((tile_rows, HEAD), lambda i: (i, 0)),
+        scratch_shapes=[pltpu.VMEM((tile_rows, key_count), jnp.float32)],
         compiler_params=pltpu.CompilerParams(vmem_limit_bytes=56 * 1024 * 1024),
         cost_estimate=cost,
-    )(own_frames, queries, kv_rows, kv_rows, key_frame)
+    )(queries, kv_rows, kv_rows, key_bias)
 
 
 def local(queries, keys, values, resid, out_weight, gain, pair_of_device, frame_of_tile):
@@ -103,14 +96,17 @@
     seq_index = lax.axis_index("seq")
     slot_frame = slot_frames(pair_of_device, frame_of_tile, 2 * seq_count)
     own_frames = lax.dynamic_slice_in_dim(slot_frame, 2 * seq_index, 2, 0).astype(jnp.int32)
-    key_frame = jnp.repeat(slot_frame.astype(jnp.int32), span_rows).reshape(1, -1)
+    key_frame = jnp.repeat(slot_frame.astype(jnp.int32), span_rows)
+    key_bias = jnp.where(
+        key_frame[None, :] <= own_frames[:, None], jnp.float32(0.0), jnp.float32(-1e30)
+    ).reshape(2, 1, -1)
 
+    kv_local = jnp.concatenate([keys, values], axis=1)
+    kv_rows = lax.all_gather(kv_local, "seq", axis=0, tiled=True)
     partial = None
     for head in range(head_count):
         cols = slice(head * HEAD, (head + 1) * HEAD)
-        kv_local = jnp.concatenate([keys[:, cols], values[:, cols]], axis=1)
-        kv_rows = lax.all_gather(kv_local, "seq", axis=0, tiled=True)
-        attn_h = head_attention(own_frames, queries, kv_rows, key_frame, head)
+        attn_h = head_attention(queries, kv_rows, key_bias, head)
         term = jnp.dot(attn_h, out_weight[cols, :], preferred_element_type=jnp.float32)
         partial = term if partial is None else partial + term
 

time: 391 us -> 299 us (0.76)
  waiting for transfers between devices: 291 us -> 205 us
  Pallas kernels: 50.4 us -> 46.4 us
    all_gather x3 -> x1, waiting for transfers between devices: 236 us -> 150 us  [local(): kv_rows = lax.all_gather(kv_local, 'seq', axis=0, tiled=True)]
    pallas_call x3, Pallas kernels: 50.4 us -> 46.4 us  [head_attention(): pl.pallas_call(attn_kernel, out_shape=jax.ShapeDtypeStruct((tok_rows, HEA...]
  transfers between devices with their start and end apart: 4 -> 2, of which waited for: 4 -> 2; matrix products, arithmetic and copies ran while one was open for 5% -> 1% of each run, Pallas kernels for 9% -> 0%
where the time goes in v2:
time: 299 us; the launch traced here: 296 us
  waiting for transfers between devices  205 us (69%)
  Pallas kernels  46.4 us (16%)
  matrix products  22.5 us (8%)
  between operations  13.5 us (5%)
  other arithmetic  6.94 us (2%)
    all_gather x1, waiting for transfers between devices, local(): kv_rows = lax.all_gather(kv_local, 'seq', axis=0, tiled=True)  150 us
    reduce_scatter x1, waiting for transfers between devices, local(): lax.psum_scatter(partial.astype(jnp.bfloat16), 'tp', scatter_dimension=0,...  55.2 us
    pallas_call x3, Pallas kernels, head_attention(): pl.pallas_call(attn_kernel, out_shape=jax.ShapeDtypeStruct((tok_rows, HEA...  46.4 us
    dot_general x3, matrix products, local(): jnp.dot(attn_h, out_weight[cols, :], preferred_element_type=jnp.float32)  22.5 us
  transfers between devices with their start and end apart: 2, of which 2 were waited for; matrix products, arithmetic and copies ran while one was open for 1% of the time, Pallas kernels for 0%

profile of v2, /device:TPU:2, one launch (start us, length us, event | category | flops | bytes accessed | tf_op | source)
XLA Modules:
  0.0 295.9 jit_solution(8027631513190362034)
XLA Ops:
  6.5 0.0 all-gather.2.cloned.1.call-start
  6.5 1.9 pad_maximum_fusion
  8.5 0.0 all-gather.2.cloned.1.call-update
  8.5 0.0 reduce-scatter.2.cloned.1.call-start
  8.5 0.7 broadcast_in_dim.32
  9.3 0.1 reshape.83
  9.4 0.8 select_reduce_fusion
  10.2 0.1 dynamic_slice.3
  10.3 0.1 broadcast_in_dim.35
  10.4 0.1 le.22
  10.5 0.8 compare_select_fusion.kf_ref
  11.2 150.1 %all-gather.2.cloned.1.call-done.k_ref.v_ref = bf16[12288,768]{1,0:T(8,128)(2,1)} async-done(((bf16[384,768]{1,0:T(8,128)(2,1)}), bf16[12288,768]{1,0:T(8,128)(2,1)}) %all-gather.2.cloned.1.call-update) | async-done | bytes 18874384 | tf_op jit(solution)/shard_map/all_gather | solution.py:105
  161.4 15.5 %shard_map.82 = bf16[384,128]{1,0:T(8,128)(2,1)} custom-call(bf16[384,384]{1,0:T(8,128)(2,1)} %q_ref.5, bf16[12288,768]{1,0:T(8,128)(2,1)} %all-gather.2.cloned.1.call-done.k_ref.v_ref, bf16[12288,768]{1,0:T(8,128)(2,1)} %all-gather.2.cloned.1.call-done.k_ref.v_ref, f32[2,1,12288]{2,1,0:T(1,128)} %compare_select_fusion.kf_ref), custom_call_target="tpu_custom_call" | custom-call | flops 2415919104 | bytes 6488064 | tf_op jit(solution)/shard_map/pallas_call | solution.py:74
  176.8 0.0 slice-start
  176.8 6.7 %fusion.3 = f32[384,6144]{1,0:T(8,128)} fusion(bf16[384,128]{1,0:T(8,128)(2,1)} %shard_map.82, bf16[384,6144]{1,0:T(8,128)(2,1)} %param.12), kind=kOutput, calls=%fused_computation.4 | convolution fusion | flops 603979776 | bytes 11108352 | tf_op jit(solution)/shard_map/dot_general | solution.py:110
  183.5 0.0 slice-start.1
  183.5 15.5 %shard_map.83 = bf16[384,128]{1,0:T(8,128)(2,1)} custom-call(bf16[384,384]{1,0:T(8,128)(2,1)} %q_ref.5, bf16[12288,768]{1,0:T(8,128)(2,1)} %all-gather.2.cloned.1.call-done.k_ref.v_ref, bf16[12288,768]{1,0:T(8,128)(2,1)} %all-gather.2.cloned.1.call-done.k_ref.v_ref, f32[2,1,12288]{2,1,0:T(1,128)} %compare_select_fusion.kf_ref), custom_call_target="tpu_custom_call" | custom-call | flops 2415919104 | bytes 6488064 | tf_op jit(solution)/shard_map/pallas_call | solution.py:74
  199.0 0.0 slice-done
  199.1 0.0 slice-done.1
  199.1 5.9 %fusion.1 = f32[384,6144]{1,0:T(8,128)} fusion(bf16[384,128]{1,0:T(8,128)(2,1)} %shard_map.83, bf16[384,6144]{1,0:T(8,128)(2,1)S(1)} %bitcast.4), kind=kOutput, calls=%fused_computation.2 | convolution fusion | flops 603979776 | bytes 11108352 | tf_op jit(solution)/shard_map/dot_general | solution.py:110
  205.0 15.5 %shard_map.84 = bf16[384,128]{1,0:T(8,128)(2,1)} custom-call(bf16[384,384]{1,0:T(8,128)(2,1)} %q_ref.5, bf16[12288,768]{1,0:T(8,128)(2,1)} %all-gather.2.cloned.1.call-done.k_ref.v_ref, bf16[12288,768]{1,0:T(8,128)(2,1)} %all-gather.2.cloned.1.call-done.k_ref.v_ref, f32[2,1,12288]{2,1,0:T(1,128)} %compare_select_fusion.kf_ref), custom_call_target="tpu_custom_call" | custom-call | flops 2415919104 | bytes 6488064 | tf_op jit(solution)/shard_map/pallas_call | solution.py:74
  220.5 9.9 %add_convert_fusion = bf16[384,6144]{1,0:T(8,128)(2,1)} fusion(f32[384,6144]{1,0:T(8,128)} %fusion.3, f32[384,6144]{1,0:T(8,128)} %fusion.1, bf16[384,128]{1,0:T(8,128)(2,1)} %shard_map.84, bf16[384,6144]{1,0:T(8,128)(2,1)S(1)} %bitcast.4), kind=kOutput, calls=%fused_computation | convolution fusion | flops 611057664 | bytes 25264128 | tf_op jit(solution)/shard_map/dot_general | solution.py:110
  230.3 0.0 copy-start
  230.3 0.0 copy-start.1
  230.4 0.0 reduce-scatter.2.cloned.1.call-update
  230.4 55.2 %reduce-scatter.2.cloned.1.call-done = bf16[48,6144]{1,0:T(8,128)(2,1)} async-done(((bf16[384,6144]{1,0:T(8,128)(2,1)}), bf16[48,6144]{1,0:T(8,128)(2,1)}) %reduce-scatter.2.cloned.1.call-update) | async-done | bytes 589840 | tf_op jit(solution)/shard_map/reduce_scatter | solution.py:113
  285.6 1.3 fusion.8
  286.9 0.0 copy-done
  286.9 0.0 copy-done.1
  286.9 2.1 fusion.7
  (3 shorter events, 0.0 us)
Async XLA Ops:
  6.5 154.8 %all-gather.2.cloned.1.call-start = ((), (), s32[]{:S(2)}) async-start(), calls=%async_computation.1 | async-start | bytes 19464192 | tf_op jit(solution)/shard_map/all_gather | solution.py:105
  8.5 277.1 %reduce-scatter.2.cloned.1.call-start = ((), (), s32[]{:S(2)}) async-start(), calls=%async_computation.2 | async-start | bytes 5308416 | tf_op jit(solution)/shard_map/reduce_scatter | solution.py:113
  176.8 22.2 %slice-start = ((s8[4718592]{0:T(1024)(128)(4,1)}), s8[4194304]{0:T(1024)(128)(4,1)S(1)}, s32[]{:S(2)}) async-start(s8[4718592]{0:T(1024)(128)(4,1)} %bitcast.3), calls=%async_computation.3 | async-start | bytes 8388608
  183.5 15.5 %slice-start.1 = ((s8[4718592]{0:T(1024)(128)(4,1)}), s8[524288]{0:T(1024)(128)(4,1)S(1)}, s32[]{:S(2)}) async-start(s8[4718592]{0:T(1024)(128)(4,1)} %bitcast.3), calls=%async_computation.4 | async-start | bytes 1048576
  230.3 56.6 %copy-start = (bf16[48,6144]{1,0:T(8,128)(2,1)S(1)}, bf16[48,6144]{1,0:T(8,128)(2,1)}, u32[]{:S(2)}) copy-start(bf16[48,6144]{1,0:T(8,128)(2,1)} %param.11) | copy-start | bytes 1769476
  230.3 56.6 %copy-start.1 = (f32[6144]{0:T(1024)S(1)}, f32[6144]{0:T(1024)}, u32[]{:S(2)}) copy-start(f32[6144]{0:T(1024)} %param.13) | copy-start | bytes 73732
Sparse Core Ops, SparseCore 0:
  10.1 151.1 all-gather.1
  230.5 55.0 reduce-scatter.1

commit v3 on v2

--- a/solution.py
+++ b/solution.py
@@ -61,27 +61,27 @@
     o_ref[...] = (acc / totals).astype(o_ref.dtype)
 
 
-def head_attention(queries, kv_rows, key_bias, head):
+def attention(queries, kv_rows, key_bias):
     tok_rows = queries.shape[0]
     tile_rows = tok_rows // 2
     key_count = kv_rows.shape[0]
     head_count = queries.shape[1] // HEAD
     cost = pl.CostEstimate(
-        flops=4 * tok_rows * key_count * HEAD,
-        transcendentals=tok_rows * key_count,
-        bytes_accessed=key_count * 2 * HEAD * 2 + tok_rows * HEAD * 4,
+        flops=4 * tok_rows * key_count * HEAD * head_count,
+        transcendentals=tok_rows * key_count * head_count,
+        bytes_accessed=(key_count * 2 * HEAD * 2 + tok_rows * HEAD * 4) * head_count,
     )
     return pl.pallas_call(
         attn_kernel,
-        out_shape=jax.ShapeDtypeStruct((tok_rows, HEAD), jnp.bfloat16),
-        grid=(2,),
+        out_shape=jax.ShapeDtypeStruct((tok_rows, head_count * HEAD), jnp.bfloat16),
+        grid=(head_count, 2),
         in_specs=[
-            pl.BlockSpec((tile_rows, HEAD), lambda i: (i, head)),
-            pl.BlockSpec((key_count, HEAD), lambda i: (0, head)),
-            pl.BlockSpec((key_count, HEAD), lambda i: (0, head_count + head)),
-            pl.BlockSpec((None, 1, key_count), lambda i: (i, 0, 0)),
+            pl.BlockSpec((tile_rows, HEAD), lambda h, i: (i, h)),
+            pl.BlockSpec((key_count, HEAD), lambda h, i: (0, h)),
+            pl.BlockSpec((key_count, HEAD), lambda h, i: (0, head_count + h)),
+            pl.BlockSpec((None, 1, key_count), lambda h, i: (i, 0, 0)),
         ],
-        out_specs=pl.BlockSpec((tile_rows, HEAD), lambda i: (i, 0)),
+        out_specs=pl.BlockSpec((tile_rows, HEAD), lambda h, i: (i, h)),
         scratch_shapes=[pltpu.VMEM((tile_rows, key_count), jnp.float32)],
         compiler_params=pltpu.CompilerParams(vmem_limit_bytes=56 * 1024 * 1024),
         cost_estimate=cost,
@@ -103,12 +103,8 @@
 
     kv_local = jnp.concatenate([keys, values], axis=1)
     kv_rows = lax.all_gather(kv_local, "seq", axis=0, tiled=True)
-    partial = None
-    for head in range(head_count):
-        cols = slice(head * HEAD, (head + 1) * HEAD)
-        attn_h = head_attention(queries, kv_rows, key_bias, head)
-        term = jnp.dot(attn_h, out_weight[cols, :], preferred_element_type=jnp.float32)
-        partial = term if partial is None else partial + term
+    attn = attention(queries, kv_rows, key_bias)
+    partial = jnp.dot(attn, out_weight, preferred_element_type=jnp.float32)
 
     branch = lax.psum_scatter(
         partial.astype(jnp.bfloat16),

time: 299 us -> 277 us (0.926)
  matrix products: 22.5 us -> 7.16 us
  Pallas kernels: 46.4 us -> 39.5 us
    dot_general x3 -> x1, matrix products: 22.5 us -> 7.16 us  [local(): partial = jnp.dot(attn, out_weight, preferred_element_type=jnp.float32)]
    pallas_call x3 -> x1, Pallas kernels: 46.4 us -> 39.5 us  [attention(): pl.pallas_call(attn_kernel, out_shape=jax.ShapeDtypeStruct((tok_rows, hea...]
where the time goes in v3:
time: 277 us; the launch traced here: 274 us
  waiting for transfers between devices  207 us (75%)
  Pallas kernels  39.5 us (14%)
  between operations  13.5 us (5%)
  matrix products  7.16 us (3%)
  other arithmetic  6.3 us (2%)
    all_gather x1, waiting for transfers between devices, local(): kv_rows = lax.all_gather(kv_local, 'seq', axis=0, tiled=True)  151 us
    reduce_scatter x1, waiting for transfers between devices, local(): lax.psum_scatter(partial.astype(jnp.bfloat16), 'tp', scatter_dimension=0,...  55.2 us
    pallas_call x1, Pallas kernels, attention(): pl.pallas_call(attn_kernel, out_shape=jax.ShapeDtypeStruct((tok_rows, hea...  39.5 us
    dot_general x1, matrix products, local(): partial = jnp.dot(attn, out_weight, preferred_element_type=jnp.float32)  7.16 us
  transfers between devices with their start and end apart: 2, of which 2 were waited for; matrix products, arithmetic and copies ran while one was open for 1% of the time, Pallas kernels for 0%

profile of v3, /device:TPU:2, one launch (start us, length us, event | category | flops | bytes accessed | tf_op | source)
XLA Modules:
  0.0 273.6 jit_solution(7640203535805996160)
XLA Ops:
  6.5 0.0 copy-start.2
  6.5 0.0 copy-start.3
  6.5 0.0 all-gather.2.cloned.1.call-start
  6.5 1.9 pad_maximum_fusion
  8.5 0.0 all-gather.2.cloned.1.call-update
  8.5 0.0 reduce-scatter.2.cloned.1.call-start
  8.6 0.0 copy-done.2
  8.6 0.1 broadcast_in_dim.32
  8.6 0.1 reshape.83
  8.8 0.0 copy-done.3
  8.8 0.2 select_reduce_fusion
  8.9 0.1 broadcast_in_dim.35
  9.0 0.1 le.22
  9.1 0.1 dynamic_slice.3
  9.2 0.8 compare_select_fusion.kf_ref
  10.0 151.4 %all-gather.2.cloned.1.call-done.k_ref.v_ref = bf16[12288,768]{1,0:T(8,128)(2,1)} async-done(((bf16[384,768]{1,0:T(8,128)(2,1)}), bf16[12288,768]{1,0:T(8,128)(2,1)}) %all-gather.2.cloned.1.call-update) | async-done | bytes 18874384 | tf_op jit(solution)/shard_map/all_gather | solution.py:105
  161.4 39.5 %shard_map.82 = bf16[384,384]{1,0:T(8,128)(2,1)} custom-call(bf16[384,384]{1,0:T(8,128)(2,1)} %q_ref.1, bf16[12288,768]{1,0:T(8,128)(2,1)} %all-gather.2.cloned.1.call-done.k_ref.v_ref, bf16[12288,768]{1,0:T(8,128)(2,1)} %all-gather.2.cloned.1.call-done.k_ref.v_ref, f32[2,1,12288]{2,1,0:T(1,128)} %compare_select_fusion.kf_ref), custom_call_target="tpu_custom_call" | custom-call | flops 7247757312 | bytes 19464192 | tf_op jit(solution)/shard_map/pallas_call | solution.py:74
  200.9 7.2 %convolution_convert_fusion = bf16[384,6144]{1,0:T(8,128)(2,1)} fusion(bf16[384,384]{1,0:T(8,128)(2,1)} %shard_map.82, bf16[384,6144]{1,0:T(8,128)(2,1)} %param.12), kind=kOutput, calls=%fused_computation | convolution fusion | flops 1814298624 | bytes 9732096 | tf_op jit(solution)/shard_map/dot_general | solution.py:107
  208.0 0.0 copy-start
  208.0 0.0 copy-start.1
  208.0 0.0 reduce-scatter.2.cloned.1.call-update
  208.1 55.2 %reduce-scatter.2.cloned.1.call-done = bf16[48,6144]{1,0:T(8,128)(2,1)} async-done(((bf16[384,6144]{1,0:T(8,128)(2,1)}), bf16[48,6144]{1,0:T(8,128)(2,1)}) %reduce-scatter.2.cloned.1.call-update) | async-done | bytes 589840 | tf_op jit(solution)/shard_map/reduce_scatter | solution.py:109
  263.3 1.3 fusion.3
  264.6 0.0 copy-done
  264.6 0.0 copy-done.1
  264.6 2.1 fusion.2
  (2 shorter events, 0.0 us)
Async XLA Ops:
  6.5 2.0 copy-start.2
  6.5 2.2 copy-start.3
  6.5 154.8 %all-gather.2.cloned.1.call-start = ((), (), s32[]{:S(2)}) async-start(), calls=%async_computation.1 | async-start | bytes 19464192 | tf_op jit(solution)/shard_map/all_gather | solution.py:105
  8.5 254.8 %reduce-scatter.2.cloned.1.call-start = ((), (), s32[]{:S(2)}) async-start(), calls=%async_computation.2 | async-start | bytes 5308416 | tf_op jit(solution)/shard_map/reduce_scatter | solution.py:109
  208.0 56.6 %copy-start = (bf16[48,6144]{1,0:T(8,128)(2,1)S(1)}, bf16[48,6144]{1,0:T(8,128)(2,1)}, u32[]{:S(2)}) copy-start(bf16[48,6144]{1,0:T(8,128)(2,1)} %param.11) | copy-start | bytes 1769476
  208.0 56.6 %copy-start.1 = (f32[6144]{0:T(1024)S(1)}, f32[6144]{0:T(1024)}, u32[]{:S(2)}) copy-start(f32[6144]{0:T(1024)} %param.13) | copy-start | bytes 73732
Sparse Core Ops, SparseCore 0:
  10.1 151.1 all-gather.1
  208.2 55.0 reduce-scatter.1

commit v4 on v3

v4 whole, which is shorter than its diff:
```python
import functools
import math

import jax
import jax.numpy as jnp
from jax import lax
from jax.experimental import pallas as pl
from jax.experimental.pallas import tpu as pltpu
from jax.sharding import PartitionSpec as P

HEAD = 128


def slot_frames(pair_of_device, frame_of_tile, tile_count):
    slot_ids = jnp.arange(tile_count, dtype=jnp.int32)
    paired = jnp.repeat(pair_of_device, 2)
    tile_ids = jnp.where(slot_ids % 2 == 0, paired, tile_count - 1 - paired)
    matches = tile_ids[:, None] == jnp.arange(tile_count, dtype=jnp.int32)[None, :]
    return jnp.sum(jnp.where(matches, frame_of_tile[None, :], 0), axis=1)


def attn_kernel(order_ref, count_ref, q_ref, k_ref, v_ref, o_ref, s_sc):
    tile = pl.program_id(1)
    visible = count_ref[tile]
    rows = q_ref.shape[0]
    span = s_sc.shape[1]
    score_scale = 1.0 / math.sqrt(HEAD)
    q = q_ref[...]

    def first(j, run_max):
        slot = order_ref[tile, j]
        start = pl.multiple_of(slot * span, span)
        k = k_ref[pl.ds(start, span), :]
        s = lax.dot_general(
            q, k, (((1,), (1,)), ((), ())), preferred_element_type=jnp.float32
        ) * score_scale
        s_sc[j] = s
        return jnp.maximum(run_max, jnp.max(s, axis=1, keepdims=True))

    row_max = lax.fori_loop(0, visible, first, jnp.full((rows, 1), -1e30, jnp.float32))

    def second(j, carry):
        totals, acc = carry
        slot = order_ref[tile, j]
        start = pl.multiple_of(slot * span, span)
        probs = jnp.exp(s_sc[j] - row_max)
        totals = totals + jnp.sum(probs, axis=1, keepdims=True)
        v = v_ref[pl.ds(start, span), :]
        acc = acc + jnp.dot(probs.astype(jnp.bfloat16), v, preferred_element_type=jnp.float32)
        return totals, acc

    totals, acc = lax.fori_loop(
        0,
        visible,
        second,
        (jnp.zeros((rows, 1), jnp.float32), jnp.zeros((rows, HEAD), jnp.float32)),
    )
    o_ref[...] = (acc / totals).astype(o_ref.dtype)


def attention(queries, kv_rows, order, count):
    tok_rows = queries.shape[0]
    tile_rows = tok_rows // 2
    key_count = kv_rows.shape[0]
    head_count = queries.shape[1] // HEAD
    slot_count = order.shape[1]
    span = key_count // slot_count
    cost = pl.CostEstimate(
        flops=2 * tok_rows * key_count * HEAD * head_count,
        transcendentals=tok_rows * key_count * head_count // 2,
        bytes_accessed=(key_count * 2 * HEAD * 2 + tok_rows * HEAD * 4) * head_count,
    )
    return pl.pallas_call(
        attn_kernel,
        out_shape=jax.ShapeDtypeStruct((tok_rows, head_count * HEAD), jnp.bfloat16),
        grid_spec=pltpu.PrefetchScalarGridSpec(
            num_scalar_prefetch=2,
            grid=(head_count, 2),
            in_specs=[
                pl.BlockSpec((tile_rows, HEAD), lambda h, i, o, c: (i, h)),
                pl.BlockSpec((key_count, HEAD), lambda h, i, o, c: (0, h)),
                pl.BlockSpec((key_count, HEAD), lambda h, i, o, c: (0, head_count + h)),
            ],
            out_specs=pl.BlockSpec((tile_rows, HEAD), lambda h, i, o, c: (i, h)),
            scratch_shapes=[pltpu.VMEM((slot_count, tile_rows, span), jnp.float32)],
        ),
        compiler_params=pltpu.CompilerParams(vmem_limit_bytes=56 * 1024 * 1024),
        cost_estimate=cost,
    )(order, count, queries, kv_rows, kv_rows)


def local(queries, keys, values, resid, out_weight, gain, pair_of_device, frame_of_tile):
    tok_rows, row_width = queries.shape
    head_count = row_width // HEAD
    span_rows = tok_rows // 2
    seq_count = lax.axis_size("seq")
    seq_index = lax.axis_index("seq")
    slot_frame = slot_frames(pair_of_device, frame_of_tile, 2 * seq_count)
    own_frames = lax.dynamic_slice_in_dim(slot_frame, 2 * seq_index, 2, 0).astype(jnp.int32)
    slot_count = slot_frame.shape[0]
    slot_ids = jnp.arange(slot_count, dtype=jnp.int32)
    allowed = (slot_frame[None, :] <= own_frames[:, None]).astype(jnp.int32)
    count = jnp.sum(allowed, axis=1).astype(jnp.int32)
    place = jnp.where(
        allowed == 1,
        jnp.cumsum(allowed, axis=1) - 1,
        count[:, None] + jnp.cumsum(1 - allowed, axis=1) - 1,
    )
    order = jnp.sum(
        jnp.where(place[:, :, None] == slot_ids[None, None, :], slot_ids[None, :, None], 0),
        axis=1,
    ).astype(jnp.int32)

    kv_local = jnp.concatenate([keys, values], axis=1)
    kv_rows = lax.all_gather(kv_local, "seq", axis=0, tiled=True)
    attn = attention(queries, kv_rows, order, count)
    partial = jnp.dot(attn, out_weight, preferred_element_type=jnp.float32)

    branch = lax.psum_scatter(
        partial.astype(jnp.bfloat16),
        "tp",
        scatter_dimension=0,
        tiled=True,
    ).astype(jnp.float32)
    rms = jnp.sqrt(jnp.mean(branch * branch, axis=-1) + 1e-06)
    layer_out = resid.astype(jnp.float32) + gain[None, :] * branch / rms[:, None]
    return layer_out.astype(jnp.bfloat16)


def solution(mesh):
    in_specs = (
        P("seq", "tp"),
        P("seq", "tp"),
        P("seq", "tp"),
        P(("seq", "tp"), None),
        P("tp", None),
        P(),
        P(),
        P(),
    )
    out_specs = P(("seq", "tp"), None)
    return jax.shard_map(local, mesh=mesh, in_specs=in_specs, out_specs=out_specs, check_vma=False)
```

time: 277 us -> 350 us (1.26)
  Pallas kernels: 39.5 us -> 99.8 us
  waiting for transfers between devices: 207 us -> 217 us
    pallas_call x1, Pallas kernels: 39.5 us -> 99.8 us  [attention(): pl.pallas_call(attn_kernel, out_shape=jax.ShapeDtypeStruct((tok_rows, hea...]
    reduce_scatter x1, waiting for transfers between devices: 55.2 us -> 66.4 us  [local(): lax.psum_scatter(partial.astype(jnp.bfloat16), 'tp', scatter_dimension=0,...]
where the time goes in v4:
time: 350 us; the launch traced here: 345 us
  waiting for transfers between devices  217 us (62%)
  Pallas kernels  99.8 us (29%)
  between operations  13.5 us (4%)
  matrix products  7.18 us (2%)
  other arithmetic  7.03 us (2%)
    all_gather x1, waiting for transfers between devices, local(): kv_rows = lax.all_gather(kv_local, 'seq', axis=0, tiled=True)  151 us
    pallas_call x1, Pallas kernels, attention(): pl.pallas_call(attn_kernel, out_shape=jax.ShapeDtypeStruct((tok_rows, hea...  99.8 us
    reduce_scatter x1, waiting for transfers between devices, local(): lax.psum_scatter(partial.astype(jnp.bfloat16), 'tp', scatter_dimension=0,...  66.4 us
    dot_general x1, matrix products, local(): partial = jnp.dot(attn, out_weight, preferred_element_type=jnp.float32)  7.18 us
  transfers between devices with their start and end apart: 2, of which 2 were waited for; matrix products, arithmetic and copies ran while one was open for 1% of the time, Pallas kernels for 0%

profile of v4, /device:TPU:2, one launch (start us, length us, event | category | flops | bytes accessed | tf_op | source)
XLA Modules:
  0.0 345.0 jit_solution(11937924077113739985)
XLA Ops:
  6.5 0.0 copy-start.3
  6.5 0.0 copy-start.4
  6.5 0.0 all-gather.2.cloned.1.call-start
  6.5 1.9 pad_maximum_fusion
  8.5 0.0 all-gather.2.cloned.1.call-update
  8.5 0.0 reduce-scatter.2.cloned.1.call-start
  8.6 0.0 copy-done.3
  8.6 0.1 broadcast_in_dim.26
  8.6 0.1 reshape.134
  8.8 0.0 copy-done.4
  8.8 0.2 select_reduce_fusion.1
  8.9 0.1 dynamic_slice.3
  9.0 0.1 compare_convert_fusion
  9.1 0.2 reduce_window_sum.17
  9.3 0.2 fusion.5
  9.5 0.0 copy-start.2
  9.5 0.2 reduce_window_sum.18
  9.8 0.1 compare_select_fusion
  9.9 0.7 select_reduce_fusion.order_ref
  10.5 150.8 %all-gather.2.cloned.1.call-done.k_ref.v_ref = bf16[12288,768]{1,0:T(8,128)(2,1)} async-done(((bf16[384,768]{1,0:T(8,128)(2,1)}), bf16[12288,768]{1,0:T(8,128)(2,1)}) %all-gather.2.cloned.1.call-update) | async-done | bytes 18874384 | tf_op jit(solution)/shard_map/all_gather | solution.py:115
  161.4 0.0 copy-done.2
  161.4 99.8 %shard_map.82 = bf16[384,384]{1,0:T(8,128)(2,1)} custom-call(s32[2,64]{1,0:T(2,128)} %select_reduce_fusion.order_ref, s32[2]{0:T(128)} %copy-done.2, bf16[384,384]{1,0:T(8,128)(2,1)} %q_ref.1, bf16[12288,768]{1,0:T(8,128)(2,1)} %all-gather.2.cloned.1.call-done.k_ref.v_ref, bf16[12288,768]{1,0:T(8,128)(2,1)} %all-gather.2.cloned.1.call-done.k_ref.v_ref), custom_call_target="tpu_custom_call" | custom-call | flops 3623878656 | bytes 19464192 | tf_op jit(solution)/shard_map/pallas_call | solution.py:73
  261.2 7.2 %convolution_convert_fusion = bf16[384,6144]{1,0:T(8,128)(2,1)} fusion(bf16[384,384]{1,0:T(8,128)(2,1)} %shard_map.82, bf16[384,6144]{1,0:T(8,128)(2,1)} %param.12), kind=kOutput, calls=%fused_computation | convolution fusion | flops 1814298624 | bytes 9732096 | tf_op jit(solution)/shard_map/dot_general | solution.py:117
  268.4 0.0 copy-start
  268.4 0.0 copy-start.1
  268.4 0.0 reduce-scatter.2.cloned.1.call-update
  268.4 66.4 %reduce-scatter.2.cloned.1.call-done = bf16[48,6144]{1,0:T(8,128)(2,1)} async-done(((bf16[384,6144]{1,0:T(8,128)(2,1)}), bf16[48,6144]{1,0:T(8,128)(2,1)}) %reduce-scatter.2.cloned.1.call-update) | async-done | bytes 589840 | tf_op jit(solution)/shard_map/reduce_scatter | solution.py:119
  334.7 1.3 fusion.3
  336.0 0.0 copy-done
  336.1 0.0 copy-done.1
  336.1 2.1 fusion.2
  (2 shorter events, 0.0 us)
Async XLA Ops:
  6.5 2.0 copy-start.3
  6.5 2.2 copy-start.4
  6.5 154.8 %all-gather.2.cloned.1.call-start = ((), (), s32[]{:S(2)}) async-start(), calls=%async_computation.1 | async-start | bytes 19464192 | tf_op jit(solution)/shard_map/all_gather | solution.py:115
  8.5 326.2 %reduce-scatter.2.cloned.1.call-start = ((), (), s32[]{:S(2)}) async-start(), calls=%async_computation.2 | async-start | bytes 5308416 | tf_op jit(solution)/shard_map/reduce_scatter | solution.py:119
  9.5 151.8 %copy-start.2 = (s32[2]{0:T(128)}, s32[2]{0:T(128)S(1)}, u32[]{:S(2)}) copy-start(s32[2]{0:T(128)S(1)} %get-tuple-element.5.count_ref) | copy-start | bytes 28
  268.4 67.7 %copy-start = (bf16[48,6144]{1,0:T(8,128)(2,1)S(1)}, bf16[48,6144]{1,0:T(8,128)(2,1)}, u32[]{:S(2)}) copy-start(bf16[48,6144]{1,0:T(8,128)(2,1)} %param.11) | copy-start | bytes 1769476
  268.4 67.7 %copy-start.1 = (f32[6144]{0:T(1024)S(1)}, f32[6144]{0:T(1024)}, u32[]{:S(2)}) copy-start(f32[6144]{0:T(1024)} %param.13) | copy-start | bytes 73732
Sparse Core Ops, SparseCore 0:
  10.1 151.1 all-gather.1
  268.5 66.1 reduce-scatter.1

commit v5 on v3

--- a/solution.py
+++ b/solution.py
@@ -106,12 +106,15 @@
     attn = attention(queries, kv_rows, key_bias)
     partial = jnp.dot(attn, out_weight, preferred_element_type=jnp.float32)
 
-    branch = lax.psum_scatter(
-        partial.astype(jnp.bfloat16),
+    tp_count = lax.axis_size("tp")
+    shares = lax.all_to_all(
+        partial.astype(jnp.bfloat16).reshape(tp_count, tok_rows // tp_count, -1),
         "tp",
-        scatter_dimension=0,
-        tiled=True,
-    ).astype(jnp.float32)
+        0,
+        0,
+        tiled=False,
+    )
+    branch = jnp.sum(shares.astype(jnp.float32), axis=0)
     rms = jnp.sqrt(jnp.mean(branch * branch, axis=-1) + 1e-06)
     layer_out = resid.astype(jnp.float32) + gain[None, :] * branch / rms[:, None]
     return layer_out.astype(jnp.bfloat16)

time: 277 us -> 276 us (level)
  blocking collectives: 0 us -> 58.9 us
  waiting for transfers between devices: 207 us -> 151 us
    all_to_all x0 -> x1, blocking collectives: none -> 58.9 us  [local(): lax.all_to_all(partial.astype(jnp.bfloat16).reshape(tp_count, tok_rows //...]
    reduce_scatter x1 -> x0, waiting for transfers between devices: 55.2 us -> none  [local(): lax.psum_scatter(partial.astype(jnp.bfloat16), 'tp', scatter_dimension=0,...]
  transfers between devices with their start and end apart: 2 -> 1, of which waited for: 2 -> 1; matrix products, arithmetic and copies ran while one was open for 1% -> 0% of each run, Pallas kernels for 0% -> 0%
where the time goes in v5:
time: 276 us; the launch traced here: 274 us
  waiting for transfers between devices  151 us (55%)
  blocking collectives  58.9 us (21%)
  Pallas kernels  39.5 us (14%)
  between operations  13.5 us (5%)
  matrix products  5.05 us (2%)
  other arithmetic  4.83 us (2%)
    all_gather x1, waiting for transfers between devices, local(): kv_rows = lax.all_gather(kv_local, 'seq', axis=0, tiled=True)  151 us
    all_to_all x1, blocking collectives, local(): lax.all_to_all(partial.astype(jnp.bfloat16).reshape(tp_count, tok_rows //...  58.9 us
    pallas_call x1, Pallas kernels, attention(): pl.pallas_call(attn_kernel, out_shape=jax.ShapeDtypeStruct((tok_rows, hea...  39.5 us
  transfers between devices with their start and end apart: 1, of which 1 were waited for; matrix products, arithmetic and copies ran while one was open for 0% of the time, Pallas kernels for 0%

profile of v5, /device:TPU:2, one launch (start us, length us, event | category | flops | bytes accessed | tf_op | source)
XLA Modules:
  0.0 274.5 jit_solution(13892688143456197924)
XLA Ops:
  6.5 0.0 copy-start.2
  6.5 0.0 copy-start.3
  6.5 0.0 all-gather.2.cloned.1.call-start
  6.5 1.9 pad_maximum_fusion
  8.5 0.0 all-gather.2.cloned.1.call-update
  8.5 0.0 copy-done.2
  8.5 0.1 broadcast_in_dim.32
  8.6 0.1 reshape.86
  8.7 0.0 copy-done.3
  8.7 0.2 select_reduce_fusion
  8.9 0.1 broadcast_in_dim.35
  9.0 0.1 le.22
  9.1 0.1 dynamic_slice.3
  9.2 0.8 compare_select_fusion.kf_ref
  9.9 151.4 %all-gather.2.cloned.1.call-done.k_ref.v_ref = bf16[12288,768]{1,0:T(8,128)(2,1)} async-done(((bf16[384,768]{1,0:T(8,128)(2,1)}), bf16[12288,768]{1,0:T(8,128)(2,1)}) %all-gather.2.cloned.1.call-update) | async-done | bytes 18874384 | tf_op jit(solution)/shard_map/all_gather | solution.py:105
  161.4 39.5 %shard_map.82 = bf16[384,384]{1,0:T(8,128)(2,1)} custom-call(bf16[384,384]{1,0:T(8,128)(2,1)} %q_ref.1, bf16[12288,768]{1,0:T(8,128)(2,1)} %all-gather.2.cloned.1.call-done.k_ref.v_ref, bf16[12288,768]{1,0:T(8,128)(2,1)} %all-gather.2.cloned.1.call-done.k_ref.v_ref, f32[2,1,12288]{2,1,0:T(1,128)} %compare_select_fusion.kf_ref), custom_call_target="tpu_custom_call" | custom-call | flops 7247757312 | bytes 19464192 | tf_op jit(solution)/shard_map/pallas_call | solution.py:74
  200.8 5.0 %convolution_convert_fusion = bf16[384,6144]{1,0:T(8,128)(2,1)S(1)} fusion(bf16[384,384]{1,0:T(8,128)(2,1)} %shard_map.82, bf16[384,6144]{1,0:T(8,128)(2,1)} %param.12), kind=kOutput, calls=%fused_computation.1 | convolution fusion | flops 1814298624 | bytes 9732096 | tf_op jit(solution)/shard_map/dot_general | solution.py:107
  205.9 58.9 %all_to_all.5 = bf16[8,48,6144]{2,1,0:T(8,128)(2,1)S(1)} all-to-all(bf16[8,48,6144]{2,1,0:T(8,128)(2,1)S(1)} %bitcast.3), channel_id=1, replica_groups=mesh['seq'=32,'tp'=8] {'tp'}, dimensions={0} | all-to-all | bytes 9437184 | tf_op jit(solution)/shard_map/all_to_all | solution.py:110
  264.8 0.7 convert_reduce_fusion
  265.5 0.0 copy-start
  265.5 0.0 copy-start.1
  265.5 0.2 multiply_reduce_fusion
  265.7 0.8 copy-done
  266.6 0.0 copy-done.1
  266.6 1.1 add_convert_fusion
  (2 shorter events, 0.0 us)
Async XLA Ops:
  6.5 2.0 copy-start.2
  6.5 2.2 copy-start.3
  6.5 154.8 %all-gather.2.cloned.1.call-start = ((), (), s32[]{:S(2)}) async-start(), calls=%async_computation.1 | async-start | bytes 19464192 | tf_op jit(solution)/shard_map/all_gather | solution.py:105
  265.5 1.1 copy-start
  265.5 1.1 copy-start.1
Sparse Core Ops, SparseCore 0:
  10.1 151.1 all-gather.1

commit v6 on v4

v6 whole, which is shorter than its diff:
```python
import functools
import math

import jax
import jax.numpy as jnp
from jax import lax
from jax.experimental import pallas as pl
from jax.experimental.pallas import tpu as pltpu
from jax.sharding import PartitionSpec as P

HEAD = 128
SLOTS_PER_CHUNK = 8


def slot_frames(pair_of_device, frame_of_tile, tile_count):
    slot_ids = jnp.arange(tile_count, dtype=jnp.int32)
    paired = jnp.repeat(pair_of_device, 2)
    tile_ids = jnp.where(slot_ids % 2 == 0, paired, tile_count - 1 - paired)
    matches = tile_ids[:, None] == jnp.arange(tile_count, dtype=jnp.int32)[None, :]
    return jnp.sum(jnp.where(matches, frame_of_tile[None, :], 0), axis=1)


def attn_kernel(order_ref, chunks_ref, q_ref, k_ref, v_ref, kb_ref, o_ref, s_sc):
    tile = pl.program_id(1)
    visible = chunks_ref[tile]
    rows = q_ref.shape[0]
    span = k_ref.shape[0] // order_ref.shape[0]
    width = span * SLOTS_PER_CHUNK
    score_scale = 1.0 / math.sqrt(HEAD)
    q = q_ref[...]

    def gather(ref, c):
        pieces = []
        for m in range(SLOTS_PER_CHUNK):
            slot = order_ref[c * SLOTS_PER_CHUNK + m]
            pieces.append(ref[pl.ds(pl.multiple_of(slot * span, span), span), :])
        return jnp.concatenate(pieces, axis=0)

    def first(c, run_max):
        start = pl.multiple_of(c * width, width)
        k = gather(k_ref, c)
        s = lax.dot_general(
            q, k, (((1,), (1,)), ((), ())), preferred_element_type=jnp.float32
        ) * score_scale
        masked = s + kb_ref[:, pl.ds(start, width)]
        s_sc[:, pl.ds(start, width)] = masked
        return jnp.maximum(run_max, jnp.max(masked, axis=1, keepdims=True))

    row_max = lax.fori_loop(0, visible, first, jnp.full((rows, 1), -1e30, jnp.float32))

    def second(c, carry):
        totals, acc = carry
        start = pl.multiple_of(c * width, width)
        probs = jnp.exp(s_sc[:, pl.ds(start, width)] - row_max)
        totals = totals + jnp.sum(probs, axis=1, keepdims=True)
        v = gather(v_ref, c)
        acc = acc + jnp.dot(probs.astype(jnp.bfloat16), v, preferred_element_type=jnp.float32)
        return totals, acc

    totals, acc = lax.fori_loop(
        0,
        visible,
        second,
        (jnp.zeros((rows, 1), jnp.float32), jnp.zeros((rows, HEAD), jnp.float32)),
    )
    o_ref[...] = (acc / totals).astype(o_ref.dtype)


def attention(queries, kv_rows, order, chunks, key_bias):
    tok_rows = queries.shape[0]
    tile_rows = tok_rows // 2
    key_count = kv_rows.shape[0]
    head_count = queries.shape[1] // HEAD
    cost = pl.CostEstimate(
        flops=2 * tok_rows * key_count * HEAD * head_count,
        transcendentals=tok_rows * key_count * head_count // 2,
        bytes_accessed=(key_count * 2 * HEAD * 2 + tok_rows * HEAD * 4) * head_count,
    )
    return pl.pallas_call(
        attn_kernel,
        out_shape=jax.ShapeDtypeStruct((tok_rows, head_count * HEAD), jnp.bfloat16),
        grid_spec=pltpu.PrefetchScalarGridSpec(
            num_scalar_prefetch=2,
            grid=(head_count, 2),
            in_specs=[
                pl.BlockSpec((tile_rows, HEAD), lambda h, i, o, c: (i, h)),
                pl.BlockSpec((key_count, HEAD), lambda h, i, o, c: (0, h)),
                pl.BlockSpec((key_count, HEAD), lambda h, i, o, c: (0, head_count + h)),
                pl.BlockSpec((None, 1, key_count), lambda h, i, o, c: (i, 0, 0)),
            ],
            out_specs=pl.BlockSpec((tile_rows, HEAD), lambda h, i, o, c: (i, h)),
            scratch_shapes=[pltpu.VMEM((tile_rows, key_count), jnp.float32)],
        ),
        compiler_params=pltpu.CompilerParams(vmem_limit_bytes=56 * 1024 * 1024),
        cost_estimate=cost,
    )(order, chunks, queries, kv_rows, kv_rows, key_bias)


def local(queries, keys, values, resid, out_weight, gain, pair_of_device, frame_of_tile):
    tok_rows, row_width = queries.shape
    head_count = row_width // HEAD
    span_rows = tok_rows // 2
    seq_count = lax.axis_size("seq")
    seq_index = lax.axis_index("seq")
    slot_frame = slot_frames(pair_of_device, frame_of_tile, 2 * seq_count)
    own_frames = lax.dynamic_slice_in_dim(slot_frame, 2 * seq_index, 2, 0).astype(jnp.int32)
    slot_count = slot_frame.shape[0]
    slot_ids = jnp.arange(slot_count, dtype=jnp.int32)
    earlier = (slot_frame[None, :] < slot_frame[:, None]) | (
        (slot_frame[None, :] == slot_frame[:, None]) & (slot_ids[None, :] < slot_ids[:, None])
    )
    rank = jnp.sum(earlier.astype(jnp.int32), axis=1)
    order = jnp.sum(
        jnp.where(rank[:, None] == slot_ids[None, :], slot_ids[:, None], 0), axis=0
    ).astype(jnp.int32)
    sorted_frame = jnp.sum(
        jnp.where(rank[:, None] == slot_ids[None, :], slot_frame[:, None], 0), axis=0
    )
    visible = jnp.sum((slot_frame[None, :] <= own_frames[:, None]).astype(jnp.int32), axis=1)
    chunks = ((visible + SLOTS_PER_CHUNK - 1) // SLOTS_PER_CHUNK).astype(jnp.int32)
    key_frame = jnp.repeat(sorted_frame.astype(jnp.int32), span_rows)
    key_bias = jnp.where(
        key_frame[None, :] <= own_frames[:, None], jnp.float32(0.0), jnp.float32(-1e30)
    ).reshape(2, 1, -1)

    kv_local = jnp.concatenate([keys, values], axis=1)
    kv_rows = lax.all_gather(kv_local, "seq", axis=0, tiled=True)
    attn = attention(queries, kv_rows, order, chunks, key_bias)
    partial = jnp.dot(attn, out_weight, preferred_element_type=jnp.float32)

    tp_count = lax.axis_size("tp")
    shares = lax.all_to_all(
        partial.astype(jnp.bfloat16).reshape(tp_count, tok_rows // tp_count, -1),
        "tp",
        0,
        0,
        tiled=False,
    )
    branch = jnp.sum(shares.astype(jnp.float32), axis=0)
    rms = jnp.sqrt(jnp.mean(branch * branch, axis=-1) + 1e-06)
    layer_out = resid.astype(jnp.float32) + gain[None, :] * branch / rms[:, None]
    return layer_out.astype(jnp.bfloat16)


def solution(mesh):
    in_specs = (
        P("seq", "tp"),
        P("seq", "tp"),
        P("seq", "tp"),
        P(("seq", "tp"), None),
        P("tp", None),
        P(),
        P(),
        P(),
    )
    out_specs = P(("seq", "tp"), None)
    return jax.shard_map(local, mesh=mesh, in_specs=in_specs, out_specs=out_specs, check_vma=False)
```

time: 350 us -> 261 us (0.75)
  Pallas kernels: 99.8 us -> 27.2 us
  waiting for transfers between devices: 217 us -> 150 us
  blocking collectives: 0 us -> 56.8 us
    pallas_call x1, Pallas kernels: 99.8 us -> 27.2 us  [attention(): pl.pallas_call(attn_kernel, out_shape=jax.ShapeDtypeStruct((tok_rows, hea...]
    reduce_scatter x1 -> x0, waiting for transfers between devices: 66.4 us -> none  [local(): lax.psum_scatter(partial.astype(jnp.bfloat16), 'tp', scatter_dimension=0,...]
    all_to_all x0 -> x1, blocking collectives: none -> 56.8 us  [local(): lax.all_to_all(partial.astype(jnp.bfloat16).reshape(tp_count, tok_rows //...]
  transfers between devices with their start and end apart: 2 -> 1, of which waited for: 2 -> 1; matrix products, arithmetic and copies ran while one was open for 1% -> 1% of each run, Pallas kernels for 0% -> 0%
where the time goes in v6:
time: 261 us; the launch traced here: 259 us
  waiting for transfers between devices  150 us (57%)
  blocking collectives  56.8 us (22%)
  Pallas kernels  27.2 us (10%)
  between operations  13.5 us (5%)
  other arithmetic  6.38 us (2%)
  matrix products  3.78 us (1%)
    all_gather x1, waiting for transfers between devices, local(): kv_rows = lax.all_gather(kv_local, 'seq', axis=0, tiled=True)  150 us
    all_to_all x1, blocking collectives, local(): lax.all_to_all(partial.astype(jnp.bfloat16).reshape(tp_count, tok_rows //...  56.8 us
    pallas_call x1, Pallas kernels, attention(): pl.pallas_call(attn_kernel, out_shape=jax.ShapeDtypeStruct((tok_rows, hea...  27.2 us
  transfers between devices with their start and end apart: 1, of which 1 were waited for; matrix products, arithmetic and copies ran while one was open for 1% of the time, Pallas kernels for 0%

profile of v6, /device:TPU:2, one launch (start us, length us, event | category | flops | bytes accessed | tf_op | source)
XLA Modules:
  0.0 258.8 jit_solution(17695327259272178275)
XLA Ops:
  6.5 0.0 copy-start.2
  6.5 0.0 copy-start.3
  6.5 0.0 all-gather.2.cloned.1.call-start
  6.5 1.9 pad_maximum_fusion
  8.5 0.0 slice-start
  8.5 0.0 all-gather.2.cloned.1.call-update
  8.5 0.0 copy-done.2
  8.5 0.1 broadcast_in_dim.34
  8.6 0.1 reshape.88
  8.7 0.0 copy-done.3
  8.7 0.2 select_reduce_fusion.2
  8.9 0.1 dynamic_slice.3
  9.0 0.2 convert_reduce_fusion.1
  9.2 0.7 select_reduce_fusion
  9.9 0.1 broadcast_in_dim.37
  9.9 0.1 le.38
  10.0 0.2 fusion.2
  10.2 0.5 and_select_fusion.chunks_ref
  10.7 0.8 compare_select_fusion.kb_ref
  11.5 149.9 %all-gather.2.cloned.1.call-done.k_ref.v_ref = bf16[12288,768]{1,0:T(8,128)(2,1)} async-done(((bf16[384,768]{1,0:T(8,128)(2,1)}), bf16[12288,768]{1,0:T(8,128)(2,1)}) %all-gather.2.cloned.1.call-update) | async-done | bytes 18874384 | tf_op jit(solution)/shard_map/all_gather | solution.py:127
  161.4 27.2 %shard_map.82 = bf16[384,384]{1,0:T(8,128)(2,1)} custom-call(s32[64]{0:T(128)} %get-tuple-element.6.order_ref, s32[2]{0:T(128)} %and_select_fusion.chunks_ref, bf16[384,384]{1,0:T(8,128)(2,1)} %q_ref.1, bf16[12288,768]{1,0:T(8,128)(2,1)} %all-gather.2.cloned.1.call-done.k_ref.v_ref, bf16[12288,768]{1,0:T(8,128)(2,1)} %all-gather.2.cloned.1.call-done.k_ref.v_ref, ...), custom_call_target="tpu_custom_call" | custom-call | flops 3623878656 | bytes 19464192 | tf_op jit(solution)/shard_map/pallas_call | solution.py:79
  188.5 0.0 slice-done
  188.5 0.0 slice-done.1
  188.5 3.8 %convolution_convert_fusion = bf16[384,6144]{1,0:T(8,128)(2,1)S(1)} fusion(bf16[384,384]{1,0:T(8,128)(2,1)} %shard_map.82, bf16[384,6144]{1,0:T(8,128)(2,1)S(1)} %bitcast.5), kind=kOutput, calls=%fused_computation.1 | convolution fusion | flops 1814298624 | bytes 9732096 | tf_op jit(solution)/shard_map/dot_general | solution.py:129
  192.3 56.8 %all_to_all.5 = bf16[8,48,6144]{2,1,0:T(8,128)(2,1)S(1)} all-to-all(bf16[8,48,6144]{2,1,0:T(8,128)(2,1)S(1)} %bitcast.3), channel_id=1, replica_groups=mesh['seq'=32,'tp'=8] {'tp'}, dimensions={0} | all-to-all | bytes 9437184 | tf_op jit(solution)/shard_map/all_to_all | solution.py:132
  249.1 0.7 convert_reduce_fusion
  249.8 0.0 copy-start
  249.8 0.0 copy-start.1
  249.8 0.2 multiply_reduce_fusion
  250.0 0.8 copy-done
  250.9 0.0 copy-done.1
  250.9 1.1 add_convert_fusion
  (4 shorter events, 0.0 us)
Async XLA Ops:
  6.5 2.0 copy-start.2
  6.5 2.2 copy-start.3
  6.5 154.8 %all-gather.2.cloned.1.call-start = ((), (), s32[]{:S(2)}) async-start(), calls=%async_computation.1 | async-start | bytes 19464192 | tf_op jit(solution)/shard_map/all_gather | solution.py:127
  8.5 180.1 %slice-start = ((s8[4718592]{0:T(1024)(128)(4,1)}), s8[524288]{0:T(1024)(128)(4,1)S(1)}, s32[]{:S(2)}) async-start(s8[4718592]{0:T(1024)(128)(4,1)} %bitcast.4), calls=%async_computation.2 | async-start | bytes 1048576
  161.4 27.2 %slice-start.1 = ((s8[4718592]{0:T(1024)(128)(4,1)}), s8[4194304]{0:T(1024)(128)(4,1)S(1)}, s32[]{:S(2)}) async-start(s8[4718592]{0:T(1024)(128)(4,1)} %bitcast.4), calls=%async_computation.3 | async-start | bytes 8388608
  249.8 1.1 copy-start
  249.8 1.1 copy-start.1
Sparse Core Ops, SparseCore 0:
  10.1 151.1 all-gather.1

commit v7 on v6

--- a/solution.py
+++ b/solution.py
@@ -126,17 +126,19 @@
     kv_local = jnp.concatenate([keys, values], axis=1)
     kv_rows = lax.all_gather(kv_local, "seq", axis=0, tiled=True)
     attn = attention(queries, kv_rows, order, chunks, key_bias)
-    partial = jnp.dot(attn, out_weight, preferred_element_type=jnp.float32)
-
     tp_count = lax.axis_size("tp")
+    share_rows = tok_rows // tp_count
+    split = out_weight.shape[1] // 2
+    part_a = jnp.dot(attn, out_weight[:, :split], preferred_element_type=jnp.float32)
+    branch_a = lax.psum_scatter(
+        part_a.astype(jnp.bfloat16), "tp", scatter_dimension=0, tiled=True
+    ).astype(jnp.float32)
+    part_b = jnp.dot(attn, out_weight[:, split:], preferred_element_type=jnp.float32)
     shares = lax.all_to_all(
-        partial.astype(jnp.bfloat16).reshape(tp_count, tok_rows // tp_count, -1),
-        "tp",
-        0,
-        0,
-        tiled=False,
+        part_b.astype(jnp.bfloat16).reshape(tp_count, share_rows, -1), "tp", 0, 0, tiled=False
     )
-    branch = jnp.sum(shares.astype(jnp.float32), axis=0)
+    branch_b = jnp.sum(shares.astype(jnp.float32), axis=0)
+    branch = jnp.concatenate([branch_a, branch_b], axis=1)
     rms = jnp.sqrt(jnp.mean(branch * branch, axis=-1) + 1e-06)
     layer_out = resid.astype(jnp.float32) + gain[None, :] * branch / rms[:, None]
     return layer_out.astype(jnp.bfloat16)

time: 261 us -> 265 us (1.015)
  blocking collectives: 56.8 us -> 51.4 us
  waiting for transfers between devices: 150 us -> 155 us
  matrix products: 3.78 us -> 6.84 us
    reduce_scatter x0 -> x1, waiting for transfers between devices: none -> 6.47 us  [local(): lax.psum_scatter(part_a.astype(jnp.bfloat16), 'tp', scatter_dimension=0,...]
    all_to_all x1, blocking collectives: 56.8 us -> 51.4 us  [local(): lax.all_to_all(part_b.astype(jnp.bfloat16).reshape(tp_count, share_rows,...]
    dot_general x1 -> x2, matrix products: 3.78 us -> 6.84 us  [the longest x1 3.79 us: local(): jnp.dot(attn, out_weight[:, :split], preferred_element_type=jnp.float32)]
  transfers between devices with their start and end apart: 1 -> 2, of which waited for: 1 -> 2; matrix products, arithmetic and copies ran while one was open for 1% -> 3% of each run, Pallas kernels for 0% -> 0%
where the time goes in v7:
time: 265 us; the launch traced here: 264 us
  waiting for transfers between devices  155 us (58%)
  blocking collectives  51.4 us (19%)
  Pallas kernels  27.2 us (10%)
  between operations  13.5 us (5%)
  other arithmetic  7.68 us (3%)
  matrix products  6.84 us (3%)
    all_gather x1, waiting for transfers between devices, local(): kv_rows = lax.all_gather(kv_local, 'seq', axis=0, tiled=True)  149 us
    all_to_all x1, blocking collectives, local(): lax.all_to_all(part_b.astype(jnp.bfloat16).reshape(tp_count, share_rows,...  51.4 us
    pallas_call x1, Pallas kernels, attention(): pl.pallas_call(attn_kernel, out_shape=jax.ShapeDtypeStruct((tok_rows, hea...  27.2 us
    reduce_scatter x1, waiting for transfers between devices, local(): lax.psum_scatter(part_a.astype(jnp.bfloat16), 'tp', scatter_dimension=0,...  6.47 us
  transfers between devices with their start and end apart: 2, of which 2 were waited for; matrix products, arithmetic and copies ran while one was open for 3% of the time, Pallas kernels for 0%

profile of v7, /device:TPU:2, one launch (start us, length us, event | category | flops | bytes accessed | tf_op | source)
XLA Modules:
  0.0 263.8 jit_solution(9652634352092530608)
XLA Ops:
  6.5 0.0 all-gather.2.cloned.1.call-start
  6.5 1.9 pad_maximum_fusion.1
  8.5 0.0 slice-start
  8.5 0.0 all-gather.2.cloned.1.call-update
  8.5 0.0 reduce-scatter.2.cloned.1.call-start
  8.5 0.8 broadcast_in_dim.34
  9.3 0.1 reshape.88
  9.4 0.8 select_reduce_fusion.2
  10.3 0.1 dynamic_slice.3
  10.3 0.2 convert_reduce_fusion.1
  10.5 0.7 select_reduce_fusion
  11.2 0.1 broadcast_in_dim.37
  11.3 0.1 le.38
  11.4 0.2 fusion.4
  11.6 0.5 and_select_fusion.chunks_ref
  12.1 0.8 compare_select_fusion.kb_ref
  12.8 148.6 %all-gather.2.cloned.1.call-done.k_ref.v_ref = bf16[12288,768]{1,0:T(8,128)(2,1)} async-done(((bf16[384,768]{1,0:T(8,128)(2,1)}), bf16[12288,768]{1,0:T(8,128)(2,1)}) %all-gather.2.cloned.1.call-update) | async-done | bytes 18874384 | tf_op jit(solution)/shard_map/all_gather | solution.py:127
  161.4 27.2 %shard_map.82 = bf16[384,384]{1,0:T(8,128)(2,1)} custom-call(s32[64]{0:T(128)} %get-tuple-element.6.order_ref, s32[2]{0:T(128)} %and_select_fusion.chunks_ref, bf16[384,384]{1,0:T(8,128)(2,1)} %q_ref.1, bf16[12288,768]{1,0:T(8,128)(2,1)} %all-gather.2.cloned.1.call-done.k_ref.v_ref, bf16[12288,768]{1,0:T(8,128)(2,1)} %all-gather.2.cloned.1.call-done.k_ref.v_ref, ...), custom_call_target="tpu_custom_call" | custom-call | flops 3623878656 | bytes 19464192 | tf_op jit(solution)/shard_map/pallas_call | solution.py:79
  188.6 0.0 slice-done
  188.6 0.0 slice-done.1
  188.6 3.8 %convolution_convert_fusion.1 = bf16[384,3072]{1,0:T(8,128)(2,1)} fusion(bf16[384,384]{1,0:T(8,128)(2,1)} %shard_map.82, bf16[384,6144]{1,0:T(8,128)(2,1)S(1)} %bitcast.5), kind=kOutput, calls=%fused_computation.2 | convolution fusion | flops 907149312 | bytes 5013504 | tf_op jit(solution)/shard_map/dot_general | solution.py:132
  192.4 0.0 reduce-scatter.2.cloned.1.call-update
  192.4 0.9 copy-done.1
  193.3 3.0 %convolution_convert_fusion = bf16[384,3072]{1,0:T(8,128)(2,1)S(1)} fusion(bf16[384,384]{1,0:T(8,128)(2,1)S(1)} %copy-done.1, bf16[384,6144]{1,0:T(8,128)(2,1)} %param.12), kind=kOutput, calls=%fused_computation.1 | convolution fusion | flops 907149312 | bytes 5013504 | tf_op jit(solution)/shard_map/dot_general | solution.py:136
  196.4 51.4 %all_to_all.5 = bf16[8,48,3072]{2,1,0:T(8,128)(2,1)S(1)} all-to-all(bf16[8,48,3072]{2,1,0:T(8,128)(2,1)S(1)} %bitcast.3), channel_id=1, replica_groups=mesh['seq'=32,'tp'=8] {'tp'}, dimensions={0} | all-to-all | bytes 4718592 | tf_op jit(solution)/shard_map/all_to_all | solution.py:137
  247.8 0.3 convert_reduce_fusion
  248.2 6.5 %reduce-scatter.2.cloned.1.call-done = bf16[48,3072]{1,0:T(8,128)(2,1)} async-done(((bf16[384,3072]{1,0:T(8,128)(2,1)}), bf16[48,3072]{1,0:T(8,128)(2,1)}) %reduce-scatter.2.cloned.1.call-update) | async-done | bytes 294928 | tf_op jit(solution)/shard_map/reduce_scatter | solution.py:133
  254.6 1.0 convert_element_type.28
  255.6 0.2 multiply_reduce_fusion
  255.9 0.0 copy-done
  255.9 0.0 copy-done.2
  255.9 1.1 add_convert_fusion
  (7 shorter events, 0.0 us)
Async XLA Ops:
  6.5 154.9 %all-gather.2.cloned.1.call-start = ((), (), s32[]{:S(2)}) async-start(), calls=%async_computation.2 | async-start | bytes 19464192 | tf_op jit(solution)/shard_map/all_gather | solution.py:127
  8.5 180.1 %slice-start = ((s8[4718592]{0:T(1024)(128)(4,1)}), s8[524288]{0:T(1024)(128)(4,1)S(1)}, s32[]{:S(2)}) async-start(s8[4718592]{0:T(1024)(128)(4,1)} %bitcast.4), calls=%async_computation.4 | async-start | bytes 1048576
  8.5 246.2 %reduce-scatter.2.cloned.1.call-start = ((), (), s32[]{:S(2)}) async-start(), calls=%async_computation.3 | async-start | bytes 2654208 | tf_op jit(solution)/shard_map/reduce_scatter | solution.py:133
  161.4 27.2 %slice-start.1 = ((s8[4718592]{0:T(1024)(128)(4,1)}), s8[4194304]{0:T(1024)(128)(4,1)S(1)}, s32[]{:S(2)}) async-start(s8[4718592]{0:T(1024)(128)(4,1)} %bitcast.4), calls=%async_computation.5 | async-start | bytes 8388608
  192.4 1.0 copy-start.1
  247.8 8.0 %copy-start = (bf16[48,6144]{1,0:T(8,128)(2,1)S(1)}, bf16[48,6144]{1,0:T(8,128)(2,1)}, u32[]{:S(2)}) copy-start(bf16[48,6144]{1,0:T(8,128)(2,1)} %param.11) | copy-start | bytes 1769476
  247.8 8.1 %copy-start.2 = (f32[6144]{0:T(1024)S(1)}, f32[6144]{0:T(1024)}, u32[]{:S(2)}) copy-start(f32[6144]{0:T(1024)} %param.13) | copy-start | bytes 73732
Sparse Core Ops, SparseCore 0:
  10.1 151.2 all-gather.1
  192.5 62.0 reduce-scatter.1

commit v8 on v6

--- a/solution.py
+++ b/solution.py
@@ -21,8 +21,7 @@
 
 
 def attn_kernel(order_ref, chunks_ref, q_ref, k_ref, v_ref, kb_ref, o_ref, s_sc):
-    tile = pl.program_id(1)
-    visible = chunks_ref[tile]
+    visible = chunks_ref[0]
     rows = q_ref.shape[0]
     span = k_ref.shape[0] // order_ref.shape[0]
     width = span * SLOTS_PER_CHUNK
@@ -66,34 +65,34 @@
     o_ref[...] = (acc / totals).astype(o_ref.dtype)
 
 
-def attention(queries, kv_rows, order, chunks, key_bias):
+def attention(queries, kv_rows, order, chunks, key_bias, tile):
     tok_rows = queries.shape[0]
     tile_rows = tok_rows // 2
     key_count = kv_rows.shape[0]
     head_count = queries.shape[1] // HEAD
     cost = pl.CostEstimate(
-        flops=2 * tok_rows * key_count * HEAD * head_count,
-        transcendentals=tok_rows * key_count * head_count // 2,
-        bytes_accessed=(key_count * 2 * HEAD * 2 + tok_rows * HEAD * 4) * head_count,
+        flops=tok_rows * key_count * HEAD * head_count,
+        transcendentals=tile_rows * key_count * head_count // 2,
+        bytes_accessed=(key_count * 2 * HEAD * 2 + tile_rows * HEAD * 4) * head_count,
     )
     return pl.pallas_call(
         attn_kernel,
-        out_shape=jax.ShapeDtypeStruct((tok_rows, head_count * HEAD), jnp.bfloat16),
+        out_shape=jax.ShapeDtypeStruct((tile_rows, head_count * HEAD), jnp.bfloat16),
         grid_spec=pltpu.PrefetchScalarGridSpec(
             num_scalar_prefetch=2,
-            grid=(head_count, 2),
+            grid=(head_count,),
             in_specs=[
-                pl.BlockSpec((tile_rows, HEAD), lambda h, i, o, c: (i, h)),
-                pl.BlockSpec((key_count, HEAD), lambda h, i, o, c: (0, h)),
-                pl.BlockSpec((key_count, HEAD), lambda h, i, o, c: (0, head_count + h)),
-                pl.BlockSpec((None, 1, key_count), lambda h, i, o, c: (i, 0, 0)),
+                pl.BlockSpec((tile_rows, HEAD), lambda h, o, c: (tile, h)),
+                pl.BlockSpec((key_count, HEAD), lambda h, o, c: (0, h)),
+                pl.BlockSpec((key_count, HEAD), lambda h, o, c: (0, head_count + h)),
+                pl.BlockSpec((None, 1, key_count), lambda h, o, c: (tile, 0, 0)),
             ],
-            out_specs=pl.BlockSpec((tile_rows, HEAD), lambda h, i, o, c: (i, h)),
+            out_specs=pl.BlockSpec((tile_rows, HEAD), lambda h, o, c: (0, h)),
             scratch_shapes=[pltpu.VMEM((tile_rows, key_count), jnp.float32)],
         ),
         compiler_params=pltpu.CompilerParams(vmem_limit_bytes=56 * 1024 * 1024),
         cost_estimate=cost,
-    )(order, chunks, queries, kv_rows, kv_rows, key_bias)
+    )(order, chunks[tile:tile + 1], queries, kv_rows, kv_rows, key_bias)
 
 
 def local(queries, keys, values, resid, out_weight, gain, pair_of_device, frame_of_tile):
@@ -125,18 +124,29 @@
 
     kv_local = jnp.concatenate([keys, values], axis=1)
     kv_rows = lax.all_gather(kv_local, "seq", axis=0, tiled=True)
-    attn = attention(queries, kv_rows, order, chunks, key_bias)
-    partial = jnp.dot(attn, out_weight, preferred_element_type=jnp.float32)
-
     tp_count = lax.axis_size("tp")
-    shares = lax.all_to_all(
-        partial.astype(jnp.bfloat16).reshape(tp_count, tok_rows // tp_count, -1),
-        "tp",
-        0,
-        0,
-        tiled=False,
-    )
-    branch = jnp.sum(shares.astype(jnp.float32), axis=0)
+    tp_index = lax.axis_index("tp")
+    share_rows = tok_rows // tp_count
+    owners = tp_count // 2
+    total = jnp.zeros((share_rows, out_weight.shape[1]), jnp.float32)
+    for tile in range(2):
+        attn = attention(queries, kv_rows, order, chunks, key_bias, tile)
+        part = jnp.dot(attn, out_weight, preferred_element_type=jnp.float32).astype(jnp.bfloat16)
+        base = tile * owners
+        mine = lax.dynamic_slice_in_dim(part, (tp_index % owners) * share_rows, share_rows, 0)
+        own = (tp_index // owners) == tile
+        total = total + jnp.where(own, mine.astype(jnp.float32), jnp.float32(0.0))
+        for shift in range(1, tp_count):
+            pairs = [
+                (src, (src + shift) % tp_count)
+                for src in range(tp_count)
+                if base <= (src + shift) % tp_count < base + owners
+            ]
+            dest = (tp_index + shift) % tp_count
+            share = lax.dynamic_slice_in_dim(part, (dest % owners) * share_rows, share_rows, 0)
+            got = lax.ppermute(share, "tp", pairs)
+            total = total + got.astype(jnp.float32)
+    branch = total
     rms = jnp.sqrt(jnp.mean(branch * branch, axis=-1) + 1e-06)
     layer_out = resid.astype(jnp.float32) + gain[None, :] * branch / rms[:, None]
     return layer_out.astype(jnp.bfloat16)

time: 261 us -> 340 us (1.30)
  waiting for transfers between devices: 150 us -> 235 us
  blocking collectives: 56.8 us -> 0 us
  starting transfers between devices: 0.01 us -> 32.9 us
  Pallas kernels: 27.2 us -> 36.8 us
    ppermute x0 -> x14, waiting for transfers between devices: none -> 85.5 us  [local(): got = lax.ppermute(share, 'tp', pairs)]
    all_to_all x1 -> x0, blocking collectives: 56.8 us -> none  [local(): lax.all_to_all(partial.astype(jnp.bfloat16).reshape(tp_count, tok_rows //...]
    ppermute x0 -> x14, starting transfers between devices: none -> 32.9 us  [local(): got = lax.ppermute(share, 'tp', pairs)]
    pallas_call x1 -> x2, Pallas kernels: 27.2 us -> 36.8 us  [attention(): pl.pallas_call(attn_kernel, out_shape=jax.ShapeDtypeStruct((tile_rows, he...]
    reduce_sum x1, other arithmetic: 0.2 us -> 4.8 us  [local(): rms = jnp.sqrt(jnp.mean(branch * branch, axis=-1) + 1e-06)]
  transfers between devices with their start and end apart: 1 -> 15, of which waited for: 1 -> 8; matrix products, arithmetic and copies ran while one was open for 1% -> 1% of each run, Pallas kernels for 0% -> 0%
where the time goes in v8:
time: 340 us; the launch traced here: 337 us
  waiting for transfers between devices  235 us (69%)
  Pallas kernels  36.8 us (11%)
  starting transfers between devices  32.9 us (10%)
  between operations  13.9 us (4%)
  other arithmetic  9.72 us (3%)
  matrix products  4.6 us (1%)
  local copies, waits for them, and re-layouts  4.16 us (1%)
    all_gather x1, waiting for transfers between devices, local(): kv_rows = lax.all_gather(kv_local, 'seq', axis=0, tiled=True)  150 us
    ppermute x14, waiting for transfers between devices, local(): got = lax.ppermute(share, 'tp', pairs)  85.5 us
    pallas_call x2, Pallas kernels, attention(): pl.pallas_call(attn_kernel, out_shape=jax.ShapeDtypeStruct((tile_rows, he...  36.8 us
    ppermute x14, starting transfers between devices, local(): got = lax.ppermute(share, 'tp', pairs)  32.9 us
  transfers between devices with their start and end apart: 15, of which 8 were waited for; matrix products, arithmetic and copies ran while one was open for 1% of the time, Pallas kernels for 0%

profile of v8, /device:TPU:2, one launch (start us, length us, event | category | flops | bytes accessed | tf_op | source)
XLA Modules:
  0.0 337.0 jit_solution(18427821153521218018)
XLA Ops:
  6.5 1.9 pad_maximum_fusion
  11.1 0.8 compare_select_fusion.kb_ref
  11.8 149.5 %all-gather.2.cloned.1.call-done.k_ref.v_ref = bf16[12288,768]{1,0:T(8,128)(2,1)} async-done(((bf16[384,768]{1,0:T(8,128)(2,1)}), bf16[12288,768]{1,0:T(8,128)(2,1)}) %all-gather.2.cloned.1.call-update) | async-done | bytes 18874384 | tf_op jit(solution)/shard_map/all_gather | solution.py:126
  161.4 13.3 %shard_map.82 = bf16[192,384]{1,0:T(8,128)(2,1)} custom-call(s32[64]{0:T(128)} %get-tuple-element.6.order_ref, s32[1]{0:T(128)} %get-tuple-element.23.chunks_ref, bf16[384,384]{1,0:T(8,128)(2,1)} %q_ref.3, bf16[12288,768]{1,0:T(8,128)(2,1)} %all-gather.2.cloned.1.call-done.k_ref.v_ref, bf16[12288,768]{1,0:T(8,128)(2,1)} %all-gather.2.cloned.1.call-done.k_ref.v_ref, ...), custom_call_target="tpu_custom_call" | custom-call | flops 1811939328 | bytes 19169280 | tf_op jit(solution)/shard_map/pallas_call | solution.py:78
  174.7 2.3 convolution_convert_fusion.1
  177.0 23.5 %shard_map.83 = bf16[192,384]{1,0:T(8,128)(2,1)} custom-call(s32[64]{0:T(128)} %get-tuple-element.6.order_ref, s32[1]{0:T(128)} %get-tuple-element.24.chunks_ref, bf16[384,384]{1,0:T(8,128)(2,1)} %q_ref.3, bf16[12288,768]{1,0:T(8,128)(2,1)} %all-gather.2.cloned.1.call-done.k_ref.v_ref, bf16[12288,768]{1,0:T(8,128)(2,1)} %all-gather.2.cloned.1.call-done.k_ref.v_ref, ...), custom_call_target="tpu_custom_call" | custom-call | flops 1811939328 | bytes 19169280 | tf_op jit(solution)/shard_map/pallas_call | solution.py:78
  200.4 2.3 convolution_convert_fusion
  203.2 0.9 copy-done
  204.2 0.7 collective-permute-start.7
  204.9 1.5 collective-permute-start.13
  206.4 8.5 %collective-permute-start.12 = (bf16[48,6144]{1,0:T(8,128)(2,1)S(1)}, bf16[48,6144]{1,0:T(8,128)(2,1)}, u32[]{:S(2)}, u32[]{:S(2)}) collective-permute-start(bf16[48,6144]{1,0:T(8,128)(2,1)S(1)} %get-tuple-element.18), channel_id=1, source_target_pairs={{0,6},{1,7},{6,4},{7,5},{8,14},{9,15},{14,12},{15,13},{16,22},{17,... | collective-permute-start | bytes 1769480 | tf_op jit(solution)/shard_map/ppermute | solution.py:147
  214.8 2.1 collective-permute-start.11
  216.9 2.1 collective-permute-start.10
  219.0 1.6 constant_dynamic-slice_fusion.11
  220.7 4.9 %collective-permute-start.9 = (bf16[48,6144]{1,0:T(8,128)(2,1)S(1)}, bf16[48,6144]{1,0:T(8,128)(2,1)}, u32[]{:S(2)}, u32[]{:S(2)}) collective-permute-start(bf16[48,6144]{1,0:T(8,128)(2,1)S(1)} %get-tuple-element.21), channel_id=1, source_target_pairs={{1,4},{2,5},{3,6},{4,7},{9,12},{10,13},{11,14},{12,15},{17,20},{18... | collective-permute-start | bytes 1769480 | tf_op jit(solution)/shard_map/ppermute | solution.py:147
  225.6 1.5 collective-permute-start.8
  227.1 4.1 %collective-permute-done.12 = bf16[48,6144]{1,0:T(8,128)(2,1)} collective-permute-done((bf16[48,6144]{1,0:T(8,128)(2,1)S(1)}, bf16[48,6144]{1,0:T(8,128)(2,1)}, u32[]{:S(2)}, u32[]{:S(2)}) %collective-permute-start.12) | collective-permute-done | bytes 589856 | tf_op jit(solution)/shard_map/ppermute | solution.py:147
  231.3 2.4 collective-permute-start
  233.6 17.3 %collective-permute-done.11 = bf16[48,6144]{1,0:T(8,128)(2,1)} collective-permute-done((bf16[48,6144]{1,0:T(8,128)(2,1)S(1)}, bf16[48,6144]{1,0:T(8,128)(2,1)}, u32[]{:S(2)}, u32[]{:S(2)}) %collective-permute-start.11) | collective-permute-done | bytes 589856 | tf_op jit(solution)/shard_map/ppermute | solution.py:147
  250.9 1.9 collective-permute-start.6
  252.8 14.3 %collective-permute-done.10 = bf16[48,6144]{1,0:T(8,128)(2,1)} collective-permute-done((bf16[48,6144]{1,0:T(8,128)(2,1)S(1)}, bf16[48,6144]{1,0:T(8,128)(2,1)}, u32[]{:S(2)}, u32[]{:S(2)}) %collective-permute-start.10) | collective-permute-done | bytes 589856 | tf_op jit(solution)/shard_map/ppermute | solution.py:147
  267.2 1.3 collective-permute-start.5
  268.5 1.3 collective-permute-start.4
  269.8 1.3 collective-permute-start.3
  271.1 1.3 collective-permute-start.2
  272.4 4.5 %collective-permute-done.6 = bf16[48,6144]{1,0:T(8,128)(2,1)} collective-permute-done((bf16[48,6144]{1,0:T(8,128)(2,1)S(1)}, bf16[48,6144]{1,0:T(8,128)(2,1)}, u32[]{:S(2)}, u32[]{:S(2)}) %collective-permute-start.6) | collective-permute-done | bytes 589856 | tf_op jit(solution)/shard_map/ppermute | solution.py:147
  276.9 2.1 collective-permute-start.1
  279.1 8.3 %collective-permute-done.5 = bf16[48,6144]{1,0:T(8,128)(2,1)} collective-permute-done((bf16[48,6144]{1,0:T(8,128)(2,1)}, bf16[48,6144]{1,0:T(8,128)(2,1)}, u32[]{:S(2)}, u32[]{:S(2)}) %collective-permute-start.5) | collective-permute-done | bytes 589856 | tf_op jit(solution)/shard_map/ppermute | solution.py:147
  287.4 16.1 %collective-permute-done.4 = bf16[48,6144]{1,0:T(8,128)(2,1)} collective-permute-done((bf16[48,6144]{1,0:T(8,128)(2,1)}, bf16[48,6144]{1,0:T(8,128)(2,1)}, u32[]{:S(2)}, u32[]{:S(2)}) %collective-permute-start.4) | collective-permute-done | bytes 589856 | tf_op jit(solution)/shard_map/ppermute | solution.py:147
  303.6 20.7 %collective-permute-done.3 = bf16[48,6144]{1,0:T(8,128)(2,1)} collective-permute-done((bf16[48,6144]{1,0:T(8,128)(2,1)}, bf16[48,6144]{1,0:T(8,128)(2,1)}, u32[]{:S(2)}, u32[]{:S(2)}) %collective-permute-start.3) | collective-permute-done | bytes 589856 | tf_op jit(solution)/shard_map/ppermute | solution.py:147
  324.3 4.8 %multiply_reduce_fusion = (f32[48]{0:T(128)S(1)}, f32[48,6144]{1,0:T(8,128)S(1)}) fusion(bf16[48,6144]{1,0:T(8,128)(2,1)} %collective-permute-done.13, bf16[48,6144]{1,0:T(8,128)(2,1)} %collective-permute-done.12, bf16[48,6144]{1,0:T(8,128)(2,1)} %collective-permute-done.11, bf16[48,6144]{1,0:T(8,128)(2,1)} %collective-permute-done.10, ...), kind=kLoop, calls=%fused_computation.3 | loop fusion | flops 10321872 | bytes 10617030 | tf_op jit(solution)/shard_map/reduce_sum | solution.py:150
  329.2 1.0 add_convert_fusion
  (37 shorter events, 2.8 us)
Async XLA Ops:
  6.5 2.2 copy-start.3
  6.5 2.4 copy-start.4
  6.5 154.8 %all-gather.2.cloned.1.call-start = ((), (), s32[]{:S(2)}) async-start(), calls=%async_computation | async-start | bytes 19464192 | tf_op jit(solution)/shard_map/all_gather | solution.py:126
  8.7 166.0 %slice-start = ((s8[4718592]{0:T(1024)(128)(4,1)}), s8[524288]{0:T(1024)(128)(4,1)S(1)}, s32[]{:S(2)}) async-start(s8[4718592]{0:T(1024)(128)(4,1)} %bitcast.4), calls=%async_computation.1 | async-start | bytes 1048576
  161.4 13.3 %slice-start.1 = ((s8[4718592]{0:T(1024)(128)(4,1)}), s8[4194304]{0:T(1024)(128)(4,1)S(1)}, s32[]{:S(2)}) async-start(s8[4718592]{0:T(1024)(128)(4,1)} %bitcast.4), calls=%async_computation.2 | async-start | bytes 8388608
  202.8 1.4 copy-start
  204.2 16.5 %collective-permute-start.7 = (bf16[48,6144]{1,0:T(8,128)(2,1)S(1)}, bf16[48,6144]{1,0:T(8,128)(2,1)S(1)}, u32[]{:S(2)}, u32[]{:S(2)}) collective-permute-start(bf16[48,6144]{1,0:T(8,128)(2,1)S(1)} %get-tuple-element.16), channel_id=1, source_target_pairs={{3,4},{4,5},{5,6},{6,7},{11,12},{12,13},{13,14},{14,15},{19,20},{2... | collective-permute-start | bytes 1769480 | tf_op jit(solution)/shard_map/ppermute | solution.py:147
  204.9 20.8 %collective-permute-start.13 = (bf16[48,6144]{1,0:T(8,128)(2,1)S(1)}, bf16[48,6144]{1,0:T(8,128)(2,1)}, u32[]{:S(2)}, u32[]{:S(2)}) collective-permute-start(bf16[48,6144]{1,0:T(8,128)(2,1)S(1)} %get-tuple-element.17), channel_id=1, source_target_pairs={{0,7},{5,4},{6,5},{7,6},{8,15},{13,12},{14,13},{15,14},{16,23},{21... | collective-permute-start | bytes 1769480 | tf_op jit(solution)/shard_map/ppermute | solution.py:147
  206.4 24.9 %collective-permute-start.12 = (bf16[48,6144]{1,0:T(8,128)(2,1)S(1)}, bf16[48,6144]{1,0:T(8,128)(2,1)}, u32[]{:S(2)}, u32[]{:S(2)}) collective-permute-start(bf16[48,6144]{1,0:T(8,128)(2,1)S(1)} %get-tuple-element.18), channel_id=1, source_target_pairs={{0,6},{1,7},{6,4},{7,5},{8,14},{9,15},{14,12},{15,13},{16,22},{17,... | collective-permute-start | bytes 1769480 | tf_op jit(solution)/shard_map/ppermute | solution.py:147
  214.8 36.1 %collective-permute-start.11 = (bf16[48,6144]{1,0:T(8,128)(2,1)S(1)}, bf16[48,6144]{1,0:T(8,128)(2,1)}, u32[]{:S(2)}, u32[]{:S(2)}) collective-permute-start(bf16[48,6144]{1,0:T(8,128)(2,1)S(1)} %get-tuple-element.19), channel_id=1, source_target_pairs={{0,5},{1,6},{2,7},{7,4},{8,13},{9,14},{10,15},{15,12},{16,21},{17,... | collective-permute-start | bytes 1769480 | tf_op jit(solution)/shard_map/ppermute | solution.py:147
  216.9 50.2 %collective-permute-start.10 = (bf16[48,6144]{1,0:T(8,128)(2,1)S(1)}, bf16[48,6144]{1,0:T(8,128)(2,1)}, u32[]{:S(2)}, u32[]{:S(2)}) collective-permute-start(bf16[48,6144]{1,0:T(8,128)(2,1)S(1)} %get-tuple-element.20), channel_id=1, source_target_pairs={{0,4},{1,5},{2,6},{3,7},{8,12},{9,13},{10,14},{11,15},{16,20},{17,... | collective-permute-start | bytes 1769480 | tf_op jit(solution)/shard_map/ppermute | solution.py:147
  220.7 47.8 %collective-permute-start.9 = (bf16[48,6144]{1,0:T(8,128)(2,1)S(1)}, bf16[48,6144]{1,0:T(8,128)(2,1)}, u32[]{:S(2)}, u32[]{:S(2)}) collective-permute-start(bf16[48,6144]{1,0:T(8,128)(2,1)S(1)} %get-tuple-element.21), channel_id=1, source_target_pairs={{1,4},{2,5},{3,6},{4,7},{9,12},{10,13},{11,14},{12,15},{17,20},{18... | collective-permute-start | bytes 1769480 | tf_op jit(solution)/shard_map/ppermute | solution.py:147
  225.6 44.1 %collective-permute-start.8 = (bf16[48,6144]{1,0:T(8,128)(2,1)S(1)}, bf16[48,6144]{1,0:T(8,128)(2,1)}, u32[]{:S(2)}, u32[]{:S(2)}) collective-permute-start(bf16[48,6144]{1,0:T(8,128)(2,1)S(1)} %get-tuple-element.22), channel_id=1, source_target_pairs={{2,4},{3,5},{4,6},{5,7},{10,12},{11,13},{12,14},{13,15},{18,20},{1... | collective-permute-start | bytes 1769480 | tf_op jit(solution)/shard_map/ppermute | solution.py:147
  231.3 39.8 %collective-permute-start = (bf16[48,6144]{1,0:T(8,128)(2,1)S(1)}, bf16[48,6144]{1,0:T(8,128)(2,1)}, u32[]{:S(2)}, u32[]{:S(2)}) collective-permute-start(bf16[48,6144]{1,0:T(8,128)(2,1)S(1)} %get-tuple-element.9), channel_id=1, source_target_pairs={{0,1},{1,2},{2,3},{7,0},{8,9},{9,10},{10,11},{15,8},{16,17},{17,18... | collective-permute-start | bytes 1769480 | tf_op jit(solution)/shard_map/ppermute | solution.py:147
  250.9 26.0 %collective-permute-start.6 = (bf16[48,6144]{1,0:T(8,128)(2,1)S(1)}, bf16[48,6144]{1,0:T(8,128)(2,1)}, u32[]{:S(2)}, u32[]{:S(2)}) collective-permute-start(bf16[48,6144]{1,0:T(8,128)(2,1)S(1)} %get-tuple-element.10), channel_id=1, source_target_pairs={{1,0},{2,1},{3,2},{4,3},{9,8},{10,9},{11,10},{12,11},{17,16},{18,1... | collective-permute-start | bytes 1769480 | tf_op jit(solution)/shard_map/ppermute | solution.py:147
  267.2 20.3 %collective-permute-start.5 = (bf16[48,6144]{1,0:T(8,128)(2,1)}, bf16[48,6144]{1,0:T(8,128)(2,1)}, u32[]{:S(2)}, u32[]{:S(2)}) collective-permute-start(bf16[48,6144]{1,0:T(8,128)(2,1)} %get-tuple-element.11), channel_id=1, source_target_pairs={{2,0},{3,1},{4,2},{5,3},{10,8},{11,9},{12,10},{13,11},{18,16},{19,... | collective-permute-start | bytes 1769480 | tf_op jit(solution)/shard_map/ppermute | solution.py:147
  268.5 35.1 %collective-permute-start.4 = (bf16[48,6144]{1,0:T(8,128)(2,1)}, bf16[48,6144]{1,0:T(8,128)(2,1)}, u32[]{:S(2)}, u32[]{:S(2)}) collective-permute-start(bf16[48,6144]{1,0:T(8,128)(2,1)} %get-tuple-element.12), channel_id=1, source_target_pairs={{3,0},{4,1},{5,2},{6,3},{11,8},{12,9},{13,10},{14,11},{19,16},{20,... | collective-permute-start | bytes 1769480 | tf_op jit(solution)/shard_map/ppermute | solution.py:147
  269.8 54.5 %collective-permute-start.3 = (bf16[48,6144]{1,0:T(8,128)(2,1)}, bf16[48,6144]{1,0:T(8,128)(2,1)}, u32[]{:S(2)}, u32[]{:S(2)}) collective-permute-start(bf16[48,6144]{1,0:T(8,128)(2,1)} %get-tuple-element.13), channel_id=1, source_target_pairs={{4,0},{5,1},{6,2},{7,3},{12,8},{13,9},{14,10},{15,11},{20,16},{21,... | collective-permute-start | bytes 1769480 | tf_op jit(solution)/shard_map/ppermute | solution.py:147
  271.1 53.2 %collective-permute-start.2 = (bf16[48,6144]{1,0:T(8,128)(2,1)}, bf16[48,6144]{1,0:T(8,128)(2,1)}, u32[]{:S(2)}, u32[]{:S(2)}) collective-permute-start(bf16[48,6144]{1,0:T(8,128)(2,1)} %get-tuple-element.14), channel_id=1, source_target_pairs={{0,3},{5,0},{6,1},{7,2},{8,11},{13,8},{14,9},{15,10},{16,19},{21,1... | collective-permute-start | bytes 1769480 | tf_op jit(solution)/shard_map/ppermute | solution.py:147
  276.9 47.4 %collective-permute-start.1 = (bf16[48,6144]{1,0:T(8,128)(2,1)}, bf16[48,6144]{1,0:T(8,128)(2,1)}, u32[]{:S(2)}, u32[]{:S(2)}) collective-permute-start(bf16[48,6144]{1,0:T(8,128)(2,1)} %get-tuple-element.15), channel_id=1, source_target_pairs={{0,2},{1,3},{6,0},{7,1},{8,10},{9,11},{14,8},{15,9},{16,18},{17,19... | collective-permute-start | bytes 1769480 | tf_op jit(solution)/shard_map/ppermute | solution.py:147
  279.1 50.0 %copy-start.1 = (bf16[48,6144]{1,0:T(8,128)(2,1)S(1)}, bf16[48,6144]{1,0:T(8,128)(2,1)}, u32[]{:S(2)}) copy-start(bf16[48,6144]{1,0:T(8,128)(2,1)} %param.11) | copy-start | bytes 1769476
  279.1 50.0 %copy-start.2 = (f32[6144]{0:T(1024)S(1)}, f32[6144]{0:T(1024)}, u32[]{:S(2)}) copy-start(f32[6144]{0:T(1024)} %param.13) | copy-start | bytes 73732
Sparse Core Ops, SparseCore 0:
  10.1 151.1 all-gather.1

commit v9 on v6

--- a/solution.py
+++ b/solution.py
@@ -9,7 +9,7 @@
 from jax.sharding import PartitionSpec as P
 
 HEAD = 128
-SLOTS_PER_CHUNK = 8
+SLOTS_PER_CHUNK = 4
 
 
 def slot_frames(pair_of_device, frame_of_tile, tile_count):

time: 261 us -> 271 us (1.038)
  Pallas kernels: 27.2 us -> 40.4 us
    pallas_call x1, Pallas kernels: 27.2 us -> 40.4 us  [attention(): pl.pallas_call(attn_kernel, out_shape=jax.ShapeDtypeStruct((tok_rows, hea...]
where the time goes in v9:
time: 271 us
  waiting for transfers between devices  150 us (55%)
  blocking collectives  55.5 us (20%)
  Pallas kernels  40.4 us (15%)
  between operations  13.5 us (5%)
  other arithmetic  6.38 us (2%)
  matrix products  3.78 us (1%)
    all_gather x1, waiting for transfers between devices, local(): kv_rows = lax.all_gather(kv_local, 'seq', axis=0, tiled=True)  150 us
    all_to_all x1, blocking collectives, local(): lax.all_to_all(partial.astype(jnp.bfloat16).reshape(tp_count, tok_rows //...  55.5 us
    pallas_call x1, Pallas kernels, attention(): pl.pallas_call(attn_kernel, out_shape=jax.ShapeDtypeStruct((tok_rows, hea...  40.4 us
  transfers between devices with their start and end apart: 1, of which 1 were waited for; matrix products, arithmetic and copies ran while one was open for 1% of the time, Pallas kernels for 0%

profile of v9, /device:TPU:2, one launch (start us, length us, event | category | flops | bytes accessed | tf_op | source)
XLA Modules:
  0.0 270.7 jit_solution(2933684755088689277)
XLA Ops:
  6.5 0.0 copy-start.2
  6.5 0.0 all-gather.2.cloned.1.call-start
  6.5 1.9 pad_maximum_fusion
  8.5 0.0 slice-start
  8.5 0.0 all-gather.2.cloned.1.call-update
  8.5 0.0 copy-done.2
  8.5 0.1 broadcast_in_dim.34
  8.6 0.1 reshape.88
  8.7 0.0 copy-done.3
  8.7 0.2 select_reduce_fusion.2
  8.9 0.1 dynamic_slice.3
  9.0 0.2 convert_reduce_fusion.1
  9.2 0.7 select_reduce_fusion
  9.9 0.1 broadcast_in_dim.37
  9.9 0.1 le.38
  10.0 0.2 fusion.2
  10.2 0.5 and_select_fusion.chunks_ref
  10.7 0.8 compare_select_fusion.kb_ref
  11.5 149.9 %all-gather.2.cloned.1.call-done.k_ref.v_ref = bf16[12288,768]{1,0:T(8,128)(2,1)} async-done(((bf16[384,768]{1,0:T(8,128)(2,1)}), bf16[12288,768]{1,0:T(8,128)(2,1)}) %all-gather.2.cloned.1.call-update) | async-done | bytes 18874384 | tf_op jit(solution)/shard_map/all_gather | solution.py:127
  161.4 0.0 slice-start.1
  161.4 40.4 %shard_map.82 = bf16[384,384]{1,0:T(8,128)(2,1)} custom-call(s32[64]{0:T(128)} %get-tuple-element.6.order_ref, s32[2]{0:T(128)} %and_select_fusion.chunks_ref, bf16[384,384]{1,0:T(8,128)(2,1)} %q_ref.1, bf16[12288,768]{1,0:T(8,128)(2,1)} %all-gather.2.cloned.1.call-done.k_ref.v_ref, bf16[12288,768]{1,0:T(8,128)(2,1)} %all-gather.2.cloned.1.call-done.k_ref.v_ref, ...), custom_call_target="tpu_custom_call" | custom-call | flops 3623878656 | bytes 19464192 | tf_op jit(solution)/shard_map/pallas_call | solution.py:79
  201.7 0.0 slice-done
  201.7 0.0 slice-done.1
  201.7 3.8 %convolution_convert_fusion = bf16[384,6144]{1,0:T(8,128)(2,1)S(1)} fusion(bf16[384,384]{1,0:T(8,128)(2,1)} %shard_map.82, bf16[384,6144]{1,0:T(8,128)(2,1)S(1)} %bitcast.5), kind=kOutput, calls=%fused_computation.1 | convolution fusion | flops 1814298624 | bytes 9732096 | tf_op jit(solution)/shard_map/dot_general | solution.py:129
  205.5 55.5 %all_to_all.5 = bf16[8,48,6144]{2,1,0:T(8,128)(2,1)S(1)} all-to-all(bf16[8,48,6144]{2,1,0:T(8,128)(2,1)S(1)} %bitcast.3), channel_id=1, replica_groups=mesh['seq'=32,'tp'=8] {'tp'}, dimensions={0} | all-to-all | bytes 9437184 | tf_op jit(solution)/shard_map/all_to_all | solution.py:132
  261.0 0.7 convert_reduce_fusion
  261.7 0.0 copy-start
  261.7 0.0 copy-start.1
  261.7 0.2 multiply_reduce_fusion
  261.9 0.8 copy-done
  262.8 0.0 copy-done.1
  262.8 1.1 add_convert_fusion
  (4 shorter events, 0.0 us)
Async XLA Ops:
  6.5 2.0 copy-start.2
  6.5 2.2 copy-start.3
  6.5 154.8 %all-gather.2.cloned.1.call-start = ((), (), s32[]{:S(2)}) async-start(), calls=%async_computation.1 | async-start | bytes 19464192 | tf_op jit(solution)/shard_map/all_gather | solution.py:127
  8.5 193.3 %slice-start = ((s8[4718592]{0:T(1024)(128)(4,1)}), s8[524288]{0:T(1024)(128)(4,1)S(1)}, s32[]{:S(2)}) async-start(s8[4718592]{0:T(1024)(128)(4,1)} %bitcast.4), calls=%async_computation.2 | async-start | bytes 1048576
  161.4 40.4 %slice-start.1 = ((s8[4718592]{0:T(1024)(128)(4,1)}), s8[4194304]{0:T(1024)(128)(4,1)S(1)}, s32[]{:S(2)}) async-start(s8[4718592]{0:T(1024)(128)(4,1)} %bitcast.4), calls=%async_computation.3 | async-start | bytes 8388608
  261.7 1.1 copy-start
  261.7 1.1 copy-start.1
Sparse Core Ops, SparseCore 0:
  10.1 151.1 all-gather.1

commit v10 on v9

--- a/solution.py
+++ b/solution.py
@@ -9,7 +9,7 @@
 from jax.sharding import PartitionSpec as P
 
 HEAD = 128
-SLOTS_PER_CHUNK = 4
+SLOTS_PER_CHUNK = 16
 
 
 def slot_frames(pair_of_device, frame_of_tile, tile_count):

time: 271 us -> 257 us (0.948)
  Pallas kernels: 40.4 us -> 21.6 us
  blocking collectives: 55.5 us -> 58.9 us
    pallas_call x1, Pallas kernels: 40.4 us -> 21.6 us  [attention(): pl.pallas_call(attn_kernel, out_shape=jax.ShapeDtypeStruct((tok_rows, hea...]
    all_to_all x1, blocking collectives: 55.5 us -> 58.9 us  [local(): lax.all_to_all(partial.astype(jnp.bfloat16).reshape(tp_count, tok_rows //...]
where the time goes in v10:
time: 257 us; the launch traced here: 255 us
  waiting for transfers between devices  150 us (58%)
  blocking collectives  58.9 us (23%)
  Pallas kernels  21.6 us (8%)
  between operations  13.5 us (5%)
  other arithmetic  6.38 us (2%)
  matrix products  3.78 us (1%)
    all_gather x1, waiting for transfers between devices, local(): kv_rows = lax.all_gather(kv_local, 'seq', axis=0, tiled=True)  150 us
    all_to_all x1, blocking collectives, local(): lax.all_to_all(partial.astype(jnp.bfloat16).reshape(tp_count, tok_rows //...  58.9 us
    pallas_call x1, Pallas kernels, attention(): pl.pallas_call(attn_kernel, out_shape=jax.ShapeDtypeStruct((tok_rows, hea...  21.6 us
  transfers between devices with their start and end apart: 1, of which 1 were waited for; matrix products, arithmetic and copies ran while one was open for 1% of the time, Pallas kernels for 0%

profile of v10, /device:TPU:2, one launch (start us, length us, event | category | flops | bytes accessed | tf_op | source)
XLA Modules:
  0.0 255.3 jit_solution(13263000032031367039)
XLA Ops:
  6.5 0.0 copy-start.2
  6.5 0.0 copy-start.3
  6.5 0.0 all-gather.2.cloned.1.call-start
  6.5 1.9 pad_maximum_fusion
  8.5 0.0 slice-start
  8.5 0.0 all-gather.2.cloned.1.call-update
  8.5 0.0 copy-done.2
  8.5 0.1 broadcast_in_dim.34
  8.6 0.1 reshape.88
  8.7 0.0 copy-done.3
  8.7 0.2 select_reduce_fusion.2
  8.9 0.1 dynamic_slice.3
  9.0 0.2 convert_reduce_fusion.1
  9.2 0.7 select_reduce_fusion
  9.9 0.1 broadcast_in_dim.37
  9.9 0.1 le.38
  10.0 0.2 fusion.2
  10.2 0.5 and_select_fusion.chunks_ref
  10.7 0.8 compare_select_fusion.kb_ref
  11.5 149.9 %all-gather.2.cloned.1.call-done.k_ref.v_ref = bf16[12288,768]{1,0:T(8,128)(2,1)} async-done(((bf16[384,768]{1,0:T(8,128)(2,1)}), bf16[12288,768]{1,0:T(8,128)(2,1)}) %all-gather.2.cloned.1.call-update) | async-done | bytes 18874384 | tf_op jit(solution)/shard_map/all_gather | solution.py:127
  161.4 21.6 %shard_map.82 = bf16[384,384]{1,0:T(8,128)(2,1)} custom-call(s32[64]{0:T(128)} %get-tuple-element.6.order_ref, s32[2]{0:T(128)} %and_select_fusion.chunks_ref, bf16[384,384]{1,0:T(8,128)(2,1)} %q_ref.1, bf16[12288,768]{1,0:T(8,128)(2,1)} %all-gather.2.cloned.1.call-done.k_ref.v_ref, bf16[12288,768]{1,0:T(8,128)(2,1)} %all-gather.2.cloned.1.call-done.k_ref.v_ref, ...), custom_call_target="tpu_custom_call" | custom-call | flops 3623878656 | bytes 19464192 | tf_op jit(solution)/shard_map/pallas_call | solution.py:79
  182.9 0.0 slice-done
  182.9 0.0 slice-done.1
  183.0 3.8 %convolution_convert_fusion = bf16[384,6144]{1,0:T(8,128)(2,1)S(1)} fusion(bf16[384,384]{1,0:T(8,128)(2,1)} %shard_map.82, bf16[384,6144]{1,0:T(8,128)(2,1)S(1)} %bitcast.5), kind=kOutput, calls=%fused_computation.1 | convolution fusion | flops 1814298624 | bytes 9732096 | tf_op jit(solution)/shard_map/dot_general | solution.py:129
  186.7 58.9 %all_to_all.5 = bf16[8,48,6144]{2,1,0:T(8,128)(2,1)S(1)} all-to-all(bf16[8,48,6144]{2,1,0:T(8,128)(2,1)S(1)} %bitcast.3), channel_id=1, replica_groups=mesh['seq'=32,'tp'=8] {'tp'}, dimensions={0} | all-to-all | bytes 9437184 | tf_op jit(solution)/shard_map/all_to_all | solution.py:132
  245.7 0.7 convert_reduce_fusion
  246.3 0.0 copy-start
  246.4 0.0 copy-start.1
  246.4 0.2 multiply_reduce_fusion
  246.6 0.8 copy-done
  247.4 0.0 copy-done.1
  247.4 1.1 add_convert_fusion
  (4 shorter events, 0.0 us)
Async XLA Ops:
  6.5 2.0 copy-start.2
  6.5 2.2 copy-start.3
  6.5 154.8 %all-gather.2.cloned.1.call-start = ((), (), s32[]{:S(2)}) async-start(), calls=%async_computation.1 | async-start | bytes 19464192 | tf_op jit(solution)/shard_map/all_gather | solution.py:127
  8.5 174.5 %slice-start = ((s8[4718592]{0:T(1024)(128)(4,1)}), s8[524288]{0:T(1024)(128)(4,1)S(1)}, s32[]{:S(2)}) async-start(s8[4718592]{0:T(1024)(128)(4,1)} %bitcast.4), calls=%async_computation.2 | async-start | bytes 1048576
  161.4 21.6 %slice-start.1 = ((s8[4718592]{0:T(1024)(128)(4,1)}), s8[4194304]{0:T(1024)(128)(4,1)S(1)}, s32[]{:S(2)}) async-start(s8[4718592]{0:T(1024)(128)(4,1)} %bitcast.4), calls=%async_computation.3 | async-start | bytes 8388608
  246.3 1.1 copy-start
  246.4 1.1 copy-start.1
Sparse Core Ops, SparseCore 0:
  10.1 151.1 all-gather.1

commit v11 on v10

--- a/solution.py
+++ b/solution.py
@@ -20,7 +20,7 @@
     return jnp.sum(jnp.where(matches, frame_of_tile[None, :], 0), axis=1)
 
 
-def attn_kernel(order_ref, chunks_ref, q_ref, k_ref, v_ref, kb_ref, o_ref, s_sc):
+def attn_kernel(order_ref, chunks_ref, q_ref, k_ref, v_ref, kb_ref, o_ref):
     tile = pl.program_id(1)
     visible = chunks_ref[tile]
     rows = q_ref.shape[0]
@@ -36,32 +36,33 @@
             pieces.append(ref[pl.ds(pl.multiple_of(slot * span, span), span), :])
         return jnp.concatenate(pieces, axis=0)
 
-    def first(c, run_max):
+    def step(c, carry):
+        run_max, totals, acc = carry
         start = pl.multiple_of(c * width, width)
         k = gather(k_ref, c)
         s = lax.dot_general(
             q, k, (((1,), (1,)), ((), ())), preferred_element_type=jnp.float32
         ) * score_scale
         masked = s + kb_ref[:, pl.ds(start, width)]
-        s_sc[:, pl.ds(start, width)] = masked
-        return jnp.maximum(run_max, jnp.max(masked, axis=1, keepdims=True))
+        new_max = jnp.maximum(run_max, jnp.max(masked, axis=1, keepdims=True))
+        rescale = jnp.exp(run_max - new_max)
+        probs = jnp.exp(masked - new_max)
+        totals = totals * rescale + jnp.sum(probs, axis=1, keepdims=True)
+        v = gather(v_ref, c)
+        acc = acc * rescale + jnp.dot(
+            probs.astype(jnp.bfloat16), v, preferred_element_type=jnp.float32
+        )
+        return new_max, totals, acc
 
-    row_max = lax.fori_loop(0, visible, first, jnp.full((rows, 1), -1e30, jnp.float32))
-
-    def second(c, carry):
-        totals, acc = carry
-        start = pl.multiple_of(c * width, width)
-        probs = jnp.exp(s_sc[:, pl.ds(start, width)] - row_max)
-        totals = totals + jnp.sum(probs, axis=1, keepdims=True)
-        v = gather(v_ref, c)
-        acc = acc + jnp.dot(probs.astype(jnp.bfloat16), v, preferred_element_type=jnp.float32)
-        return totals, acc
-
-    totals, acc = lax.fori_loop(
+    row_max, totals, acc = lax.fori_loop(
         0,
         visible,
-        second,
-        (jnp.zeros((rows, 1), jnp.float32), jnp.zeros((rows, HEAD), jnp.float32)),
+        step,
+        (
+            jnp.full((rows, 1), -1e30, jnp.float32),
+            jnp.zeros((rows, 1), jnp.float32),
+            jnp.zeros((rows, HEAD), jnp.float32),
+        ),
     )
     o_ref[...] = (acc / totals).astype(o_ref.dtype)
 
@@ -89,7 +90,6 @@
                 pl.BlockSpec((None, 1, key_count), lambda h, i, o, c: (i, 0, 0)),
             ],
             out_specs=pl.BlockSpec((tile_rows, HEAD), lambda h, i, o, c: (i, h)),
-            scratch_shapes=[pltpu.VMEM((tile_rows, key_count), jnp.float32)],
         ),
         compiler_params=pltpu.CompilerParams(vmem_limit_bytes=56 * 1024 * 1024),
         cost_estimate=cost,

time: 257 us -> 261 us (1.016)
  Pallas kernels: 21.6 us -> 27.9 us
  blocking collectives: 58.9 us -> 55.1 us
    pallas_call x1, Pallas kernels: 21.6 us -> 27.9 us  [attention(): pl.pallas_call(attn_kernel, out_shape=jax.ShapeDtypeStruct((tok_rows, hea...]
    all_to_all x1, blocking collectives: 58.9 us -> 55.1 us  [local(): lax.all_to_all(partial.astype(jnp.bfloat16).reshape(tp_count, tok_rows //...]
where the time goes in v11:
time: 261 us; the launch traced here: 258 us
  waiting for transfers between devices  150 us (57%)
  blocking collectives  55.1 us (21%)
  Pallas kernels  27.9 us (11%)
  between operations  13.5 us (5%)
  other arithmetic  6.38 us (2%)
  matrix products  3.78 us (1%)
    all_gather x1, waiting for transfers between devices, local(): kv_rows = lax.all_gather(kv_local, 'seq', axis=0, tiled=True)  150 us
    all_to_all x1, blocking collectives, local(): lax.all_to_all(partial.astype(jnp.bfloat16).reshape(tp_count, tok_rows //...  55.1 us
    pallas_call x1, Pallas kernels, attention(): pl.pallas_call(attn_kernel, out_shape=jax.ShapeDtypeStruct((tok_rows, hea...  27.9 us
  transfers between devices with their start and end apart: 1, of which 1 were waited for; matrix products, arithmetic and copies ran while one was open for 1% of the time, Pallas kernels for 0%

profile of v11, /device:TPU:2, one launch (start us, length us, event | category | flops | bytes accessed | tf_op | source)
XLA Modules:
  0.0 257.9 jit_solution(14530505538259835772)
XLA Ops:
  6.5 0.0 copy-start.3
  6.5 0.0 all-gather.2.cloned.1.call-start
  6.5 1.9 pad_maximum_fusion
  8.5 0.0 slice-start
  8.5 0.0 all-gather.2.cloned.1.call-update
  8.5 0.0 copy-done.2
  8.5 0.1 broadcast_in_dim.34
  8.6 0.1 reshape.88
  8.7 0.0 copy-done.3
  8.7 0.2 select_reduce_fusion.2
  8.9 0.1 dynamic_slice.3
  9.0 0.2 convert_reduce_fusion.1
  9.2 0.7 select_reduce_fusion
  9.9 0.1 broadcast_in_dim.37
  9.9 0.1 le.38
  10.0 0.2 fusion.2
  10.2 0.5 and_select_fusion.chunks_ref
  10.7 0.8 compare_select_fusion.kb_ref
  11.5 149.9 %all-gather.2.cloned.1.call-done.k_ref.v_ref = bf16[12288,768]{1,0:T(8,128)(2,1)} async-done(((bf16[384,768]{1,0:T(8,128)(2,1)}), bf16[12288,768]{1,0:T(8,128)(2,1)}) %all-gather.2.cloned.1.call-update) | async-done | bytes 18874384 | tf_op jit(solution)/shard_map/all_gather | solution.py:127
  161.4 0.0 slice-start.1
  161.4 27.9 %shard_map.82 = bf16[384,384]{1,0:T(8,128)(2,1)} custom-call(s32[64]{0:T(128)} %get-tuple-element.6.order_ref, s32[2]{0:T(128)} %and_select_fusion.chunks_ref, bf16[384,384]{1,0:T(8,128)(2,1)} %q_ref.1, bf16[12288,768]{1,0:T(8,128)(2,1)} %all-gather.2.cloned.1.call-done.k_ref.v_ref, bf16[12288,768]{1,0:T(8,128)(2,1)} %all-gather.2.cloned.1.call-done.k_ref.v_ref, ...), custom_call_target="tpu_custom_call" | custom-call | flops 3623878656 | bytes 19464192 | tf_op jit(solution)/shard_map/pallas_call | solution.py:80
  189.3 0.0 slice-done
  189.3 0.0 slice-done.1
  189.3 3.8 %convolution_convert_fusion = bf16[384,6144]{1,0:T(8,128)(2,1)S(1)} fusion(bf16[384,384]{1,0:T(8,128)(2,1)} %shard_map.82, bf16[384,6144]{1,0:T(8,128)(2,1)S(1)} %bitcast.5), kind=kOutput, calls=%fused_computation.1 | convolution fusion | flops 1814298624 | bytes 9732096 | tf_op jit(solution)/shard_map/dot_general | solution.py:129
  193.1 55.1 %all_to_all.5 = bf16[8,48,6144]{2,1,0:T(8,128)(2,1)S(1)} all-to-all(bf16[8,48,6144]{2,1,0:T(8,128)(2,1)S(1)} %bitcast.3), channel_id=1, replica_groups=mesh['seq'=32,'tp'=8] {'tp'}, dimensions={0} | all-to-all | bytes 9437184 | tf_op jit(solution)/shard_map/all_to_all | solution.py:132
  248.2 0.7 convert_reduce_fusion
  248.9 0.0 copy-start
  248.9 0.0 copy-start.1
  248.9 0.2 multiply_reduce_fusion
  249.2 0.8 copy-done
  250.0 0.0 copy-done.1
  250.0 1.1 add_convert_fusion
  (4 shorter events, 0.0 us)
Async XLA Ops:
  6.5 2.0 copy-start.2
  6.5 2.2 copy-start.3
  6.5 154.8 %all-gather.2.cloned.1.call-start = ((), (), s32[]{:S(2)}) async-start(), calls=%async_computation.1 | async-start | bytes 19464192 | tf_op jit(solution)/shard_map/all_gather | solution.py:127
  8.5 180.8 %slice-start = ((s8[4718592]{0:T(1024)(128)(4,1)}), s8[524288]{0:T(1024)(128)(4,1)S(1)}, s32[]{:S(2)}) async-start(s8[4718592]{0:T(1024)(128)(4,1)} %bitcast.4), calls=%async_computation.2 | async-start | bytes 1048576
  161.4 27.9 %slice-start.1 = ((s8[4718592]{0:T(1024)(128)(4,1)}), s8[4194304]{0:T(1024)(128)(4,1)S(1)}, s32[]{:S(2)}) async-start(s8[4718592]{0:T(1024)(128)(4,1)} %bitcast.4), calls=%async_computation.3 | async-start | bytes 8388608
  248.9 1.1 copy-start
  248.9 1.1 copy-start.1
Sparse Core Ops, SparseCore 0:
  10.1 151.1 all-gather.1

commit v12 on v10

--- a/solution.py
+++ b/solution.py
@@ -10,6 +10,7 @@
 
 HEAD = 128
 SLOTS_PER_CHUNK = 16
+GATHER_PIECE_COLS = 32
 
 
 def slot_frames(pair_of_device, frame_of_tile, tile_count):
@@ -124,7 +125,14 @@
     ).reshape(2, 1, -1)
 
     kv_local = jnp.concatenate([keys, values], axis=1)
-    kv_rows = lax.all_gather(kv_local, "seq", axis=0, tiled=True)
+    piece = GATHER_PIECE_COLS
+    kv_rows = jnp.concatenate(
+        [
+            lax.all_gather(kv_local[:, i:i + piece], "seq", axis=0, tiled=True)
+            for i in range(0, kv_local.shape[1], piece)
+        ],
+        axis=1,
+    )
     attn = attention(queries, kv_rows, order, chunks, key_bias)
     partial = jnp.dot(attn, out_weight, preferred_element_type=jnp.float32)
 

time: 257 us -> 1580 us (6.15)
  blocking collectives: 58.9 us -> 1470 us
  waiting for transfers between devices: 150 us -> 0 us
  local copies, waits for them, and re-layouts: 1.27 us -> 69.6 us
    all_gather x0 -> x24, blocking collectives: none -> 1400 us  [local(): lax.all_gather(kv_local[:, i:i + piece], 'seq', axis=0, tiled=True)]
    all_gather x1 -> x0, waiting for transfers between devices: 150 us -> none  [local(): kv_rows = lax.all_gather(kv_local, 'seq', axis=0, tiled=True)]
    concatenate x0 -> x1, local copies, waits for them, and re-layouts: none -> 67 us  [local(): jnp.concatenate([lax.all_gather(kv_local[:, i:i + piece], 'seq', axis=0,...]
  transfers between devices with their start and end apart: 1 -> 0, of which waited for: 1 -> 0; matrix products, arithmetic and copies ran while one was open for 1% -> 0% of each run, Pallas kernels for 0% -> 0%
where the time goes in v12:
time: 1580 us
  blocking collectives  1470 us (93%)
  local copies, waits for them, and re-layouts  69.6 us (4%)
  Pallas kernels  24.3 us (2%)
    all_gather x24, blocking collectives, local(): lax.all_gather(kv_local[:, i:i + piece], 'seq', axis=0, tiled=True)  1400 us
    all_to_all x1, blocking collectives, local(): lax.all_to_all(partial.astype(jnp.bfloat16).reshape(tp_count, tok_rows //...  74.4 us
    concatenate x1, local copies, waits for them, and re-layouts, local(): jnp.concatenate([lax.all_gather(kv_local[:, i:i + piece], 'seq', axis=0,...  67 us

profile of v12, /device:TPU:2, one launch (start us, length us, event | category | flops | bytes accessed | tf_op | source)
XLA Modules:
  0.0 1576.1 jit_solution(7089152422685810499)
XLA Ops:
  0.0 1.7 fusion.4
  1.7 58.4 %all_gather.72 = bf16[12288,32]{1,0:T(8,128)(2,1)S(1)} all-gather(bf16[384,32]{1,0:T(8,128)(2,1)S(1)} %get-tuple-element.29), channel_id=1, replica_groups=mesh['seq'=32,'tp'=8] {'seq'}, dimensions={0}, use_global_device_ids=true | all-gather | bytes 811008 | tf_op jit(solution)/shard_map/all_gather | solution.py:131
  60.1 59.3 %all_gather.73 = bf16[12288,32]{1,0:T(8,128)(2,1)} all-gather(bf16[384,32]{1,0:T(8,128)(2,1)S(1)} %get-tuple-element.28), channel_id=1, replica_groups=mesh['seq'=32,'tp'=8] {'seq'}, dimensions={0}, use_global_device_ids=true | all-gather | bytes 811008 | tf_op jit(solution)/shard_map/all_gather | solution.py:131
  119.4 55.6 %all_gather.74 = bf16[12288,32]{1,0:T(8,128)(2,1)} all-gather(bf16[384,32]{1,0:T(8,128)(2,1)S(1)} %get-tuple-element.27), channel_id=1, replica_groups=mesh['seq'=32,'tp'=8] {'seq'}, dimensions={0}, use_global_device_ids=true | all-gather | bytes 811008 | tf_op jit(solution)/shard_map/all_gather | solution.py:131
  175.0 57.4 %all_gather.75 = bf16[12288,32]{1,0:T(8,128)(2,1)} all-gather(bf16[384,32]{1,0:T(8,128)(2,1)S(1)} %get-tuple-element.26), channel_id=1, replica_groups=mesh['seq'=32,'tp'=8] {'seq'}, dimensions={0}, use_global_device_ids=true | all-gather | bytes 811008 | tf_op jit(solution)/shard_map/all_gather | solution.py:131
  232.5 56.7 %all_gather.76 = bf16[12288,32]{1,0:T(8,128)(2,1)} all-gather(bf16[384,32]{1,0:T(8,128)(2,1)S(1)} %get-tuple-element.25), channel_id=1, replica_groups=mesh['seq'=32,'tp'=8] {'seq'}, dimensions={0}, use_global_device_ids=true | all-gather | bytes 811008 | tf_op jit(solution)/shard_map/all_gather | solution.py:131
  289.2 54.8 %all_gather.77 = bf16[12288,32]{1,0:T(8,128)(2,1)} all-gather(bf16[384,32]{1,0:T(8,128)(2,1)S(1)} %get-tuple-element.24), channel_id=1, replica_groups=mesh['seq'=32,'tp'=8] {'seq'}, dimensions={0}, use_global_device_ids=true | all-gather | bytes 811008 | tf_op jit(solution)/shard_map/all_gather | solution.py:131
  344.0 63.8 %all_gather.78 = bf16[12288,32]{1,0:T(8,128)(2,1)} all-gather(bf16[384,32]{1,0:T(8,128)(2,1)S(1)} %get-tuple-element.23), channel_id=1, replica_groups=mesh['seq'=32,'tp'=8] {'seq'}, dimensions={0}, use_global_device_ids=true | all-gather | bytes 811008 | tf_op jit(solution)/shard_map/all_gather | solution.py:131
  407.8 59.7 %all_gather.79 = bf16[12288,32]{1,0:T(8,128)(2,1)} all-gather(bf16[384,32]{1,0:T(8,128)(2,1)S(1)} %get-tuple-element.22), channel_id=1, replica_groups=mesh['seq'=32,'tp'=8] {'seq'}, dimensions={0}, use_global_device_ids=true | all-gather | bytes 811008 | tf_op jit(solution)/shard_map/all_gather | solution.py:131
  467.5 66.0 %all_gather.80 = bf16[12288,32]{1,0:T(8,128)(2,1)} all-gather(bf16[384,32]{1,0:T(8,128)(2,1)S(1)} %get-tuple-element.21), channel_id=1, replica_groups=mesh['seq'=32,'tp'=8] {'seq'}, dimensions={0}, use_global_device_ids=true | all-gather | bytes 811008 | tf_op jit(solution)/shard_map/all_gather | solution.py:131
  533.5 57.2 %all_gather.81 = bf16[12288,32]{1,0:T(8,128)(2,1)} all-gather(bf16[384,32]{1,0:T(8,128)(2,1)S(1)} %get-tuple-element.20), channel_id=1, replica_groups=mesh['seq'=32,'tp'=8] {'seq'}, dimensions={0}, use_global_device_ids=true | all-gather | bytes 811008 | tf_op jit(solution)/shard_map/all_gather | solution.py:131
  590.6 66.4 %all_gather.82 = bf16[12288,32]{1,0:T(8,128)(2,1)} all-gather(bf16[384,32]{1,0:T(8,128)(2,1)S(1)} %get-tuple-element.30), channel_id=1, replica_groups=mesh['seq'=32,'tp'=8] {'seq'}, dimensions={0}, use_global_device_ids=true | all-gather | bytes 811008 | tf_op jit(solution)/shard_map/all_gather | solution.py:131
  657.0 58.2 %all_gather.83 = bf16[12288,32]{1,0:T(8,128)(2,1)} all-gather(bf16[384,32]{1,0:T(8,128)(2,1)S(1)} %get-tuple-element.19), channel_id=1, replica_groups=mesh['seq'=32,'tp'=8] {'seq'}, dimensions={0}, use_global_device_ids=true | all-gather | bytes 811008 | tf_op jit(solution)/shard_map/all_gather | solution.py:131
  715.5 60.2 %all_gather.84 = bf16[12288,32]{1,0:T(8,128)(2,1)} all-gather(bf16[384,32]{1,0:T(8,128)(2,1)S(1)} %get-tuple-element.17), channel_id=1, replica_groups=mesh['seq'=32,'tp'=8] {'seq'}, dimensions={0}, use_global_device_ids=true | all-gather | bytes 811008 | tf_op jit(solution)/shard_map/all_gather | solution.py:131
  775.8 57.1 %all_gather.85 = bf16[12288,32]{1,0:T(8,128)(2,1)} all-gather(bf16[384,32]{1,0:T(8,128)(2,1)S(1)} %get-tuple-element.16), channel_id=1, replica_groups=mesh['seq'=32,'tp'=8] {'seq'}, dimensions={0}, use_global_device_ids=true | all-gather | bytes 811008 | tf_op jit(solution)/shard_map/all_gather | solution.py:131
  832.9 56.2 %all_gather.86 = bf16[12288,32]{1,0:T(8,128)(2,1)} all-gather(bf16[384,32]{1,0:T(8,128)(2,1)S(1)} %get-tuple-element.15), channel_id=1, replica_groups=mesh['seq'=32,'tp'=8] {'seq'}, dimensions={0}, use_global_device_ids=true | all-gather | bytes 811008 | tf_op jit(solution)/shard_map/all_gather | solution.py:131
  889.1 54.7 %all_gather.87 = bf16[12288,32]{1,0:T(8,128)(2,1)} all-gather(bf16[384,32]{1,0:T(8,128)(2,1)S(1)} %get-tuple-element.14), channel_id=1, replica_groups=mesh['seq'=32,'tp'=8] {'seq'}, dimensions={0}, use_global_device_ids=true | all-gather | bytes 811008 | tf_op jit(solution)/shard_map/all_gather | solution.py:131
  943.9 55.5 %all_gather.88 = bf16[12288,32]{1,0:T(8,128)(2,1)} all-gather(bf16[384,32]{1,0:T(8,128)(2,1)S(1)} %get-tuple-element.13), channel_id=1, replica_groups=mesh['seq'=32,'tp'=8] {'seq'}, dimensions={0}, use_global_device_ids=true | all-gather | bytes 811008 | tf_op jit(solution)/shard_map/all_gather | solution.py:131
  999.4 58.3 %all_gather.89 = bf16[12288,32]{1,0:T(8,128)(2,1)} all-gather(bf16[384,32]{1,0:T(8,128)(2,1)S(1)} %get-tuple-element.12), channel_id=1, replica_groups=mesh['seq'=32,'tp'=8] {'seq'}, dimensions={0}, use_global_device_ids=true | all-gather | bytes 811008 | tf_op jit(solution)/shard_map/all_gather | solution.py:131
  1057.7 52.9 %all_gather.90 = bf16[12288,32]{1,0:T(8,128)(2,1)} all-gather(bf16[384,32]{1,0:T(8,128)(2,1)S(1)} %get-tuple-element.11), channel_id=1, replica_groups=mesh['seq'=32,'tp'=8] {'seq'}, dimensions={0}, use_global_device_ids=true | all-gather | bytes 811008 | tf_op jit(solution)/shard_map/all_gather | solution.py:131
  1110.6 56.9 %all_gather.91 = bf16[12288,32]{1,0:T(8,128)(2,1)} all-gather(bf16[384,32]{1,0:T(8,128)(2,1)S(1)} %get-tuple-element.10), channel_id=1, replica_groups=mesh['seq'=32,'tp'=8] {'seq'}, dimensions={0}, use_global_device_ids=true | all-gather | bytes 811008 | tf_op jit(solution)/shard_map/all_gather | solution.py:131
  1167.6 53.8 %all_gather.92 = bf16[12288,32]{1,0:T(8,128)(2,1)} all-gather(bf16[384,32]{1,0:T(8,128)(2,1)S(1)} %get-tuple-element.9), channel_id=1, replica_groups=mesh['seq'=32,'tp'=8] {'seq'}, dimensions={0}, use_global_device_ids=true | all-gather | bytes 811008 | tf_op jit(solution)/shard_map/all_gather | solution.py:131
  1221.3 55.9 %all_gather.93 = bf16[12288,32]{1,0:T(8,128)(2,1)} all-gather(bf16[384,32]{1,0:T(8,128)(2,1)S(1)} %get-tuple-element.8), channel_id=1, replica_groups=mesh['seq'=32,'tp'=8] {'seq'}, dimensions={0}, use_global_device_ids=true | all-gather | bytes 811008 | tf_op jit(solution)/shard_map/all_gather | solution.py:131
  1277.3 62.0 %all_gather.94 = bf16[12288,32]{1,0:T(8,128)(2,1)} all-gather(bf16[384,32]{1,0:T(8,128)(2,1)S(1)} %get-tuple-element.18), channel_id=1, replica_groups=mesh['seq'=32,'tp'=8] {'seq'}, dimensions={0}, use_global_device_ids=true | all-gather | bytes 811008 | tf_op jit(solution)/shard_map/all_gather | solution.py:131
  1339.3 61.1 %all_gather.95 = bf16[12288,32]{1,0:T(8,128)(2,1)} all-gather(bf16[384,32]{1,0:T(8,128)(2,1)S(1)} %get-tuple-element.7), channel_id=1, replica_groups=mesh['seq'=32,'tp'=8] {'seq'}, dimensions={0}, use_global_device_ids=true | all-gather | bytes 811008 | tf_op jit(solution)/shard_map/all_gather | solution.py:131
  1401.9 0.8 compare_select_fusion.kb_ref
  1403.2 67.0 %concatenate.3.k_ref.v_ref = bf16[12288,768]{1,0:T(8,128)(2,1)} concatenate(bf16[12288,32]{1,0:T(8,128)(2,1)S(1)} %all_gather.72, bf16[12288,32]{1,0:T(8,128)(2,1)} %all_gather.73, bf16[12288,32]{1,0:T(8,128)(2,1)} %all_gather.74, bf16[12288,32]{1,0:T(8,128)(2,1)} %all_gather.75, bf16[12288,32]{1,0:T(8,128)(2,1)} %all_gather.76, bf16[12288,32]{1,0:T(8,128)(2,1)} %all_gather.77, ...), dimensions={1} | concatenate | bytes 37748736 | tf_op jit(solution)/shard_map/concatenate | solution.py:129
  1470.2 24.3 %shard_map.82 = bf16[384,384]{1,0:T(8,128)(2,1)} custom-call(s32[64]{0:T(128)} %get-tuple-element.6.order_ref, s32[2]{0:T(128)} %and_select_fusion.chunks_ref, bf16[384,384]{1,0:T(8,128)(2,1)} %q_ref.1, bf16[12288,768]{1,0:T(8,128)(2,1)} %concatenate.3.k_ref.v_ref, bf16[12288,768]{1,0:T(8,128)(2,1)} %concatenate.3.k_ref.v_ref, ...), custom_call_target="tpu_custom_call" | custom-call | flops 3623878656 | bytes 19464192 | tf_op jit(solution)/shard_map/pallas_call | solution.py:80
  1494.5 5.0 convolution_convert_fusion
  1499.6 74.4 %all_to_all.5 = bf16[8,48,6144]{2,1,0:T(8,128)(2,1)S(1)} all-to-all(bf16[8,48,6144]{2,1,0:T(8,128)(2,1)S(1)} %bitcast.3), channel_id=1, replica_groups=mesh['seq'=32,'tp'=8] {'tp'}, dimensions={0} | all-to-all | bytes 9437184 | tf_op jit(solution)/shard_map/all_to_all | solution.py:140
  1574.0 0.7 convert_reduce_fusion
  1575.1 1.0 add_convert_fusion
  (24 shorter events, 2.8 us)
Async XLA Ops:
  590.6 124.6 %copy-start = (bf16[384,384]{1,0:T(8,128)(2,1)S(1)}, bf16[384,384]{1,0:T(8,128)(2,1)}, u32[]{:S(2)}) copy-start(bf16[384,384]{1,0:T(8,128)(2,1)} %param.10) | copy-start | bytes 884740
  1277.3 123.1 %copy-start.3 = (s32[32]{0:T(128)S(1)}, s32[32]{0:T(128)}, u32[]{:S(2)}) copy-start(s32[32]{0:T(128)} %param.14) | copy-start | bytes 388
  1277.3 123.2 %copy-start.4 = (s32[64]{0:T(128)S(1)}, s32[64]{0:T(128)}, u32[]{:S(2)}) copy-start(s32[64]{0:T(128)} %param.15) | copy-start | bytes 772
  1574.0 1.1 copy-start.1
  1574.0 1.1 copy-start.2

commit v13 on v10

--- a/solution.py
+++ b/solution.py
@@ -9,7 +9,7 @@
 from jax.sharding import PartitionSpec as P
 
 HEAD = 128
-SLOTS_PER_CHUNK = 16
+SLOTS_PER_UNIT = 8
 
 
 def slot_frames(pair_of_device, frame_of_tile, tile_count):
@@ -20,25 +20,28 @@
     return jnp.sum(jnp.where(matches, frame_of_tile[None, :], 0), axis=1)
 
 
-def attn_kernel(order_ref, chunks_ref, q_ref, k_ref, v_ref, kb_ref, o_ref, s_sc):
+def attn_kernel(order_ref, units_ref, q_ref, k_ref, v_ref, kb_ref, o_ref, s_sc):
     tile = pl.program_id(1)
-    visible = chunks_ref[tile]
+    units = units_ref[tile]
+    pairs = units // 2
+    odd = units % 2
     rows = q_ref.shape[0]
     span = k_ref.shape[0] // order_ref.shape[0]
-    width = span * SLOTS_PER_CHUNK
+    unit = span * SLOTS_PER_UNIT
     score_scale = 1.0 / math.sqrt(HEAD)
     q = q_ref[...]
 
-    def gather(ref, c):
+    def gather(ref, first, count):
         pieces = []
-        for m in range(SLOTS_PER_CHUNK):
-            slot = order_ref[c * SLOTS_PER_CHUNK + m]
+        for m in range(count):
+            slot = order_ref[first + m]
             pieces.append(ref[pl.ds(pl.multiple_of(slot * span, span), span), :])
         return jnp.concatenate(pieces, axis=0)
 
-    def first(c, run_max):
-        start = pl.multiple_of(c * width, width)
-        k = gather(k_ref, c)
+    def first_pass(start_unit, count, run_max):
+        start = pl.multiple_of(start_unit * unit, unit)
+        width = count * unit
+        k = gather(k_ref, start_unit * SLOTS_PER_UNIT, count * SLOTS_PER_UNIT)
         s = lax.dot_general(
             q, k, (((1,), (1,)), ((), ())), preferred_element_type=jnp.float32
         ) * score_scale
@@ -46,23 +49,28 @@
         s_sc[:, pl.ds(start, width)] = masked
         return jnp.maximum(run_max, jnp.max(masked, axis=1, keepdims=True))
 
-    row_max = lax.fori_loop(0, visible, first, jnp.full((rows, 1), -1e30, jnp.float32))
+    row_max = lax.fori_loop(
+        0, pairs, lambda c, m: first_pass(2 * c, 2, m), jnp.full((rows, 1), -1e30, jnp.float32)
+    )
+    row_max = lax.fori_loop(0, odd, lambda c, m: first_pass(2 * pairs, 1, m), row_max)
 
-    def second(c, carry):
+    def second_pass(start_unit, count, carry):
         totals, acc = carry
-        start = pl.multiple_of(c * width, width)
+        start = pl.multiple_of(start_unit * unit, unit)
+        width = count * unit
         probs = jnp.exp(s_sc[:, pl.ds(start, width)] - row_max)
         totals = totals + jnp.sum(probs, axis=1, keepdims=True)
-        v = gather(v_ref, c)
+        v = gather(v_ref, start_unit * SLOTS_PER_UNIT, count * SLOTS_PER_UNIT)
         acc = acc + jnp.dot(probs.astype(jnp.bfloat16), v, preferred_element_type=jnp.float32)
         return totals, acc
 
-    totals, acc = lax.fori_loop(
+    carry = lax.fori_loop(
         0,
-        visible,
-        second,
+        pairs,
+        lambda c, t: second_pass(2 * c, 2, t),
         (jnp.zeros((rows, 1), jnp.float32), jnp.zeros((rows, HEAD), jnp.float32)),
     )
+    totals, acc = lax.fori_loop(0, odd, lambda c, t: second_pass(2 * pairs, 1, t), carry)
     o_ref[...] = (acc / totals).astype(o_ref.dtype)
 
 
@@ -117,7 +125,7 @@
         jnp.where(rank[:, None] == slot_ids[None, :], slot_frame[:, None], 0), axis=0
     )
     visible = jnp.sum((slot_frame[None, :] <= own_frames[:, None]).astype(jnp.int32), axis=1)
-    chunks = ((visible + SLOTS_PER_CHUNK - 1) // SLOTS_PER_CHUNK).astype(jnp.int32)
+    chunks = ((visible + SLOTS_PER_UNIT - 1) // SLOTS_PER_UNIT).astype(jnp.int32)
     key_frame = jnp.repeat(sorted_frame.astype(jnp.int32), span_rows)
     key_bias = jnp.where(
         key_frame[None, :] <= own_frames[:, None], jnp.float32(0.0), jnp.float32(-1e30)

time: 257 us -> 259 us (level)
  no operation moved by 1% of the time
where the time goes in v13:
time: 259 us; the launch traced here: 258 us
  waiting for transfers between devices  150 us (58%)
  blocking collectives  58.9 us (23%)
  Pallas kernels  23.9 us (9%)
  between operations  13.5 us (5%)
  other arithmetic  6.38 us (2%)
  matrix products  3.78 us (1%)
    all_gather x1, waiting for transfers between devices, local(): kv_rows = lax.all_gather(kv_local, 'seq', axis=0, tiled=True)  150 us
    all_to_all x1, blocking collectives, local(): lax.all_to_all(partial.astype(jnp.bfloat16).reshape(tp_count, tok_rows //...  58.9 us
    pallas_call x1, Pallas kernels, attention(): pl.pallas_call(attn_kernel, out_shape=jax.ShapeDtypeStruct((tok_rows, hea...  23.9 us
  transfers between devices with their start and end apart: 1, of which 1 were waited for; matrix products, arithmetic and copies ran while one was open for 1% of the time, Pallas kernels for 0%

profile of v13, /device:TPU:2, one launch (start us, length us, event | category | flops | bytes accessed | tf_op | source)
XLA Modules:
  0.0 257.6 jit_solution(18385581227132997337)
XLA Ops:
  6.5 0.0 copy-start.2
  6.5 0.0 copy-start.3
  6.5 0.0 all-gather.2.cloned.1.call-start
  6.5 1.9 pad_maximum_fusion
  8.5 0.0 slice-start
  8.5 0.0 all-gather.2.cloned.1.call-update
  8.5 0.0 copy-done.2
  8.5 0.1 broadcast_in_dim.34
  8.6 0.1 reshape.88
  8.7 0.0 copy-done.3
  8.7 0.2 select_reduce_fusion.2
  8.9 0.1 dynamic_slice.3
  9.0 0.2 convert_reduce_fusion.1
  9.2 0.7 select_reduce_fusion
  9.9 0.1 broadcast_in_dim.37
  9.9 0.1 le.38
  10.0 0.2 fusion.2
  10.2 0.5 and_select_fusion.units_ref
  10.7 0.8 compare_select_fusion.kb_ref
  11.5 149.9 %all-gather.2.cloned.1.call-done.k_ref.v_ref = bf16[12288,768]{1,0:T(8,128)(2,1)} async-done(((bf16[384,768]{1,0:T(8,128)(2,1)}), bf16[12288,768]{1,0:T(8,128)(2,1)}) %all-gather.2.cloned.1.call-update) | async-done | bytes 18874384 | tf_op jit(solution)/shard_map/all_gather | solution.py:135
  161.4 23.9 %shard_map.82 = bf16[384,384]{1,0:T(8,128)(2,1)} custom-call(s32[64]{0:T(128)} %get-tuple-element.6.order_ref, s32[2]{0:T(128)} %and_select_fusion.units_ref, bf16[384,384]{1,0:T(8,128)(2,1)} %q_ref.1, bf16[12288,768]{1,0:T(8,128)(2,1)} %all-gather.2.cloned.1.call-done.k_ref.v_ref, bf16[12288,768]{1,0:T(8,128)(2,1)} %all-gather.2.cloned.1.call-done.k_ref.v_ref, ...), custom_call_target="tpu_custom_call" | custom-call | flops 3623878656 | bytes 19464192 | tf_op jit(solution)/shard_map/pallas_call | solution.py:87
  185.2 0.0 slice-done
  185.2 0.0 slice-done.1
  185.3 3.8 %convolution_convert_fusion = bf16[384,6144]{1,0:T(8,128)(2,1)S(1)} fusion(bf16[384,384]{1,0:T(8,128)(2,1)} %shard_map.82, bf16[384,6144]{1,0:T(8,128)(2,1)S(1)} %bitcast.5), kind=kOutput, calls=%fused_computation.1 | convolution fusion | flops 1814298624 | bytes 9732096 | tf_op jit(solution)/shard_map/dot_general | solution.py:137
  189.0 58.9 %all_to_all.5 = bf16[8,48,6144]{2,1,0:T(8,128)(2,1)S(1)} all-to-all(bf16[8,48,6144]{2,1,0:T(8,128)(2,1)S(1)} %bitcast.3), channel_id=1, replica_groups=mesh['seq'=32,'tp'=8] {'tp'}, dimensions={0} | all-to-all | bytes 9437184 | tf_op jit(solution)/shard_map/all_to_all | solution.py:140
  248.0 0.7 convert_reduce_fusion
  248.6 0.0 copy-start
  248.7 0.0 copy-start.1
  248.7 0.2 multiply_reduce_fusion
  248.9 0.8 copy-done
  249.7 0.0 copy-done.1
  249.7 1.1 add_convert_fusion
  (4 shorter events, 0.0 us)
Async XLA Ops:
  6.5 2.0 copy-start.2
  6.5 2.2 copy-start.3
  6.5 154.8 %all-gather.2.cloned.1.call-start = ((), (), s32[]{:S(2)}) async-start(), calls=%async_computation.1 | async-start | bytes 19464192 | tf_op jit(solution)/shard_map/all_gather | solution.py:135
  8.5 176.8 %slice-start = ((s8[4718592]{0:T(1024)(128)(4,1)}), s8[524288]{0:T(1024)(128)(4,1)S(1)}, s32[]{:S(2)}) async-start(s8[4718592]{0:T(1024)(128)(4,1)} %bitcast.4), calls=%async_computation.2 | async-start | bytes 1048576
  161.4 23.9 %slice-start.1 = ((s8[4718592]{0:T(1024)(128)(4,1)}), s8[4194304]{0:T(1024)(128)(4,1)S(1)}, s32[]{:S(2)}) async-start(s8[4718592]{0:T(1024)(128)(4,1)} %bitcast.4), calls=%async_computation.3 | async-start | bytes 8388608
  248.6 1.1 copy-start
  248.7 1.1 copy-start.1
Sparse Core Ops, SparseCore 0:
  10.1 151.1 all-gather.1

commit v14 on v10

--- a/solution.py
+++ b/solution.py
@@ -20,25 +20,26 @@
     return jnp.sum(jnp.where(matches, frame_of_tile[None, :], 0), axis=1)
 
 
-def attn_kernel(order_ref, chunks_ref, q_ref, k_ref, v_ref, kb_ref, o_ref, s_sc):
+def attn_kernel(order_ref, chunks_ref, q_ref, kv_ref, kb_ref, o_ref, s_sc):
     tile = pl.program_id(1)
     visible = chunks_ref[tile]
     rows = q_ref.shape[0]
-    span = k_ref.shape[0] // order_ref.shape[0]
+    span = kv_ref.shape[0] // (2 * order_ref.shape[0])
     width = span * SLOTS_PER_CHUNK
     score_scale = 1.0 / math.sqrt(HEAD)
     q = q_ref[...]
 
-    def gather(ref, c):
+    def gather(base, c):
         pieces = []
         for m in range(SLOTS_PER_CHUNK):
             slot = order_ref[c * SLOTS_PER_CHUNK + m]
-            pieces.append(ref[pl.ds(pl.multiple_of(slot * span, span), span), :])
+            row = (slot // 2) * 4 * span + (slot % 2) * span + base
+            pieces.append(kv_ref[pl.ds(pl.multiple_of(row, span), span), :])
         return jnp.concatenate(pieces, axis=0)
 
     def first(c, run_max):
         start = pl.multiple_of(c * width, width)
-        k = gather(k_ref, c)
+        k = gather(0, c)
         s = lax.dot_general(
             q, k, (((1,), (1,)), ((), ())), preferred_element_type=jnp.float32
         ) * score_scale
@@ -53,7 +54,7 @@
         start = pl.multiple_of(c * width, width)
         probs = jnp.exp(s_sc[:, pl.ds(start, width)] - row_max)
         totals = totals + jnp.sum(probs, axis=1, keepdims=True)
-        v = gather(v_ref, c)
+        v = gather(2 * span, c)
         acc = acc + jnp.dot(probs.astype(jnp.bfloat16), v, preferred_element_type=jnp.float32)
         return totals, acc
 
@@ -69,7 +70,7 @@
 def attention(queries, kv_rows, order, chunks, key_bias):
     tok_rows = queries.shape[0]
     tile_rows = tok_rows // 2
-    key_count = kv_rows.shape[0]
+    key_count = kv_rows.shape[0] // 2
     head_count = queries.shape[1] // HEAD
     cost = pl.CostEstimate(
         flops=2 * tok_rows * key_count * HEAD * head_count,
@@ -84,8 +85,7 @@
             grid=(head_count, 2),
             in_specs=[
                 pl.BlockSpec((tile_rows, HEAD), lambda h, i, o, c: (i, h)),
-                pl.BlockSpec((key_count, HEAD), lambda h, i, o, c: (0, h)),
-                pl.BlockSpec((key_count, HEAD), lambda h, i, o, c: (0, head_count + h)),
+                pl.BlockSpec((2 * key_count, HEAD), lambda h, i, o, c: (0, h)),
                 pl.BlockSpec((None, 1, key_count), lambda h, i, o, c: (i, 0, 0)),
             ],
             out_specs=pl.BlockSpec((tile_rows, HEAD), lambda h, i, o, c: (i, h)),
@@ -93,7 +93,7 @@
         ),
         compiler_params=pltpu.CompilerParams(vmem_limit_bytes=56 * 1024 * 1024),
         cost_estimate=cost,
-    )(order, chunks, queries, kv_rows, kv_rows, key_bias)
+    )(order, chunks, queries, kv_rows, key_bias)
 
 
 def local(queries, keys, values, resid, out_weight, gain, pair_of_device, frame_of_tile):
@@ -123,7 +123,7 @@
         key_frame[None, :] <= own_frames[:, None], jnp.float32(0.0), jnp.float32(-1e30)
     ).reshape(2, 1, -1)
 
-    kv_local = jnp.concatenate([keys, values], axis=1)
+    kv_local = jnp.concatenate([keys, values], axis=0)
     kv_rows = lax.all_gather(kv_local, "seq", axis=0, tiled=True)
     attn = attention(queries, kv_rows, order, chunks, key_bias)
     partial = jnp.dot(attn, out_weight, preferred_element_type=jnp.float32)

time: 257 us -> 258 us (level)
  no operation moved by 1% of the time
where the time goes in v14:
time: 258 us; the launch traced here: 254 us
  waiting for transfers between devices  150 us (58%)
  blocking collectives  57.5 us (22%)
  Pallas kernels  21.9 us (8%)
  between operations  13.5 us (5%)
  other arithmetic  6.4 us (2%)
  matrix products  3.78 us (1%)
    all_gather x1, waiting for transfers between devices, local(): kv_rows = lax.all_gather(kv_local, 'seq', axis=0, tiled=True)  150 us
    all_to_all x1, blocking collectives, local(): lax.all_to_all(partial.astype(jnp.bfloat16).reshape(tp_count, tok_rows //...  57.5 us
    pallas_call x1, Pallas kernels, attention(): pl.pallas_call(attn_kernel, out_shape=jax.ShapeDtypeStruct((tok_rows, hea...  21.9 us
  transfers between devices with their start and end apart: 1, of which 1 were waited for; matrix products, arithmetic and copies ran while one was open for 1% of the time, Pallas kernels for 0%

profile of v14, /device:TPU:2, one launch (start us, length us, event | category | flops | bytes accessed | tf_op | source)
XLA Modules:
  0.0 254.3 jit_solution(8873012826494022070)
XLA Ops:
  6.5 0.0 copy-start.2
  6.5 0.0 copy-start.3
  6.5 0.0 all-gather.2.cloned.1.call-start
  6.5 1.9 pad_maximum_fusion
  8.5 0.0 all-gather.2.cloned.1.call-update
  8.5 0.0 copy-done.2
  8.5 0.1 broadcast_in_dim.34
  8.6 0.1 reshape.88
  8.7 0.0 copy-done.3
  8.7 0.2 select_reduce_fusion.2
  8.9 0.1 dynamic_slice.3
  9.0 0.2 convert_reduce_fusion.1
  9.2 0.7 select_reduce_fusion
  9.9 0.1 broadcast_in_dim.37
  9.9 0.0 slice-start
  9.9 0.1 le.38
  10.0 0.2 fusion.2
  10.2 0.5 and_select_fusion.chunks_ref
  10.7 0.8 compare_select_fusion.kb_ref
  11.5 149.9 %all-gather.2.cloned.1.call-done.kv_ref = bf16[24576,384]{1,0:T(8,128)(2,1)} async-done(((bf16[768,384]{1,0:T(8,128)(2,1)}), bf16[24576,384]{1,0:T(8,128)(2,1)}) %all-gather.2.cloned.1.call-update) | async-done | bytes 18874384 | tf_op jit(solution)/shard_map/all_gather | solution.py:127
  161.4 21.9 %shard_map.82 = bf16[384,384]{1,0:T(8,128)(2,1)} custom-call(s32[64]{0:T(128)} %get-tuple-element.6.order_ref, s32[2]{0:T(128)} %and_select_fusion.chunks_ref, bf16[384,384]{1,0:T(8,128)(2,1)} %q_ref.1, bf16[24576,384]{1,0:T(8,128)(2,1)} %all-gather.2.cloned.1.call-done.kv_ref, f32[2,1,12288]{2,1,0:T(1,128)} %compare_select_fusion.kb_ref), custom_call_target="tpu_custom_call" | custom-call | flops 3623878656 | bytes 19464192 | tf_op jit(solution)/shard_map/pallas_call | solution.py:80
  183.3 0.0 slice-done
  183.3 0.0 slice-done.1
  183.3 3.8 %convolution_convert_fusion = bf16[384,6144]{1,0:T(8,128)(2,1)S(1)} fusion(bf16[384,384]{1,0:T(8,128)(2,1)} %shard_map.82, bf16[384,6144]{1,0:T(8,128)(2,1)S(1)} %bitcast.5), kind=kOutput, calls=%fused_computation.1 | convolution fusion | flops 1814298624 | bytes 9732096 | tf_op jit(solution)/shard_map/dot_general | solution.py:129
  187.1 57.5 %all_to_all.5 = bf16[8,48,6144]{2,1,0:T(8,128)(2,1)S(1)} all-to-all(bf16[8,48,6144]{2,1,0:T(8,128)(2,1)S(1)} %bitcast.3), channel_id=1, replica_groups=mesh['seq'=32,'tp'=8] {'tp'}, dimensions={0} | all-to-all | bytes 9437184 | tf_op jit(solution)/shard_map/all_to_all | solution.py:132
  244.6 0.7 convert_reduce_fusion
  245.3 0.0 copy-start
  245.3 0.0 copy-start.1
  245.3 0.2 multiply_reduce_fusion
  245.5 0.8 copy-done
  246.3 0.0 copy-done.1
  246.4 1.1 add_convert_fusion
  (4 shorter events, 0.0 us)
Async XLA Ops:
  6.5 2.0 copy-start.2
  6.5 2.2 copy-start.3
  6.5 154.8 %all-gather.2.cloned.1.call-start = ((), (), s32[]{:S(2)}) async-start(), calls=%async_computation.1 | async-start | bytes 19464192 | tf_op jit(solution)/shard_map/all_gather | solution.py:127
  9.9 173.3 %slice-start = ((s8[4718592]{0:T(1024)(128)(4,1)}), s8[524288]{0:T(1024)(128)(4,1)S(1)}, s32[]{:S(2)}) async-start(s8[4718592]{0:T(1024)(128)(4,1)} %bitcast.4), calls=%async_computation.2 | async-start | bytes 1048576
  161.4 21.9 %slice-start.1 = ((s8[4718592]{0:T(1024)(128)(4,1)}), s8[4194304]{0:T(1024)(128)(4,1)S(1)}, s32[]{:S(2)}) async-start(s8[4718592]{0:T(1024)(128)(4,1)} %bitcast.4), calls=%async_computation.3 | async-start | bytes 8388608
  245.3 1.1 copy-start
  245.3 1.1 copy-start.1
Sparse Core Ops, SparseCore 0:
  10.1 151.1 all-gather.1

commit v15 on v7

--- a/solution.py
+++ b/solution.py
@@ -9,7 +9,7 @@
 from jax.sharding import PartitionSpec as P
 
 HEAD = 128
-SLOTS_PER_CHUNK = 8
+SLOTS_PER_CHUNK = 16
 
 
 def slot_frames(pair_of_device, frame_of_tile, tile_count):
@@ -128,7 +128,7 @@
     attn = attention(queries, kv_rows, order, chunks, key_bias)
     tp_count = lax.axis_size("tp")
     share_rows = tok_rows // tp_count
-    split = out_weight.shape[1] // 2
+    split = out_weight.shape[1] // 4
     part_a = jnp.dot(attn, out_weight[:, :split], preferred_element_type=jnp.float32)
     branch_a = lax.psum_scatter(
         part_a.astype(jnp.bfloat16), "tp", scatter_dimension=0, tiled=True

time: 265 us -> 283 us (1.068)
  the two profiles are of different devices: /device:TPU:2 before, /device:TPU:112 now
where the time goes in v15:
time: 283 us; the launch traced here: 282 us
  waiting for transfers between devices  221 us (78%)
  Pallas kernels  24.8 us (9%)
  between operations  13.5 us (5%)
  matrix products  7.91 us (3%)
  other arithmetic  7.82 us (3%)
  starting transfers between devices  5.81 us (2%)
    all_gather x1, waiting for transfers between devices, local(): kv_rows = lax.all_gather(kv_local, 'seq', axis=0, tiled=True)  146 us
    reduce_scatter x1, waiting for transfers between devices, local(): lax.psum_scatter(part_a.astype(jnp.bfloat16), 'tp', scatter_dimension=0,...  75 us
    pallas_call x1, Pallas kernels, attention(): pl.pallas_call(attn_kernel, out_shape=jax.ShapeDtypeStruct((tok_rows, hea...  24.8 us
    all_to_all x1, starting transfers between devices, local(): lax.all_to_all(part_b.astype(jnp.bfloat16).reshape(tp_count, share_rows,...  5.77 us
  transfers between devices with their start and end apart: 3, of which 2 were waited for; matrix products, arithmetic and copies ran while one was open for 3% of the time, Pallas kernels for 0%

profile of v15, /device:TPU:112, one launch (start us, length us, event | category | flops | bytes accessed | tf_op | source)
XLA Modules:
  0.0 282.2 jit_solution(9680363389992769127)
XLA Ops:
  6.5 0.0 all-gather.2.cloned.1.call-start
  6.5 1.9 pad_maximum_fusion.1
  8.5 0.0 all-gather.2.cloned.1.call-update
  8.5 0.0 copy-done.3
  8.5 0.1 broadcast_in_dim.34
  8.6 0.1 reshape.88
  8.7 0.0 copy-done.4
  8.7 0.2 select_reduce_fusion.2
  8.9 0.1 dynamic_slice.3
  9.0 0.2 convert_reduce_fusion.1
  9.2 0.7 select_reduce_fusion
  9.9 0.1 broadcast_in_dim.37
  9.9 0.1 le.38
  10.0 0.2 fusion.4
  10.2 0.5 and_select_fusion.chunks_ref
  10.7 0.8 compare_select_fusion.kb_ref
  11.5 145.5 %all-gather.2.cloned.1.call-done.k_ref.v_ref = bf16[12288,768]{1,0:T(8,128)(2,1)} async-done(((bf16[384,768]{1,0:T(8,128)(2,1)}), bf16[12288,768]{1,0:T(8,128)(2,1)}) %all-gather.2.cloned.1.call-update) | async-done | bytes 18874384 | tf_op jit(solution)/shard_map/all_gather | solution.py:127
  157.0 24.8 %shard_map.82 = bf16[384,384]{1,0:T(8,128)(2,1)} custom-call(s32[64]{0:T(128)} %get-tuple-element.6.order_ref, s32[2]{0:T(128)} %and_select_fusion.chunks_ref, bf16[384,384]{1,0:T(8,128)(2,1)} %q_ref.1, bf16[12288,768]{1,0:T(8,128)(2,1)} %all-gather.2.cloned.1.call-done.k_ref.v_ref, bf16[12288,768]{1,0:T(8,128)(2,1)} %all-gather.2.cloned.1.call-done.k_ref.v_ref, ...), custom_call_target="tpu_custom_call" | custom-call | flops 3623878656 | bytes 19464192 | tf_op jit(solution)/shard_map/pallas_call | solution.py:79
  181.8 0.0 slice-done.1
  181.8 4.8 %convolution_convert_fusion = bf16[384,4608]{1,0:T(8,128)(2,1)} fusion(bf16[384,384]{1,0:T(8,128)(2,1)} %shard_map.82, bf16[384,6144]{1,0:T(8,128)(2,1)S(1)} %bitcast.5), kind=kOutput, calls=%fused_computation.1 | convolution fusion | flops 1360723968 | bytes 7372800 | tf_op jit(solution)/shard_map/dot_general | solution.py:136
  186.6 5.8 %all-to-all-start = ((bf16[8,48,4608]{2,1,0:T(8,128)(2,1)}), bf16[8,48,4608]{2,1,0:T(8,128)(2,1)S(1)}, u32[]{:S(2)}, u32[]{:S(2)}) async-start(bf16[8,48,4608]{2,1,0:T(8,128)(2,1)} %bitcast.3), calls=%async_computation.1 | async-start | bytes 7077888 | tf_op jit(solution)/shard_map/all_to_all | solution.py:137
  192.4 0.0 reduce-scatter.2.cloned.1.call-start
  192.4 3.1 %convolution_convert_fusion.1 = bf16[384,1536]{1,0:T(8,128)(2,1)} fusion(bf16[384,384]{1,0:T(8,128)(2,1)} %shard_map.82, bf16[384,6144]{1,0:T(8,128)(2,1)} %param.12), kind=kOutput, calls=%fused_computation.3 | convolution fusion | flops 453574656 | bytes 2654208 | tf_op jit(solution)/shard_map/dot_general | solution.py:132
  195.6 0.0 reduce-scatter.2.cloned.1.call-update
  195.6 75.0 %reduce-scatter.2.cloned.1.call-done = bf16[48,1536]{1,0:T(8,128)(2,1)} async-done(((bf16[384,1536]{1,0:T(8,128)(2,1)}), bf16[48,1536]{1,0:T(8,128)(2,1)}) %reduce-scatter.2.cloned.1.call-update) | async-done | bytes 147472 | tf_op jit(solution)/shard_map/reduce_scatter | solution.py:133
  270.6 1.6 convert_element_type.28
  272.2 0.0 all-to-all-done
  272.2 0.5 convert_reduce_fusion
  272.7 0.5 copy-done
  273.2 0.2 multiply_reduce_fusion
  273.4 0.8 copy-done.1
  274.3 1.1 add_convert_fusion
  (12 shorter events, 0.0 us)
Async XLA Ops:
  6.5 2.0 copy-start.3
  6.5 2.2 copy-start.4
  6.5 150.5 %all-gather.2.cloned.1.call-start = ((), (), s32[]{:S(2)}) async-start(), calls=%async_computation.2 | async-start | bytes 19464192 | tf_op jit(solution)/shard_map/all_gather | solution.py:127
  8.5 173.3 %slice-start = ((s8[4718592]{0:T(1024)(128)(4,1)}), s8[524288]{0:T(1024)(128)(4,1)S(1)}, s32[]{:S(2)}) async-start(s8[4718592]{0:T(1024)(128)(4,1)} %bitcast.4), calls=%async_computation.4 | async-start | bytes 1048576
  157.0 24.8 %slice-start.1 = ((s8[4718592]{0:T(1024)(128)(4,1)}), s8[4194304]{0:T(1024)(128)(4,1)S(1)}, s32[]{:S(2)}) async-start(s8[4718592]{0:T(1024)(128)(4,1)} %bitcast.4), calls=%async_computation.5 | async-start | bytes 8388608
  186.6 85.6 %all-to-all-start = ((bf16[8,48,4608]{2,1,0:T(8,128)(2,1)}), bf16[8,48,4608]{2,1,0:T(8,128)(2,1)S(1)}, u32[]{:S(2)}, u32[]{:S(2)}) async-start(bf16[8,48,4608]{2,1,0:T(8,128)(2,1)} %bitcast.3), calls=%async_computation.1 | async-start | bytes 7077888 | tf_op jit(solution)/shard_map/all_to_all | solution.py:137
  192.4 78.2 %reduce-scatter.2.cloned.1.call-start = ((), (), s32[]{:S(2)}) async-start(), calls=%async_computation.3 | async-start | bytes 1327104 | tf_op jit(solution)/shard_map/reduce_scatter | solution.py:133
  272.2 1.0 copy-start
  273.2 1.1 copy-start.1
  273.2 1.1 copy-start.2
Sparse Core Ops, SparseCore 0:
  10.1 146.8 all-gather.1
  195.8 74.7 reduce-scatter.1

commit v16 on v10

--- a/solution.py
+++ b/solution.py
@@ -10,6 +10,7 @@
 
 HEAD = 128
 SLOTS_PER_CHUNK = 16
+PROJ_BLOCKS = 8
 
 
 def slot_frames(pair_of_device, frame_of_tile, tile_count):
@@ -20,7 +21,7 @@
     return jnp.sum(jnp.where(matches, frame_of_tile[None, :], 0), axis=1)
 
 
-def attn_kernel(order_ref, chunks_ref, q_ref, k_ref, v_ref, kb_ref, o_ref, s_sc):
+def attn_kernel(order_ref, chunks_ref, q_ref, k_ref, v_ref, kb_ref, w_ref, o_ref, s_sc, a_sc):
     tile = pl.program_id(1)
     visible = chunks_ref[tile]
     rows = q_ref.shape[0]
@@ -63,22 +64,33 @@
         second,
         (jnp.zeros((rows, 1), jnp.float32), jnp.zeros((rows, HEAD), jnp.float32)),
     )
-    o_ref[...] = (acc / totals).astype(o_ref.dtype)
+    head = pl.program_id(0)
+    a_sc[tile, :, pl.ds(pl.multiple_of(head * HEAD, HEAD), HEAD)] = (acc / totals).astype(a_sc.dtype)
+
+    @pl.when(head == pl.num_programs(0) - 1)
+    def _():
+        attn = a_sc[tile]
+        cols = w_ref.shape[1] // PROJ_BLOCKS
+        for j in range(PROJ_BLOCKS):
+            o_ref[:, j * cols:(j + 1) * cols] = jnp.dot(
+                attn, w_ref[:, j * cols:(j + 1) * cols], preferred_element_type=jnp.float32
+            ).astype(o_ref.dtype)
 
 
-def attention(queries, kv_rows, order, chunks, key_bias):
+def attention(queries, kv_rows, order, chunks, key_bias, out_weight):
     tok_rows = queries.shape[0]
     tile_rows = tok_rows // 2
     key_count = kv_rows.shape[0]
     head_count = queries.shape[1] // HEAD
     cost = pl.CostEstimate(
-        flops=2 * tok_rows * key_count * HEAD * head_count,
+        flops=2 * tok_rows * key_count * HEAD * head_count
+        + 2 * tok_rows * out_weight.shape[0] * out_weight.shape[1],
         transcendentals=tok_rows * key_count * head_count // 2,
         bytes_accessed=(key_count * 2 * HEAD * 2 + tok_rows * HEAD * 4) * head_count,
     )
     return pl.pallas_call(
         attn_kernel,
-        out_shape=jax.ShapeDtypeStruct((tok_rows, head_count * HEAD), jnp.bfloat16),
+        out_shape=jax.ShapeDtypeStruct((tok_rows, out_weight.shape[1]), jnp.bfloat16),
         grid_spec=pltpu.PrefetchScalarGridSpec(
             num_scalar_prefetch=2,
             grid=(head_count, 2),
@@ -87,13 +99,17 @@
                 pl.BlockSpec((key_count, HEAD), lambda h, i, o, c: (0, h)),
                 pl.BlockSpec((key_count, HEAD), lambda h, i, o, c: (0, head_count + h)),
                 pl.BlockSpec((None, 1, key_count), lambda h, i, o, c: (i, 0, 0)),
+                pl.BlockSpec(out_weight.shape, lambda h, i, o, c: (0, 0)),
             ],
-            out_specs=pl.BlockSpec((tile_rows, HEAD), lambda h, i, o, c: (i, h)),
-            scratch_shapes=[pltpu.VMEM((tile_rows, key_count), jnp.float32)],
+            out_specs=pl.BlockSpec((tile_rows, out_weight.shape[1]), lambda h, i, o, c: (i, 0)),
+            scratch_shapes=[
+                pltpu.VMEM((tile_rows, key_count), jnp.float32),
+                pltpu.VMEM((2, tile_rows, head_count * HEAD), jnp.bfloat16),
+            ],
         ),
         compiler_params=pltpu.CompilerParams(vmem_limit_bytes=56 * 1024 * 1024),
         cost_estimate=cost,
-    )(order, chunks, queries, kv_rows, kv_rows, key_bias)
+    )(order, chunks, queries, kv_rows, kv_rows, key_bias, out_weight)
 
 
 def local(queries, keys, values, resid, out_weight, gain, pair_of_device, frame_of_tile):
@@ -125,8 +141,7 @@
 
     kv_local = jnp.concatenate([keys, values], axis=1)
     kv_rows = lax.all_gather(kv_local, "seq", axis=0, tiled=True)
-    attn = attention(queries, kv_rows, order, chunks, key_bias)
-    partial = jnp.dot(attn, out_weight, preferred_element_type=jnp.float32)
+    partial = attention(queries, kv_rows, order, chunks, key_bias, out_weight)
 
     tp_count = lax.axis_size("tp")
     shares = lax.all_to_all(

time: 257 us -> 259 us (level)
  Pallas kernels: 21.6 us -> 29.9 us
  matrix products: 3.78 us -> 0 us
  blocking collectives: 58.9 us -> 55.4 us
    pallas_call x1, Pallas kernels: 21.6 us -> 29.9 us  [attention(): pl.pallas_call(attn_kernel, out_shape=jax.ShapeDtypeStruct((tok_rows, out...]
    dot_general x1 -> x0, matrix products: 3.78 us -> none  [local(): partial = jnp.dot(attn, out_weight, preferred_element_type=jnp.float32)]
    all_to_all x1, blocking collectives: 58.9 us -> 55.4 us  [local(): lax.all_to_all(partial.astype(jnp.bfloat16).reshape(tp_count, tok_rows //...]
where the time goes in v16:
time: 259 us; the launch traced here: 256 us
  waiting for transfers between devices  150 us (58%)
  blocking collectives  55.4 us (21%)
  Pallas kernels  29.9 us (12%)
  between operations  13.5 us (5%)
  other arithmetic  6.44 us (2%)
    all_gather x1, waiting for transfers between devices, local(): kv_rows = lax.all_gather(kv_local, 'seq', axis=0, tiled=True)  150 us
    all_to_all x1, blocking collectives, local(): lax.all_to_all(partial.astype(jnp.bfloat16).reshape(tp_count, tok_rows //...  55.4 us
    pallas_call x1, Pallas kernels, attention(): pl.pallas_call(attn_kernel, out_shape=jax.ShapeDtypeStruct((tok_rows, out...  29.9 us
  transfers between devices with their start and end apart: 1, of which 1 were waited for; matrix products, arithmetic and copies ran while one was open for 1% of the time, Pallas kernels for 0%

profile of v16, /device:TPU:2, one launch (start us, length us, event | category | flops | bytes accessed | tf_op | source)
XLA Modules:
  0.0 256.4 jit_solution(4796622926423279748)
XLA Ops:
  6.5 0.0 copy-start.2
  6.5 0.0 copy-start.3
  6.5 0.0 all-gather.2.cloned.1.call-start
  6.5 1.9 pad_maximum_fusion
  8.5 0.0 all-gather.2.cloned.1.call-update
  8.5 0.0 copy-done.2
  8.5 0.1 broadcast_in_dim.34
  8.6 0.1 reshape.88
  8.7 0.0 copy-done.3
  8.7 0.2 select_reduce_fusion.2
  8.9 0.1 dynamic_slice.3
  9.0 0.2 convert_reduce_fusion.1
  9.2 0.7 select_reduce_fusion
  9.8 0.1 broadcast_in_dim.37
  9.9 0.1 le.38
  10.0 0.2 fusion.2
  10.2 0.6 and_select_fusion.chunks_ref
  10.7 0.8 compare_select_fusion.kb_ref
  11.5 149.8 %all-gather.2.cloned.1.call-done.k_ref.v_ref = bf16[12288,768]{1,0:T(8,128)(2,1)} async-done(((bf16[384,768]{1,0:T(8,128)(2,1)}), bf16[12288,768]{1,0:T(8,128)(2,1)}) %all-gather.2.cloned.1.call-update) | async-done | bytes 18874384 | tf_op jit(solution)/shard_map/all_gather | solution.py:143
  161.4 29.9 %shard_map.82 = bf16[384,6144]{1,0:T(8,128)(2,1)} custom-call(s32[64]{0:T(128)} %get-tuple-element.6.order_ref, s32[2]{0:T(128)} %and_select_fusion.chunks_ref, bf16[384,384]{1,0:T(8,128)(2,1)} %q_ref.1, bf16[12288,768]{1,0:T(8,128)(2,1)} %all-gather.2.cloned.1.call-done.k_ref.v_ref, bf16[12288,768]{1,0:T(8,128)(2,1)} %all-gather.2.cloned.1.call-done.k_ref.v_ref, ...), custom_call_target="tpu_custom_call" | custom-call | flops 5435817984 | bytes 19464192 | tf_op jit(solution)/shard_map/pallas_call | solution.py:91
  191.3 55.4 %all_to_all.5 = bf16[8,48,6144]{2,1,0:T(8,128)(2,1)S(1)} all-to-all(bf16[8,48,6144]{2,1,0:T(8,128)(2,1)} %bitcast.1), channel_id=1, replica_groups=mesh['seq'=32,'tp'=8] {'tp'}, dimensions={0} | all-to-all | bytes 9437184 | tf_op jit(solution)/shard_map/all_to_all | solution.py:147
  246.8 0.7 convert_reduce_fusion
  247.4 0.0 copy-start
  247.5 0.0 copy-start.1
  247.5 0.2 multiply_reduce_fusion
  247.7 0.8 copy-done
  248.5 0.0 copy-done.1
  248.5 1.1 add_convert_fusion
  (2 shorter events, 0.0 us)
Async XLA Ops:
  6.5 2.0 copy-start.2
  6.5 2.2 copy-start.3
  6.5 154.8 %all-gather.2.cloned.1.call-start = ((), (), s32[]{:S(2)}) async-start(), calls=%async_computation.1 | async-start | bytes 19464192 | tf_op jit(solution)/shard_map/all_gather | solution.py:143
  247.4 1.1 copy-start
  247.5 1.1 copy-start.1
Sparse Core Ops, SparseCore 0:
  10.1 151.1 all-gather.1

commit v17 on v10

--- a/solution.py
+++ b/solution.py
@@ -9,7 +9,7 @@
 from jax.sharding import PartitionSpec as P
 
 HEAD = 128
-SLOTS_PER_CHUNK = 16
+SLOTS_PER_CHUNK = 32
 
 
 def slot_frames(pair_of_device, frame_of_tile, tile_count):

time: 257 us -> 259 us (level)
  no operation moved by 1% of the time
where the time goes in v17:
time: 259 us; the launch traced here: 256 us
  waiting for transfers between devices  150 us (58%)
  blocking collectives  58.9 us (23%)
  Pallas kernels  21.9 us (8%)
  between operations  13.5 us (5%)
  other arithmetic  6.38 us (2%)
  matrix products  3.78 us (1%)
    all_gather x1, waiting for transfers between devices, local(): kv_rows = lax.all_gather(kv_local, 'seq', axis=0, tiled=True)  150 us
    all_to_all x1, blocking collectives, local(): lax.all_to_all(partial.astype(jnp.bfloat16).reshape(tp_count, tok_rows //...  58.9 us
    pallas_call x1, Pallas kernels, attention(): pl.pallas_call(attn_kernel, out_shape=jax.ShapeDtypeStruct((tok_rows, hea...  21.9 us
  transfers between devices with their start and end apart: 1, of which 1 were waited for; matrix products, arithmetic and copies ran while one was open for 1% of the time, Pallas kernels for 0%

profile of v17, /device:TPU:2, one launch (start us, length us, event | category | flops | bytes accessed | tf_op | source)
XLA Modules:
  0.0 255.6 jit_solution(10630818337796582099)
XLA Ops:
  6.5 0.0 copy-start.2
  6.5 0.0 copy-start.3
  6.5 0.0 all-gather.2.cloned.1.call-start
  6.5 1.9 pad_maximum_fusion
  8.5 0.0 all-gather.2.cloned.1.call-update
  8.5 0.0 copy-done.2
  8.5 0.1 broadcast_in_dim.34
  8.6 0.1 reshape.88
  8.7 0.0 copy-done.3
  8.7 0.2 select_reduce_fusion.2
  8.9 0.1 dynamic_slice.3
  9.0 0.2 convert_reduce_fusion.1
  9.2 0.7 select_reduce_fusion
  9.9 0.1 broadcast_in_dim.37
  9.9 0.1 le.38
  10.0 0.2 fusion.2
  10.2 0.5 and_select_fusion.chunks_ref
  10.7 0.8 compare_select_fusion.kb_ref
  11.5 149.9 %all-gather.2.cloned.1.call-done.k_ref.v_ref = bf16[12288,768]{1,0:T(8,128)(2,1)} async-done(((bf16[384,768]{1,0:T(8,128)(2,1)}), bf16[12288,768]{1,0:T(8,128)(2,1)}) %all-gather.2.cloned.1.call-update) | async-done | bytes 18874384 | tf_op jit(solution)/shard_map/all_gather | solution.py:127
  161.4 0.0 slice-start.1
  161.4 21.9 %shard_map.82 = bf16[384,384]{1,0:T(8,128)(2,1)} custom-call(s32[64]{0:T(128)} %get-tuple-element.6.order_ref, s32[2]{0:T(128)} %and_select_fusion.chunks_ref, bf16[384,384]{1,0:T(8,128)(2,1)} %q_ref.1, bf16[12288,768]{1,0:T(8,128)(2,1)} %all-gather.2.cloned.1.call-done.k_ref.v_ref, bf16[12288,768]{1,0:T(8,128)(2,1)} %all-gather.2.cloned.1.call-done.k_ref.v_ref, ...), custom_call_target="tpu_custom_call" | custom-call | flops 3623878656 | bytes 19464192 | tf_op jit(solution)/shard_map/pallas_call | solution.py:79
  183.2 0.0 slice-done
  183.2 0.0 slice-done.1
  183.2 3.8 %convolution_convert_fusion = bf16[384,6144]{1,0:T(8,128)(2,1)S(1)} fusion(bf16[384,384]{1,0:T(8,128)(2,1)} %shard_map.82, bf16[384,6144]{1,0:T(8,128)(2,1)S(1)} %bitcast.5), kind=kOutput, calls=%fused_computation.1 | convolution fusion | flops 1814298624 | bytes 9732096 | tf_op jit(solution)/shard_map/dot_general | solution.py:129
  187.0 58.9 %all_to_all.5 = bf16[8,48,6144]{2,1,0:T(8,128)(2,1)S(1)} all-to-all(bf16[8,48,6144]{2,1,0:T(8,128)(2,1)S(1)} %bitcast.3), channel_id=1, replica_groups=mesh['seq'=32,'tp'=8] {'tp'}, dimensions={0} | all-to-all | bytes 9437184 | tf_op jit(solution)/shard_map/all_to_all | solution.py:132
  245.9 0.7 convert_reduce_fusion
  246.6 0.0 copy-start
  246.6 0.0 copy-start.1
  246.6 0.2 multiply_reduce_fusion
  246.8 0.8 copy-done
  247.7 0.0 copy-done.1
  247.7 1.1 add_convert_fusion
  (4 shorter events, 0.0 us)
Async XLA Ops:
  6.5 2.0 copy-start.2
  6.5 2.2 copy-start.3
  6.5 154.8 %all-gather.2.cloned.1.call-start = ((), (), s32[]{:S(2)}) async-start(), calls=%async_computation.1 | async-start | bytes 19464192 | tf_op jit(solution)/shard_map/all_gather | solution.py:127
  8.5 174.7 %slice-start = ((s8[4718592]{0:T(1024)(128)(4,1)}), s8[524288]{0:T(1024)(128)(4,1)S(1)}, s32[]{:S(2)}) async-start(s8[4718592]{0:T(1024)(128)(4,1)} %bitcast.4), calls=%async_computation.2 | async-start | bytes 1048576
  161.4 21.9 %slice-start.1 = ((s8[4718592]{0:T(1024)(128)(4,1)}), s8[4194304]{0:T(1024)(128)(4,1)S(1)}, s32[]{:S(2)}) async-start(s8[4718592]{0:T(1024)(128)(4,1)} %bitcast.4), calls=%async_computation.3 | async-start | bytes 8388608
  246.6 1.1 copy-start
  246.6 1.1 copy-start.1
Sparse Core Ops, SparseCore 0:
  10.1 151.1 all-gather.1
